TPU v7x, 512 devices: a whole 4x8x8 slice. The times are simulated.
512 devices in a mesh: particle: 32 (over x, z), band: 16 (over y, core).
Axes of the slice: x: 4, y: 8, z: 8, core: 2. Of those that a mesh axis runs over, the one named last changes fastest.
Arguments:
- states: float32 [128, 2, 256, 1024], P('particle', None, 'band'), may hold values from -4 to 4
- counts: int32 [128], replicated, may hold values from 0 to 2, as said below
Outputs:
- forecast: float32 [128, 2, 256, 1024], P('particle', None, 'band')
Inputs may be any that keep to these rules, and one draw needn't show every extreme that they name: Counts sum to 128; particle 0 and particle 128 - 1 have count 1, and for every m the particles 2m + 1 and 2m + 2 have counts summing to 2, so each slot's ancestor is the slot itself or a particle next to it; where 2m + 2 is a multiple of 4, the pair's counts are (2, 0).
All inputs are finite; a program needn't handle non-finite values.
Results may differ from a plain program's by a relative error of at most 0.00002.
Values sent between devices are 32-bit elements; how exact they have to be, the bound alone decides.
No kernel may reach another device: no remote copies, remote signals or barrier semaphores. Data moves between devices by JAX's collectives and lax.ppermute only.
A program may use at most 64 MiB of HBM per device.

v0:
```python
import jax
import jax.numpy as jnp
from jax import lax
from jax.sharding import PartitionSpec as P

GRID_HIERARCHY = 3
COARSE_SWEEPS = 6


smoothing_weight = 0.8
deform_term = 0.1
beta_slope = 0.5
bottom_friction_coefficient = 0.2
time_step = 0.5
meridional_weight = 1.8
zonal_weight = 0.2


def padded(cells, sides, width):
    for axis, dim in sides:
        count = lax.axis_size(axis)
        ends = count - 1
        head = lax.slice_in_dim(cells, 0, width, axis=dim)
        tail = lax.slice_in_dim(cells, cells.shape[dim] - width, cells.shape[dim], axis=dim)
        cells = jnp.concatenate(
            [
                lax.ppermute(tail, axis, [(i, (i + 1) % count) for i in range(ends)]),
                cells,
                lax.ppermute(head, axis, [((i + 1) % count, i) for i in range(ends)]),
            ],
            axis=dim,
        )
    return cells


def shifted(value, axis, steps):
    count = lax.axis_size(axis)
    first, last = (max(0, -steps), min(count, count - steps))
    return lax.ppermute(value, axis, [(source, source + steps) for source in range(first, last)])


def strip_row_count(field):
    return padded(field, (("band", 2),), 1)


def coarse_rows(field):
    return padded(field, (("band", 2),), 1)


def neighbours(field, widened_field):
    across = widened_field[..., 2:, :] + widened_field[..., :-2, :]
    along = jnp.roll(field, -1, axis=-1) + jnp.roll(field, 1, axis=-1)
    return meridional_weight * across + zonal_weight * along


def smooth(field, forcing_term, diagonal_term, padder):
    applied = diagonal_term * field - neighbours(field, padder(field))
    return field + smoothing_weight * (forcing_term - applied) / diagonal_term


def restrict(field):
    leading = field.shape[:-2]
    height, breadth = (field.shape[-2], field.shape[-1])
    blocks = field.reshape(leading + (height // 2, 2, breadth // 2, 2))
    return jnp.sum(blocks, axis=(-3, -1))


def prolong(field):
    return jnp.repeat(jnp.repeat(field, 2, axis=-2), 2, axis=-1)


def diagonal_at(level):
    return 4.0 + jnp.array([0.0, deform_term], jnp.float32).reshape(2, 1, 1) * 4.0**level


def coarse_solve(forcing_term, diagonal_term, padder):
    field = smoothing_weight * forcing_term / diagonal_term
    for repeat in range(COARSE_SWEEPS - 1):
        field = smooth(field, forcing_term, diagonal_term, padder)
    return field


def coarse_level(forcing_term, diagonal_term):
    return coarse_solve(forcing_term, diagonal_term, coarse_rows)


def cycle(forcing_term, level):
    diagonal_term = diagonal_at(level)
    if level == GRID_HIERARCHY - 1:
        return coarse_level(forcing_term, diagonal_term)
    field = smoothing_weight * forcing_term / diagonal_term
    field = smooth(field, forcing_term, diagonal_term, strip_row_count)
    remainder = forcing_term - (diagonal_term * field - neighbours(field, strip_row_count(field)))
    field = field + prolong(cycle(restrict(remainder), level + 1))
    field = smooth(field, forcing_term, diagonal_term, strip_row_count)
    field = smooth(field, forcing_term, diagonal_term, strip_row_count)
    return field


def advance_step(potential_curl_grid, stream, padded_stream, padded_vorticity):
    stream_x = 0.5 * (jnp.roll(stream, -1, axis=-1) - jnp.roll(stream, 1, axis=-1))
    meridional_streamfunction_gradient = 0.5 * (
        padded_stream[..., 2:, :] - padded_stream[..., :-2, :]
    )
    vort_x = 0.5 * (
        jnp.roll(potential_curl_grid, -1, axis=-1) - jnp.roll(potential_curl_grid, 1, axis=-1)
    )
    vort_y = 0.5 * (padded_vorticity[..., 2:, :] - padded_vorticity[..., :-2, :])
    laplace = neighbours(stream, padded_stream) - 4.0 * stream
    drag = jnp.array([0.0, bottom_friction_coefficient], jnp.float32).reshape(2, 1, 1)
    jacobian = stream_x * vort_y - meridional_streamfunction_gradient * vort_x
    return potential_curl_grid - time_step * (jacobian + beta_slope * stream_x + drag * laplace)


def mode_sources(redrawn_ensemble):
    upper = redrawn_ensemble[:, 0]
    lower = redrawn_ensemble[:, 1]
    return -jnp.stack([0.5 * (upper + lower), 0.5 * (upper - lower)], axis=1)


def stream_of(modes):
    return jnp.stack([modes[:, 0] + modes[:, 1], modes[:, 0] - modes[:, 1]], axis=1)


def per_device(states, counts):
    group = lax.axis_index("particle")
    per_group = states.shape[0]
    totals = jnp.cumsum(counts, dtype=jnp.int32)
    slots = group * per_group + jnp.arange(per_group, dtype=jnp.int32)
    ancestor = jnp.sum(
        (totals[None, :] <= slots[:, None]).astype(jnp.int32), axis=1, dtype=jnp.int32
    )
    below_last = shifted(states[-1:], "particle", 1)
    extended = jnp.concatenate([below_last, states], axis=0)
    local_index = ancestor - (group * per_group - 1)
    redrawn_ensemble = jnp.take(extended, local_index, axis=0)
    modes = cycle(mode_sources(redrawn_ensemble), 0)
    stream = stream_of(modes)
    joined = jnp.concatenate([stream, redrawn_ensemble], axis=1)
    widened_field = padded(joined, (("band", 2),), 1)
    return advance_step(redrawn_ensemble, stream, widened_field[:, :2], widened_field[:, 2:])


def solution(mesh):
    in_specs = (P("particle", None, "band", None), P())
    out_specs = P("particle", None, "band", None)
    return jax.shard_map(
        per_device, mesh=mesh, in_specs=in_specs, out_specs=out_specs, check_vma=False
    )
```

profile of v0, /device:TPU:31, one launch (start us, length us, event | category | flops | bytes accessed | tf_op | source)
XLA Modules:
  0.0 198.2 jit_solution(5987644875547892997)
XLA Ops:
  0.0 0.9 slice.425
  0.9 4.0 %collective-permute-start = (f32[1,2,16,1024]{3,2,1,0:T(8,128)S(1)}, f32[1,2,16,1024]{3,2,1,0:T(8,128)S(1)}, u32[]{:S(2)}, u32[]{:S(2)}) collective-permute-start(f32[1,2,16,1024]{3,2,1,0:T(8,128)S(1)} %slice.425), channel_id=1, source_target_pairs={{0,16},{16,32},{32,48},{48,64},{64,80},{80,96},{96,112},{112,128},... | collective-permute-start | bytes 393224 | tf_op jit(solution)/shard_map/ppermute | solution.py:39
  5.0 0.8 copy.419
  6.2 8.8 %collective-permute-done = f32[1,2,16,1024]{3,2,1,0:T(8,128)S(1)} collective-permute-done((f32[1,2,16,1024]{3,2,1,0:T(8,128)S(1)}, f32[1,2,16,1024]{3,2,1,0:T(8,128)S(1)}, u32[]{:S(2)}, u32[]{:S(2)}) %collective-permute-start) | collective-permute-done | bytes 131104 | tf_op jit(solution)/shard_map/ppermute | solution.py:39
  15.1 1.1 pad_maximum_fusion.1
  16.1 0.6 gather_fusion
  17.4 1.0 fusion.129
  18.4 3.1 %collective-permute-start.1 = (f32[4,2,1,1024]{3,2,1,0:T(1,128)S(1)}, f32[4,2,1,1024]{3,2,1,0:T(1,128)S(1)}, u32[]{:S(2)}, u32[]{:S(2)}) collective-permute-start(f32[4,2,1,1024]{3,2,1,0:T(1,128)S(1)} %get-tuple-element.39), channel_id=1, source_target_pairs={{1,0},{2,1},{3,2},{4,3},{5,4},{6,5},{7,6},{8,7},{9,8},{10,9},{11,1... | collective-permute-start | bytes 98312 | tf_op jit(solution)/shard_map/ppermute | solution.py:29
  21.6 4.3 %collective-permute-start.2 = (f32[4,2,1,1024]{3,2,1,0:T(1,128)S(1)}, f32[4,2,1,1024]{3,2,1,0:T(1,128)S(1)}, u32[]{:S(2)}, u32[]{:S(2)}) collective-permute-start(f32[4,2,1,1024]{3,2,1,0:T(1,128)S(1)} %get-tuple-element.40), channel_id=1, source_target_pairs={{0,1},{1,2},{2,3},{3,4},{4,5},{5,6},{6,7},{7,8},{8,9},{9,10},{10,1... | collective-permute-start | bytes 98312 | tf_op jit(solution)/shard_map/ppermute | solution.py:27
  25.9 0.6 fusion.128
  26.9 0.4 fusion.40
  27.6 1.9 collective-permute-start.3
  29.5 5.4 %collective-permute-start.4 = (f32[4,2,1,1024]{3,2,1,0:T(1,128)S(1)}, f32[4,2,1,1024]{3,2,1,0:T(1,128)S(1)}, u32[]{:S(2)}, u32[]{:S(2)}) collective-permute-start(f32[4,2,1,1024]{3,2,1,0:T(1,128)S(1)} %get-tuple-element.34), channel_id=1, source_target_pairs={{0,1},{1,2},{2,3},{3,4},{4,5},{5,6},{6,7},{7,8},{8,9},{9,10},{10,1... | collective-permute-start | bytes 98312 | tf_op jit(solution)/shard_map/ppermute | solution.py:27
  35.0 0.9 collective-permute-done.4
  36.3 8.7 %copy.420 = f32[4,2,16,1024]{0,3,2,1:T(8,128)} copy(f32[4,2,16,1024]{3,2,1,0:T(8,128)S(1)} %fusion.32) | data formatting | bytes 1048576 | tf_op jit(solution)/shard_map/sub | solution.py:93
  45.0 17.6 %reduce_sum.28 = f32[4,2,8,512]{0,3,2,1:T(8,128)} reduce(f32[4,2,8,2,512,2]{0,5,4,3,2,1:T(2,128)} %bitcast.11, f32[]{:T(128)} %constant.29.clone.1), dimensions={3,5}, to_apply=%region_2.3 | reduce | flops 98304 | bytes 655364 | tf_op jit(solution)/shard_map/reduce_sum | solution.py:65
  62.7 2.9 %copy.421 = f32[4,2,8,512]{3,2,1,0:T(8,128)S(1)} copy(f32[4,2,8,512]{0,3,2,1:T(8,128)} %reduce_sum.28) | data formatting | bytes 262144 | tf_op jit(solution)/shard_map/reduce_sum | solution.py:65
  65.8 1.9 collective-permute-start.5
  67.8 5.4 %collective-permute-start.6 = (f32[4,2,1,512]{3,0,2,1:T(4,128)S(1)}, f32[4,2,1,512]{3,0,2,1:T(4,128)S(1)}, u32[]{:S(2)}, u32[]{:S(2)}) collective-permute-start(f32[4,2,1,512]{3,0,2,1:T(4,128)S(1)} %copy.424), channel_id=1, source_target_pairs={{0,1},{1,2},{2,3},{3,4},{4,5},{5,6},{6,7},{7,8},{8,9},{9,10},{10,1... | collective-permute-start | bytes 49160 | tf_op jit(solution)/shard_map/ppermute | solution.py:27
  73.3 0.7 collective-permute-done.6
  74.4 1.9 collective-permute-start.7
  76.3 5.4 %collective-permute-start.8 = (f32[4,2,1,512]{3,0,2,1:T(4,128)S(1)}, f32[4,2,1,512]{3,0,2,1:T(4,128)S(1)}, u32[]{:S(2)}, u32[]{:S(2)}) collective-permute-start(f32[4,2,1,512]{3,0,2,1:T(4,128)S(1)} %copy.429), channel_id=1, source_target_pairs={{0,1},{1,2},{2,3},{3,4},{4,5},{5,6},{6,7},{7,8},{8,9},{9,10},{10,1... | collective-permute-start | bytes 49160 | tf_op jit(solution)/shard_map/ppermute | solution.py:27
  81.8 0.7 collective-permute-done.8
  82.7 2.7 %copy.432 = f32[4,2,8,512]{0,3,2,1:T(8,128)} copy(f32[4,2,8,512]{3,2,1,0:T(8,128)S(1)} %fusion.67) | data formatting | bytes 262144 | tf_op jit(solution)/shard_map/sub | solution.py:93
  85.4 5.8 %reduce_sum.29 = f32[4,2,4,256]{0,3,2,1:T(8,128)S(1)} reduce(f32[4,2,4,2,256,2]{0,5,4,3,2,1:T(2,128)} %bitcast.13, f32[]{:T(128)} %constant.29.clone.1), dimensions={3,5}, to_apply=%region_3.4 | reduce | flops 24576 | bytes 163844 | tf_op jit(solution)/shard_map/reduce_sum | solution.py:65
  91.7 5.4 %collective-permute-start.10 = (f32[4,2,1,256]{3,2,1,0:T(1,128)S(1)}, f32[4,2,1,256]{3,2,1,0:T(1,128)S(1)}, u32[]{:S(2)}, u32[]{:S(2)}) collective-permute-start(f32[4,2,1,256]{3,2,1,0:T(1,128)S(1)} %get-tuple-element.96), channel_id=1, source_target_pairs={{0,1},{1,2},{2,3},{3,4},{4,5},{5,6},{6,7},{7,8},{8,9},{9,10},{10,1... | collective-permute-start | bytes 24584 | tf_op jit(solution)/shard_map/ppermute | solution.py:27
  97.1 1.9 collective-permute-start.9
  99.1 4.2 %collective-permute-done.9 = f32[4,2,1,256]{3,2,1,0:T(1,128)S(1)} collective-permute-done((f32[4,2,1,256]{3,2,1,0:T(1,128)S(1)}, f32[4,2,1,256]{3,2,1,0:T(1,128)S(1)}, u32[]{:S(2)}, u32[]{:S(2)}) %collective-permute-start.9) | collective-permute-done | bytes 8224 | tf_op jit(solution)/shard_map/ppermute | solution.py:29
  103.5 1.9 collective-permute-start.11
  105.5 4.9 %collective-permute-start.12 = (f32[4,2,1,256]{3,2,1,0:T(1,128)S(1)}, f32[4,2,1,256]{3,2,1,0:T(1,128)S(1)}, u32[]{:S(2)}, u32[]{:S(2)}) collective-permute-start(f32[4,2,1,256]{3,2,1,0:T(1,128)S(1)} %get-tuple-element.90), channel_id=1, source_target_pairs={{0,1},{1,2},{2,3},{3,4},{4,5},{5,6},{6,7},{7,8},{8,9},{9,10},{10,1... | collective-permute-start | bytes 24584 | tf_op jit(solution)/shard_map/ppermute | solution.py:27
  110.4 0.7 collective-permute-done.12
  111.3 1.9 collective-permute-start.13
  113.2 5.4 %collective-permute-start.14 = (f32[4,2,1,256]{3,2,1,0:T(1,128)S(1)}, f32[4,2,1,256]{3,2,1,0:T(1,128)S(1)}, u32[]{:S(2)}, u32[]{:S(2)}) collective-permute-start(f32[4,2,1,256]{3,2,1,0:T(1,128)S(1)} %get-tuple-element.84), channel_id=1, source_target_pairs={{0,1},{1,2},{2,3},{3,4},{4,5},{5,6},{6,7},{7,8},{8,9},{9,10},{10,1... | collective-permute-start | bytes 24584 | tf_op jit(solution)/shard_map/ppermute | solution.py:27
  118.7 0.7 collective-permute-done.14
  119.6 1.9 collective-permute-start.15
  121.6 5.4 %collective-permute-start.16 = (f32[4,2,1,256]{3,2,1,0:T(1,128)S(1)}, f32[4,2,1,256]{3,2,1,0:T(1,128)S(1)}, u32[]{:S(2)}, u32[]{:S(2)}) collective-permute-start(f32[4,2,1,256]{3,2,1,0:T(1,128)S(1)} %get-tuple-element.78), channel_id=1, source_target_pairs={{0,1},{1,2},{2,3},{3,4},{4,5},{5,6},{6,7},{7,8},{8,9},{9,10},{10,1... | collective-permute-start | bytes 24584 | tf_op jit(solution)/shard_map/ppermute | solution.py:27
  127.1 0.7 collective-permute-done.16
  128.0 1.9 collective-permute-start.17
  129.9 5.6 %collective-permute-start.18 = (f32[4,2,1,256]{3,2,1,0:T(1,128)S(1)}, f32[4,2,1,256]{3,2,1,0:T(1,128)S(1)}, u32[]{:S(2)}, u32[]{:S(2)}) collective-permute-start(f32[4,2,1,256]{3,2,1,0:T(1,128)S(1)} %get-tuple-element.72), channel_id=1, source_target_pairs={{0,1},{1,2},{2,3},{3,4},{4,5},{5,6},{6,7},{7,8},{8,9},{9,10},{10,1... | collective-permute-start | bytes 24584 | tf_op jit(solution)/shard_map/ppermute | solution.py:27
  135.6 0.5 collective-permute-done.18
  136.2 0.6 broadcast_in_dim.20
  136.9 1.2 copy.440
  138.0 2.1 %broadcast_in_dim.21 = f32[4,2,8,256,2]{2,4,3,1,0:T(2,128)} broadcast(f32[4,2,8,256]{2,3,1,0:T(8,128)S(1)} %copy.440), dimensions={0,1,2,3} | broadcast | bytes 196608 | tf_op jit(solution)/shard_map/broadcast_in_dim | solution.py:69
  140.1 2.2 %copy.441 = f32[4,2,8,512]{3,2,1,0:T(8,128)S(1)} copy(f32[4,2,8,512]{2,3,1,0:T(8,128)} %bitcast.14) | data formatting | bytes 262144 | tf_op jit(solution)/shard_map/reshape | solution.py:69
  142.4 1.9 collective-permute-start.19
  144.4 5.4 %collective-permute-start.20 = (f32[4,2,1,512]{3,0,2,1:T(4,128)S(1)}, f32[4,2,1,512]{3,0,2,1:T(4,128)S(1)}, u32[]{:S(2)}, u32[]{:S(2)}) collective-permute-start(f32[4,2,1,512]{3,0,2,1:T(4,128)S(1)} %copy.444), channel_id=1, source_target_pairs={{0,1},{1,2},{2,3},{3,4},{4,5},{5,6},{6,7},{7,8},{8,9},{9,10},{10,1... | collective-permute-start | bytes 49160 | tf_op jit(solution)/shard_map/ppermute | solution.py:27
  149.9 0.7 collective-permute-done.20
  150.9 1.9 collective-permute-start.21
  152.9 5.4 %collective-permute-start.22 = (f32[4,2,1,512]{3,0,2,1:T(4,128)S(1)}, f32[4,2,1,512]{3,0,2,1:T(4,128)S(1)}, u32[]{:S(2)}, u32[]{:S(2)}) collective-permute-start(f32[4,2,1,512]{3,0,2,1:T(4,128)S(1)} %copy.449), channel_id=1, source_target_pairs={{0,1},{1,2},{2,3},{3,4},{4,5},{5,6},{6,7},{7,8},{8,9},{9,10},{10,1... | collective-permute-start | bytes 49160 | tf_op jit(solution)/shard_map/ppermute | solution.py:27
  158.4 0.7 collective-permute-done.22
  159.5 2.0 %copy.453 = f32[4,2,16,512]{2,3,1,0:T(8,128)} copy(f32[4,2,16,512]{3,1,2,0:T(2,128)S(1)} %bitcast.15) | data formatting | bytes 524288 | tf_op jit(solution)/shard_map/reshape | solution.py:69
  161.5 5.0 %broadcast_in_dim.23 = f32[4,2,16,512,2]{2,4,3,1,0:T(2,128)} broadcast(f32[4,2,16,512]{2,3,1,0:T(8,128)} %copy.453), dimensions={0,1,2,3} | broadcast | bytes 786432 | tf_op jit(solution)/shard_map/broadcast_in_dim | solution.py:69
  166.5 2.8 %copy.454 = f32[4,2,16,1024]{3,2,1,0:T(8,128)S(1)} copy(f32[4,2,16,1024]{2,3,1,0:T(8,128)} %bitcast.12) | data formatting | bytes 1048576 | tf_op jit(solution)/shard_map/reshape | solution.py:69
  169.6 1.9 collective-permute-start.23
  171.6 5.4 %collective-permute-start.24 = (f32[4,2,1,1024]{3,2,1,0:T(1,128)S(1)}, f32[4,2,1,1024]{3,2,1,0:T(1,128)S(1)}, u32[]{:S(2)}, u32[]{:S(2)}) collective-permute-start(f32[4,2,1,1024]{3,2,1,0:T(1,128)S(1)} %get-tuple-element.28), channel_id=1, source_target_pairs={{0,1},{1,2},{2,3},{3,4},{4,5},{5,6},{6,7},{7,8},{8,9},{9,10},{10,1... | collective-permute-start | bytes 98312 | tf_op jit(solution)/shard_map/ppermute | solution.py:27
  177.1 0.9 collective-permute-done.24
  178.7 2.1 %collective-permute-start.25 = (f32[4,2,1,1024]{3,2,1,0:T(1,128)S(1)}, f32[4,2,1,1024]{3,2,1,0:T(1,128)S(1)}, u32[]{:S(2)}, u32[]{:S(2)}) collective-permute-start(f32[4,2,1,1024]{3,2,1,0:T(1,128)S(1)} %get-tuple-element.21), channel_id=1, source_target_pairs={{1,0},{2,1},{3,2},{4,3},{5,4},{6,5},{7,6},{8,7},{9,8},{10,9},{11,1... | collective-permute-start | bytes 98312 | tf_op jit(solution)/shard_map/ppermute | solution.py:29
  180.8 5.4 %collective-permute-start.26 = (f32[4,2,1,1024]{3,2,1,0:T(1,128)S(1)}, f32[4,2,1,1024]{3,2,1,0:T(1,128)S(1)}, u32[]{:S(2)}, u32[]{:S(2)}) collective-permute-start(f32[4,2,1,1024]{3,2,1,0:T(1,128)S(1)} %get-tuple-element.22), channel_id=1, source_target_pairs={{0,1},{1,2},{2,3},{3,4},{4,5},{5,6},{6,7},{7,8},{8,9},{9,10},{10,1... | collective-permute-start | bytes 98312 | tf_op jit(solution)/shard_map/ppermute | solution.py:27
  186.3 0.9 collective-permute-done.26
  187.2 0.4 fusion.19
  188.0 1.9 collective-permute-start.27
  189.9 5.4 %collective-permute-start.28 = (f32[4,4,1,1024]{3,2,1,0:T(1,128)S(1)}, f32[4,4,1,1024]{3,2,1,0:T(1,128)S(1)}, u32[]{:S(2)}, u32[]{:S(2)}) collective-permute-start(f32[4,4,1,1024]{3,2,1,0:T(1,128)S(1)} %get-tuple-element.6), channel_id=1, source_target_pairs={{0,1},{1,2},{2,3},{3,4},{4,5},{5,6},{6,7},{7,8},{8,9},{9,10},{10,1... | collective-permute-start | bytes 196616 | tf_op jit(solution)/shard_map/ppermute | solution.py:27
  195.4 1.2 collective-permute-done.28
  196.7 1.5 fusion.7
  (121 shorter events, 7.4 us)
Async XLA Ops:
  0.0 16.9 %copy-start.4 = (f32[2]{0:T(128)S(1)}, f32[2]{0:T(128)}, u32[]{:S(2)}) copy-start(f32[2]{0:T(128)} %constant.66) | copy-start | bytes 28
  0.9 14.1 %collective-permute-start = (f32[1,2,16,1024]{3,2,1,0:T(8,128)S(1)}, f32[1,2,16,1024]{3,2,1,0:T(8,128)S(1)}, u32[]{:S(2)}, u32[]{:S(2)}) collective-permute-start(f32[1,2,16,1024]{3,2,1,0:T(8,128)S(1)} %slice.425), channel_id=1, source_target_pairs={{0,16},{16,32},{32,48},{48,64},{64,80},{80,96},{96,112},{112,128},... | collective-permute-start | bytes 393224 | tf_op jit(solution)/shard_map/ppermute | solution.py:39
  16.7 10.1 %copy-start.5 = (f32[2]{0:T(128)S(1)}, f32[2]{0:T(128)}, u32[]{:S(2)}) copy-start(f32[2]{0:T(128)} %constant.61) | copy-start | bytes 28
  18.4 8.1 %collective-permute-start.1 = (f32[4,2,1,1024]{3,2,1,0:T(1,128)S(1)}, f32[4,2,1,1024]{3,2,1,0:T(1,128)S(1)}, u32[]{:S(2)}, u32[]{:S(2)}) collective-permute-start(f32[4,2,1,1024]{3,2,1,0:T(1,128)S(1)} %get-tuple-element.39), channel_id=1, source_target_pairs={{1,0},{2,1},{3,2},{4,3},{5,4},{6,5},{7,6},{8,7},{9,8},{10,9},{11,1... | collective-permute-start | bytes 98312 | tf_op jit(solution)/shard_map/ppermute | solution.py:29
  21.6 5.3 %collective-permute-start.2 = (f32[4,2,1,1024]{3,2,1,0:T(1,128)S(1)}, f32[4,2,1,1024]{3,2,1,0:T(1,128)S(1)}, u32[]{:S(2)}, u32[]{:S(2)}) collective-permute-start(f32[4,2,1,1024]{3,2,1,0:T(1,128)S(1)} %get-tuple-element.40), channel_id=1, source_target_pairs={{0,1},{1,2},{2,3},{3,4},{4,5},{5,6},{6,7},{7,8},{8,9},{9,10},{10,1... | collective-permute-start | bytes 98312 | tf_op jit(solution)/shard_map/ppermute | solution.py:27
  27.6 7.5 %collective-permute-start.3 = (f32[4,2,1,1024]{3,2,1,0:T(1,128)S(1)}, f32[4,2,1,1024]{3,2,1,0:T(1,128)S(1)}, u32[]{:S(2)}, u32[]{:S(2)}) collective-permute-start(f32[4,2,1,1024]{3,2,1,0:T(1,128)S(1)} %get-tuple-element.33), channel_id=1, source_target_pairs={{1,0},{2,1},{3,2},{4,3},{5,4},{6,5},{7,6},{8,7},{9,8},{10,9},{11,1... | collective-permute-start | bytes 98312 | tf_op jit(solution)/shard_map/ppermute | solution.py:29
  29.5 6.4 %collective-permute-start.4 = (f32[4,2,1,1024]{3,2,1,0:T(1,128)S(1)}, f32[4,2,1,1024]{3,2,1,0:T(1,128)S(1)}, u32[]{:S(2)}, u32[]{:S(2)}) collective-permute-start(f32[4,2,1,1024]{3,2,1,0:T(1,128)S(1)} %get-tuple-element.34), channel_id=1, source_target_pairs={{0,1},{1,2},{2,3},{3,4},{4,5},{5,6},{6,7},{7,8},{8,9},{9,10},{10,1... | collective-permute-start | bytes 98312 | tf_op jit(solution)/shard_map/ppermute | solution.py:27
  62.7 2.9 %copy-start.6 = (f32[2]{0:T(128)S(1)}, f32[2]{0:T(128)}, u32[]{:S(2)}) copy-start(f32[2]{0:T(128)} %constant.68) | copy-start | bytes 28
  62.7 11.4 %copy-start.7 = (f32[2]{0:T(128)S(1)}, f32[2]{0:T(128)}, u32[]{:S(2)}) copy-start(f32[2]{0:T(128)} %constant.63) | copy-start | bytes 28
  65.8 7.5 %collective-permute-start.5 = (f32[4,2,1,512]{3,0,2,1:T(4,128)S(1)}, f32[4,2,1,512]{3,0,2,1:T(4,128)S(1)}, u32[]{:S(2)}, u32[]{:S(2)}) collective-permute-start(f32[4,2,1,512]{3,0,2,1:T(4,128)S(1)} %copy.422), channel_id=1, source_target_pairs={{1,0},{2,1},{3,2},{4,3},{5,4},{6,5},{7,6},{8,7},{9,8},{10,9},{11,1... | collective-permute-start | bytes 49160 | tf_op jit(solution)/shard_map/ppermute | solution.py:29
  67.8 6.3 %collective-permute-start.6 = (f32[4,2,1,512]{3,0,2,1:T(4,128)S(1)}, f32[4,2,1,512]{3,0,2,1:T(4,128)S(1)}, u32[]{:S(2)}, u32[]{:S(2)}) collective-permute-start(f32[4,2,1,512]{3,0,2,1:T(4,128)S(1)} %copy.424), channel_id=1, source_target_pairs={{0,1},{1,2},{2,3},{3,4},{4,5},{5,6},{6,7},{7,8},{8,9},{9,10},{10,1... | collective-permute-start | bytes 49160 | tf_op jit(solution)/shard_map/ppermute | solution.py:27
  74.4 7.4 %collective-permute-start.7 = (f32[4,2,1,512]{3,0,2,1:T(4,128)S(1)}, f32[4,2,1,512]{3,0,2,1:T(4,128)S(1)}, u32[]{:S(2)}, u32[]{:S(2)}) collective-permute-start(f32[4,2,1,512]{3,0,2,1:T(4,128)S(1)} %copy.427), channel_id=1, source_target_pairs={{1,0},{2,1},{3,2},{4,3},{5,4},{6,5},{7,6},{8,7},{9,8},{10,9},{11,1... | collective-permute-start | bytes 49160 | tf_op jit(solution)/shard_map/ppermute | solution.py:29
  76.3 6.3 %collective-permute-start.8 = (f32[4,2,1,512]{3,0,2,1:T(4,128)S(1)}, f32[4,2,1,512]{3,0,2,1:T(4,128)S(1)}, u32[]{:S(2)}, u32[]{:S(2)}) collective-permute-start(f32[4,2,1,512]{3,0,2,1:T(4,128)S(1)} %copy.429), channel_id=1, source_target_pairs={{0,1},{1,2},{2,3},{3,4},{4,5},{5,6},{6,7},{7,8},{8,9},{9,10},{10,1... | collective-permute-start | bytes 49160 | tf_op jit(solution)/shard_map/ppermute | solution.py:27
  85.4 6.1 %copy-start.2 = (f32[2]{0:T(128)S(1)}, f32[2]{0:T(128)}, u32[]{:S(2)}) copy-start(f32[2]{0:T(128)} %constant.70) | copy-start | bytes 28
  85.4 17.9 %copy-start.3 = (f32[2]{0:T(128)S(1)}, f32[2]{0:T(128)}, u32[]{:S(2)}) copy-start(f32[2]{0:T(128)} %constant.65) | copy-start | bytes 28
  91.7 7.4 %collective-permute-start.10 = (f32[4,2,1,256]{3,2,1,0:T(1,128)S(1)}, f32[4,2,1,256]{3,2,1,0:T(1,128)S(1)}, u32[]{:S(2)}, u32[]{:S(2)}) collective-permute-start(f32[4,2,1,256]{3,2,1,0:T(1,128)S(1)} %get-tuple-element.96), channel_id=1, source_target_pairs={{0,1},{1,2},{2,3},{3,4},{4,5},{5,6},{6,7},{7,8},{8,9},{9,10},{10,1... | collective-permute-start | bytes 24584 | tf_op jit(solution)/shard_map/ppermute | solution.py:27
  97.1 6.2 %collective-permute-start.9 = (f32[4,2,1,256]{3,2,1,0:T(1,128)S(1)}, f32[4,2,1,256]{3,2,1,0:T(1,128)S(1)}, u32[]{:S(2)}, u32[]{:S(2)}) collective-permute-start(f32[4,2,1,256]{3,2,1,0:T(1,128)S(1)} %get-tuple-element.95), channel_id=1, source_target_pairs={{1,0},{2,1},{3,2},{4,3},{5,4},{6,5},{7,6},{8,7},{9,8},{10,9},{11,1... | collective-permute-start | bytes 24584 | tf_op jit(solution)/shard_map/ppermute | solution.py:29
  103.5 6.9 %collective-permute-start.11 = (f32[4,2,1,256]{3,2,1,0:T(1,128)S(1)}, f32[4,2,1,256]{3,2,1,0:T(1,128)S(1)}, u32[]{:S(2)}, u32[]{:S(2)}) collective-permute-start(f32[4,2,1,256]{3,2,1,0:T(1,128)S(1)} %get-tuple-element.89), channel_id=1, source_target_pairs={{1,0},{2,1},{3,2},{4,3},{5,4},{6,5},{7,6},{8,7},{9,8},{10,9},{11,1... | collective-permute-start | bytes 24584 | tf_op jit(solution)/shard_map/ppermute | solution.py:29
  105.5 5.6 %collective-permute-start.12 = (f32[4,2,1,256]{3,2,1,0:T(1,128)S(1)}, f32[4,2,1,256]{3,2,1,0:T(1,128)S(1)}, u32[]{:S(2)}, u32[]{:S(2)}) collective-permute-start(f32[4,2,1,256]{3,2,1,0:T(1,128)S(1)} %get-tuple-element.90), channel_id=1, source_target_pairs={{0,1},{1,2},{2,3},{3,4},{4,5},{5,6},{6,7},{7,8},{8,9},{9,10},{10,1... | collective-permute-start | bytes 24584 | tf_op jit(solution)/shard_map/ppermute | solution.py:27
  111.3 7.4 %collective-permute-start.13 = (f32[4,2,1,256]{3,2,1,0:T(1,128)S(1)}, f32[4,2,1,256]{3,2,1,0:T(1,128)S(1)}, u32[]{:S(2)}, u32[]{:S(2)}) collective-permute-start(f32[4,2,1,256]{3,2,1,0:T(1,128)S(1)} %get-tuple-element.83), channel_id=1, source_target_pairs={{1,0},{2,1},{3,2},{4,3},{5,4},{6,5},{7,6},{8,7},{9,8},{10,9},{11,1... | collective-permute-start | bytes 24584 | tf_op jit(solution)/shard_map/ppermute | solution.py:29
  113.2 6.2 %collective-permute-start.14 = (f32[4,2,1,256]{3,2,1,0:T(1,128)S(1)}, f32[4,2,1,256]{3,2,1,0:T(1,128)S(1)}, u32[]{:S(2)}, u32[]{:S(2)}) collective-permute-start(f32[4,2,1,256]{3,2,1,0:T(1,128)S(1)} %get-tuple-element.84), channel_id=1, source_target_pairs={{0,1},{1,2},{2,3},{3,4},{4,5},{5,6},{6,7},{7,8},{8,9},{9,10},{10,1... | collective-permute-start | bytes 24584 | tf_op jit(solution)/shard_map/ppermute | solution.py:27
  119.6 7.4 %collective-permute-start.15 = (f32[4,2,1,256]{3,2,1,0:T(1,128)S(1)}, f32[4,2,1,256]{3,2,1,0:T(1,128)S(1)}, u32[]{:S(2)}, u32[]{:S(2)}) collective-permute-start(f32[4,2,1,256]{3,2,1,0:T(1,128)S(1)} %get-tuple-element.77), channel_id=1, source_target_pairs={{1,0},{2,1},{3,2},{4,3},{5,4},{6,5},{7,6},{8,7},{9,8},{10,9},{11,1... | collective-permute-start | bytes 24584 | tf_op jit(solution)/shard_map/ppermute | solution.py:29
  121.6 6.2 %collective-permute-start.16 = (f32[4,2,1,256]{3,2,1,0:T(1,128)S(1)}, f32[4,2,1,256]{3,2,1,0:T(1,128)S(1)}, u32[]{:S(2)}, u32[]{:S(2)}) collective-permute-start(f32[4,2,1,256]{3,2,1,0:T(1,128)S(1)} %get-tuple-element.78), channel_id=1, source_target_pairs={{0,1},{1,2},{2,3},{3,4},{4,5},{5,6},{6,7},{7,8},{8,9},{9,10},{10,1... | collective-permute-start | bytes 24584 | tf_op jit(solution)/shard_map/ppermute | solution.py:27
  128.0 7.6 %collective-permute-start.17 = (f32[4,2,1,256]{3,2,1,0:T(1,128)S(1)}, f32[4,2,1,256]{3,2,1,0:T(1,128)S(1)}, u32[]{:S(2)}, u32[]{:S(2)}) collective-permute-start(f32[4,2,1,256]{3,2,1,0:T(1,128)S(1)} %get-tuple-element.71), channel_id=1, source_target_pairs={{1,0},{2,1},{3,2},{4,3},{5,4},{6,5},{7,6},{8,7},{9,8},{10,9},{11,1... | collective-permute-start | bytes 24584 | tf_op jit(solution)/shard_map/ppermute | solution.py:29
  129.9 6.2 %collective-permute-start.18 = (f32[4,2,1,256]{3,2,1,0:T(1,128)S(1)}, f32[4,2,1,256]{3,2,1,0:T(1,128)S(1)}, u32[]{:S(2)}, u32[]{:S(2)}) collective-permute-start(f32[4,2,1,256]{3,2,1,0:T(1,128)S(1)} %get-tuple-element.72), channel_id=1, source_target_pairs={{0,1},{1,2},{2,3},{3,4},{4,5},{5,6},{6,7},{7,8},{8,9},{9,10},{10,1... | collective-permute-start | bytes 24584 | tf_op jit(solution)/shard_map/ppermute | solution.py:27
  142.4 7.4 %collective-permute-start.19 = (f32[4,2,1,512]{3,0,2,1:T(4,128)S(1)}, f32[4,2,1,512]{3,0,2,1:T(4,128)S(1)}, u32[]{:S(2)}, u32[]{:S(2)}) collective-permute-start(f32[4,2,1,512]{3,0,2,1:T(4,128)S(1)} %copy.442), channel_id=1, source_target_pairs={{1,0},{2,1},{3,2},{4,3},{5,4},{6,5},{7,6},{8,7},{9,8},{10,9},{11,1... | collective-permute-start | bytes 49160 | tf_op jit(solution)/shard_map/ppermute | solution.py:29
  144.4 6.3 %collective-permute-start.20 = (f32[4,2,1,512]{3,0,2,1:T(4,128)S(1)}, f32[4,2,1,512]{3,0,2,1:T(4,128)S(1)}, u32[]{:S(2)}, u32[]{:S(2)}) collective-permute-start(f32[4,2,1,512]{3,0,2,1:T(4,128)S(1)} %copy.444), channel_id=1, source_target_pairs={{0,1},{1,2},{2,3},{3,4},{4,5},{5,6},{6,7},{7,8},{8,9},{9,10},{10,1... | collective-permute-start | bytes 49160 | tf_op jit(solution)/shard_map/ppermute | solution.py:27
  150.9 7.4 %collective-permute-start.21 = (f32[4,2,1,512]{3,0,2,1:T(4,128)S(1)}, f32[4,2,1,512]{3,0,2,1:T(4,128)S(1)}, u32[]{:S(2)}, u32[]{:S(2)}) collective-permute-start(f32[4,2,1,512]{3,0,2,1:T(4,128)S(1)} %copy.447), channel_id=1, source_target_pairs={{1,0},{2,1},{3,2},{4,3},{5,4},{6,5},{7,6},{8,7},{9,8},{10,9},{11,1... | collective-permute-start | bytes 49160 | tf_op jit(solution)/shard_map/ppermute | solution.py:29
  152.9 6.3 %collective-permute-start.22 = (f32[4,2,1,512]{3,0,2,1:T(4,128)S(1)}, f32[4,2,1,512]{3,0,2,1:T(4,128)S(1)}, u32[]{:S(2)}, u32[]{:S(2)}) collective-permute-start(f32[4,2,1,512]{3,0,2,1:T(4,128)S(1)} %copy.449), channel_id=1, source_target_pairs={{0,1},{1,2},{2,3},{3,4},{4,5},{5,6},{6,7},{7,8},{8,9},{9,10},{10,1... | collective-permute-start | bytes 49160 | tf_op jit(solution)/shard_map/ppermute | solution.py:27
  169.6 7.4 %collective-permute-start.23 = (f32[4,2,1,1024]{3,2,1,0:T(1,128)S(1)}, f32[4,2,1,1024]{3,2,1,0:T(1,128)S(1)}, u32[]{:S(2)}, u32[]{:S(2)}) collective-permute-start(f32[4,2,1,1024]{3,2,1,0:T(1,128)S(1)} %get-tuple-element.27), channel_id=1, source_target_pairs={{1,0},{2,1},{3,2},{4,3},{5,4},{6,5},{7,6},{8,7},{9,8},{10,9},{11,1... | collective-permute-start | bytes 98312 | tf_op jit(solution)/shard_map/ppermute | solution.py:29
  171.6 6.4 %collective-permute-start.24 = (f32[4,2,1,1024]{3,2,1,0:T(1,128)S(1)}, f32[4,2,1,1024]{3,2,1,0:T(1,128)S(1)}, u32[]{:S(2)}, u32[]{:S(2)}) collective-permute-start(f32[4,2,1,1024]{3,2,1,0:T(1,128)S(1)} %get-tuple-element.28), channel_id=1, source_target_pairs={{0,1},{1,2},{2,3},{3,4},{4,5},{5,6},{6,7},{7,8},{8,9},{9,10},{10,1... | collective-permute-start | bytes 98312 | tf_op jit(solution)/shard_map/ppermute | solution.py:27
  178.6 18.1 %copy-start = (f32[4,2,16,1023]{3,2,1,0:T(8,128)S(1)}, f32[4,2,16,1023]{3,2,1,0:T(8,128)}, u32[]{:S(2)}) copy-start(f32[4,2,16,1023]{3,2,1,0:T(8,128)} %get-tuple-element.14) | copy-start | bytes 1571332
  178.6 18.1 %copy-start.1 = (f32[4,2,16,1]{3,2,1,0:T(8,128)S(1)}, f32[4,2,16,1]{3,2,1,0:T(8,128)}, u32[]{:S(2)}) copy-start(f32[4,2,16,1]{3,2,1,0:T(8,128)} %get-tuple-element.12) | copy-start | bytes 1540
  178.6 18.0 %copy-start.8 = (f32[2]{0:T(128)S(1)}, f32[2]{0:T(128)}, u32[]{:S(2)}) copy-start(f32[2]{0:T(128)} %constant.59.clone) | copy-start | bytes 28
  178.7 7.6 %collective-permute-start.25 = (f32[4,2,1,1024]{3,2,1,0:T(1,128)S(1)}, f32[4,2,1,1024]{3,2,1,0:T(1,128)S(1)}, u32[]{:S(2)}, u32[]{:S(2)}) collective-permute-start(f32[4,2,1,1024]{3,2,1,0:T(1,128)S(1)} %get-tuple-element.21), channel_id=1, source_target_pairs={{1,0},{2,1},{3,2},{4,3},{5,4},{6,5},{7,6},{8,7},{9,8},{10,9},{11,1... | collective-permute-start | bytes 98312 | tf_op jit(solution)/shard_map/ppermute | solution.py:29
  180.8 6.4 %collective-permute-start.26 = (f32[4,2,1,1024]{3,2,1,0:T(1,128)S(1)}, f32[4,2,1,1024]{3,2,1,0:T(1,128)S(1)}, u32[]{:S(2)}, u32[]{:S(2)}) collective-permute-start(f32[4,2,1,1024]{3,2,1,0:T(1,128)S(1)} %get-tuple-element.22), channel_id=1, source_target_pairs={{0,1},{1,2},{2,3},{3,4},{4,5},{5,6},{6,7},{7,8},{8,9},{9,10},{10,1... | collective-permute-start | bytes 98312 | tf_op jit(solution)/shard_map/ppermute | solution.py:27
  188.0 7.5 %collective-permute-start.27 = (f32[4,4,1,1024]{3,2,1,0:T(1,128)S(1)}, f32[4,4,1,1024]{3,2,1,0:T(1,128)S(1)}, u32[]{:S(2)}, u32[]{:S(2)}) collective-permute-start(f32[4,4,1,1024]{3,2,1,0:T(1,128)S(1)} %get-tuple-element.5), channel_id=1, source_target_pairs={{1,0},{2,1},{3,2},{4,3},{5,4},{6,5},{7,6},{8,7},{9,8},{10,9},{11,1... | collective-permute-start | bytes 196616 | tf_op jit(solution)/shard_map/ppermute | solution.py:29
  189.9 6.8 %collective-permute-start.28 = (f32[4,4,1,1024]{3,2,1,0:T(1,128)S(1)}, f32[4,4,1,1024]{3,2,1,0:T(1,128)S(1)}, u32[]{:S(2)}, u32[]{:S(2)}) collective-permute-start(f32[4,4,1,1024]{3,2,1,0:T(1,128)S(1)} %get-tuple-element.6), channel_id=1, source_target_pairs={{0,1},{1,2},{2,3},{3,4},{4,5},{5,6},{6,7},{7,8},{8,9},{9,10},{10,1... | collective-permute-start | bytes 196616 | tf_op jit(solution)/shard_map/ppermute | solution.py:27
where the time goes:
time: 200 us; the launch traced here: 198 us
  starting transfers between devices  107 us (54%)
  local copies, waits for them, and re-layouts  37.7 us (19%)
  other arithmetic  30.2 us (15%)
  waiting for transfers between devices  22.9 us (11%)
    ppermute x14, starting transfers between devices, padded(): lax.ppermute(tail, axis, [(i, (i + 1) % count) for i in range(ends)])  74.3 us
    ppermute x14, starting transfers between devices, padded(): lax.ppermute(head, axis, [((i + 1) % count, i) for i in range(ends)])  28.2 us
    reduce_sum x2, other arithmetic, restrict(): return jnp.sum(blocks, axis=(-3, -1))  23.4 us
    sub x2, local copies, waits for them, and re-layouts, cycle(): forcing_term - (diagonal_term * field - neighbours(field, strip_row_count...  11.4 us
    ppermute x14, waiting for transfers between devices, padded(): lax.ppermute(tail, axis, [(i, (i + 1) % count) for i in range(ends)])  9.89 us
    ppermute x1, waiting for transfers between devices, shifted(): lax.ppermute(value, axis, [(source, source + steps) for source in range(f...  8.82 us
    reshape x4, local copies, waits for them, and re-layouts, prolong(): return jnp.repeat(jnp.repeat(field, 2, axis=-2), 2, axis=-1)  8.09 us
    broadcast_in_dim x4, local copies, waits for them, and re-layouts, prolong(): return jnp.repeat(jnp.repeat(field, 2, axis=-2), 2, axis=-1)  7.79 us
  transfers between devices with their start and end apart: 29, of which 15 were waited for; matrix products, arithmetic and copies ran while one was open for 2% of the time, Pallas kernels for 0%

commit v1 on v0

v1 whole, which is shorter than its diff:
```python
import numpy as np
import jax
import jax.numpy as jnp
from jax import lax
from jax.experimental import pallas as pl
from jax.experimental.pallas import tpu as pltpu
from jax.sharding import PartitionSpec as P

GRID_HIERARCHY = 3
COARSE_SWEEPS = 6


smoothing_weight = 0.8
deform_term = 0.1
beta_slope = 0.5
bottom_friction_coefficient = 0.2
time_step = 0.5
meridional_weight = 1.8
zonal_weight = 0.2

SLOTS = 4
FIELDS = 2 * SLOTS
ROWS0 = 16
COLS0 = 1024
F0 = 3 * ROWS0
F1 = F0 // 2
F2 = F1
CHUNK = 8


def diag(level, mode):
    extra = np.float32(deform_term) * np.float32(4.0**level) if mode else np.float32(0.0)
    return float(np.float32(4.0) + extra)


def shifted(value, axis, steps):
    count = lax.axis_size(axis)
    first, last = (max(0, -steps), min(count, count - steps))
    return lax.ppermute(value, axis, [(source, source + steps) for source in range(first, last)])


def rolled(x, shift, axis):
    return pltpu.roll(x, shift % x.shape[axis], axis)


def stencil(f):
    up = rolled(f, -1, 0)
    down = rolled(f, 1, 0)
    along = rolled(f, -1, 1) + rolled(f, 1, 1)
    return meridional_weight * (up + down) + zonal_weight * along


def smooth(f, s, d, mask):
    applied = d * f - stencil(f)
    out = f + smoothing_weight * (s - applied) / d
    return jnp.where(mask, out, 0.0)


def residual(f, s, d, mask):
    return jnp.where(mask, s - (d * f - stencil(f)), 0.0)


def row_mask(band, count, lo, per_device, total):
    rows = band * per_device + lo + lax.broadcasted_iota(jnp.int32, (count, 1), 0)
    return (rows >= 0) & (rows < total)


def pair_matrix(fine, coarse_first):
    if coarse_first:
        shape, fine_dim = (fine // 2, fine), 1
    else:
        shape, fine_dim = (fine, fine // 2), 0
    f_idx = lax.broadcasted_iota(jnp.int32, shape, fine_dim)
    c_idx = lax.broadcasted_iota(jnp.int32, shape, 1 - fine_dim)
    return jnp.where(jnp.right_shift(f_idx, 1) == c_idx, 1.0, 0.0).astype(jnp.bfloat16)


def split_dot(x, m):
    hi = x.astype(jnp.bfloat16)
    rest = x - hi.astype(jnp.float32)
    mid = rest.astype(jnp.bfloat16)
    lo = (rest - mid.astype(jnp.float32)).astype(jnp.bfloat16)
    out = jnp.dot(hi, m, preferred_element_type=jnp.float32)
    out = out + jnp.dot(mid, m, preferred_element_type=jnp.float32)
    return out + jnp.dot(lo, m, preferred_element_type=jnp.float32)


def put_blocks(ref, rows, value):
    for j in range(ref.shape[0]):
        ref[j, rows, :] = value[:, j * 128 : (j + 1) * 128]


def get_blocks(ref, rows):
    return jnp.concatenate([ref[j, rows, :] for j in range(ref.shape[0])], axis=1)


def sources(lo_ref, own_ref, hi_ref, slot):
    q = [
        jnp.concatenate([lo_ref[slot, layer], own_ref[slot, layer], hi_ref[slot, layer]], axis=0)
        for layer in range(2)
    ]
    return q, [-(0.5 * (q[0] + q[1])), -(0.5 * (q[0] - q[1]))]


def first_kernel(band_ref, lo_ref, own_ref, hi_ref, f1_ref, s1_ref, g1_ref, t_ref, r0_ref, r1_ref):
    band = band_ref[0]
    mask0 = row_mask(band, F0, -ROWS0, ROWS0, ROWS0 * 16)
    for slot in range(SLOTS):
        _, src = sources(lo_ref, own_ref, hi_ref, slot)
        for mode in range(2):
            d = diag(0, mode)
            s = src[mode]
            f0 = smoothing_weight * s / d
            f1 = smooth(f0, s, d, mask0)
            rows = pl.ds((2 * slot + mode) * F0, F0)
            f1_ref[rows, :] = f1
            put_blocks(r0_ref, rows, residual(f1, s, d, mask0))
    half = FIELDS * F1
    paired = get_blocks(r0_ref, pl.ds(0, half, stride=2)) + get_blocks(r0_ref, pl.ds(1, half, stride=2))
    s1_ref[...] = split_dot(paired, pair_matrix(COLS0, False))
    mask1 = row_mask(band, F1, -ROWS0 // 2, ROWS0 // 2, ROWS0 * 8)
    for field in range(FIELDS):
        d = diag(1, field % 2)
        rows = pl.ds(field * F1, F1)
        s = s1_ref[rows, :]
        g0 = smoothing_weight * s / d
        g1 = smooth(g0, s, d, mask1)
        g1_ref[rows, :] = g1
        put_blocks(r1_ref, rows, residual(g1, s, d, mask1))
    chunks = []
    for field in range(FIELDS):
        start = field * F1 + ROWS0 // 2
        chunks.append(
            get_blocks(r1_ref, pl.ds(start, CHUNK, stride=2))
            + get_blocks(r1_ref, pl.ds(start + 1, CHUNK, stride=2))
        )
    paired = jnp.concatenate(chunks, axis=0)
    keep = jnp.bitwise_and(lax.broadcasted_iota(jnp.int32, (FIELDS * CHUNK, 1), 0), CHUNK - 1) < ROWS0 // 4
    paired = jnp.where(keep, paired, 0.0)
    t_ref[...] = split_dot(paired, pair_matrix(COLS0 // 2, False))


def second_kernel(
    band_ref, lo_ref, own_ref, hi_ref, f1_ref, s1_ref, g1_ref,
    tm2_ref, tm1_ref, t0_ref, tp1_ref, tp2_ref,
    out_ref,
    s2_ref, e2_ref, up1_ref, g4_ref, up0_ref,
):
    band = band_ref[0]
    below = rolled(tm1_ref[...], CHUNK // 2, 0)
    above = rolled(tp1_ref[...], CHUNK // 2, 0)
    for field in range(FIELDS):
        piece = pl.ds(field * CHUNK, CHUNK)
        base = field * F2
        s2_ref[pl.ds(base, CHUNK), :] = tm2_ref[piece, :] + below[field * CHUNK : (field + 1) * CHUNK]
        s2_ref[pl.ds(base + CHUNK, CHUNK), :] = t0_ref[piece, :] + above[field * CHUNK : (field + 1) * CHUNK]
        s2_ref[pl.ds(base + 2 * CHUNK, CHUNK), :] = tp2_ref[piece, :]
    mask2 = row_mask(band, F2, -CHUNK, ROWS0 // 4, ROWS0 * 4)
    for field in range(FIELDS):
        d = diag(2, field % 2)
        rows = pl.ds(field * F2, F2)
        s = s2_ref[rows, :]
        e = smoothing_weight * s / d
        for repeat in range(COARSE_SWEEPS - 1):
            e = smooth(e, s, d, mask2)
        e2_ref[rows, :] = e
    cols = split_dot(e2_ref[...], pair_matrix(COLS0 // 2, True))
    n2 = FIELDS * F2
    put_blocks(up1_ref, pl.ds(0, n2, stride=2), cols)
    put_blocks(up1_ref, pl.ds(1, n2, stride=2), cols)
    mask1 = row_mask(band, F1, -ROWS0 // 2, ROWS0 // 2, ROWS0 * 8)
    for field in range(FIELDS):
        d = diag(1, field % 2)
        rows = pl.ds(field * F1, F1)
        s = s1_ref[rows, :]
        g2 = g1_ref[rows, :] + get_blocks(up1_ref, pl.ds(field * 2 * F2 + CHUNK, F1))
        g3 = smooth(g2, s, d, mask1)
        g4_ref[rows, :] = smooth(g3, s, d, mask1)
    cols = split_dot(g4_ref[...], pair_matrix(COLS0, True))
    n1 = FIELDS * F1
    put_blocks(up0_ref, pl.ds(0, n1, stride=2), cols)
    put_blocks(up0_ref, pl.ds(1, n1, stride=2), cols)
    mask0 = row_mask(band, F0, -ROWS0, ROWS0, ROWS0 * 16)
    for slot in range(SLOTS):
        q, src = sources(lo_ref, own_ref, hi_ref, slot)
        modes = []
        for mode in range(2):
            d = diag(0, mode)
            rows = pl.ds((2 * slot + mode) * F0, F0)
            f2 = f1_ref[rows, :] + get_blocks(up0_ref, rows)
            f3 = smooth(f2, src[mode], d, mask0)
            modes.append(smooth(f3, src[mode], d, mask0))
        streams = [modes[0] + modes[1], modes[0] - modes[1]]
        for layer in range(2):
            stream = streams[layer]
            pv = q[layer]
            stream_x = 0.5 * (rolled(stream, -1, 1) - rolled(stream, 1, 1))
            stream_y = 0.5 * (rolled(stream, -1, 0) - rolled(stream, 1, 0))
            vort_x = 0.5 * (rolled(pv, -1, 1) - rolled(pv, 1, 1))
            vort_y = 0.5 * (rolled(pv, -1, 0) - rolled(pv, 1, 0))
            laplace = stencil(stream) - 4.0 * stream
            drag = bottom_friction_coefficient if layer else 0.0
            jacobian = stream_x * vort_y - stream_y * vort_x
            new = pv - time_step * (jacobian + beta_slope * stream_x + drag * laplace)
            out_ref[slot, layer] = new[ROWS0 : 2 * ROWS0]


def vmem():
    return pl.BlockSpec(memory_space=pltpu.VMEM)


def smem():
    return pl.BlockSpec(memory_space=pltpu.SMEM)


PARAMS = pltpu.CompilerParams(vmem_limit_bytes=48 * 1024 * 1024)


def per_device(states, counts):
    group = lax.axis_index("particle")
    per_group = states.shape[0]
    totals = jnp.cumsum(counts, dtype=jnp.int32)
    slots = group * per_group + jnp.arange(per_group, dtype=jnp.int32)
    ancestor = jnp.sum(
        (totals[None, :] <= slots[:, None]).astype(jnp.int32), axis=1, dtype=jnp.int32
    )
    below_last = shifted(states[-1:], "particle", 1)
    extended = jnp.concatenate([below_last, states], axis=0)
    local_index = ancestor - (group * per_group - 1)
    redrawn = jnp.take(extended, local_index, axis=0)

    band = lax.axis_index("band").astype(jnp.int32).reshape(1)
    lo_q = shifted(redrawn, "band", 1)
    hi_q = shifted(redrawn, "band", -1)
    f32 = jnp.float32
    f1, s1, g1, t = pl.pallas_call(
        first_kernel,
        out_shape=(
            jax.ShapeDtypeStruct((FIELDS * F0, COLS0), f32),
            jax.ShapeDtypeStruct((FIELDS * F1, COLS0 // 2), f32),
            jax.ShapeDtypeStruct((FIELDS * F1, COLS0 // 2), f32),
            jax.ShapeDtypeStruct((FIELDS * CHUNK, COLS0 // 4), f32),
        ),
        in_specs=[smem(), vmem(), vmem(), vmem()],
        out_specs=(vmem(), vmem(), vmem(), vmem()),
        scratch_shapes=[
            pltpu.VMEM((COLS0 // 128, FIELDS * F0, 128), f32),
            pltpu.VMEM((COLS0 // 256, FIELDS * F1, 128), f32),
        ],
        compiler_params=PARAMS,
    )(band, lo_q, redrawn, hi_q)
    tm2 = shifted(t, "band", 2)
    tm1 = shifted(t, "band", 1)
    tp1 = shifted(t, "band", -1)
    tp2 = shifted(t, "band", -2)
    return pl.pallas_call(
        second_kernel,
        out_shape=jax.ShapeDtypeStruct(redrawn.shape, f32),
        in_specs=[smem()] + [vmem()] * 11,
        out_specs=vmem(),
        scratch_shapes=[
            pltpu.VMEM((FIELDS * F2, COLS0 // 4), f32),
            pltpu.VMEM((FIELDS * F2, COLS0 // 4), f32),
            pltpu.VMEM((COLS0 // 256, 2 * FIELDS * F2, 128), f32),
            pltpu.VMEM((FIELDS * F1, COLS0 // 2), f32),
            pltpu.VMEM((COLS0 // 128, FIELDS * F0, 128), f32),
        ],
        compiler_params=PARAMS,
    )(band, lo_q, redrawn, hi_q, f1, s1, g1, tm2, tm1, t, tp1, tp2)


def solution(mesh):
    in_specs = (P("particle", None, "band", None), P())
    out_specs = P("particle", None, "band", None)
    return jax.shard_map(
        per_device, mesh=mesh, in_specs=in_specs, out_specs=out_specs, check_vma=False
    )
```

time: 200 us -> 57.7 us (0.29)
  the two profiles are of different devices: /device:TPU:31 before, /device:TPU:39 now
where the time goes in v1:
time: 57.7 us; the launch traced here: 57.4 us
  starting transfers between devices  22.2 us (38%)
  waiting for transfers between devices  19.1 us (33%)
  Pallas kernels  12 us (21%)
  local copies, waits for them, and re-layouts  2.26 us (4%)
  other arithmetic  1.68 us (3%)
    ppermute x7, starting transfers between devices, shifted(): lax.ppermute(value, axis, [(source, source + steps) for source in range(f...  22.2 us
    ppermute x7, waiting for transfers between devices, shifted(): lax.ppermute(value, axis, [(source, source + steps) for source in range(f...  19.1 us
    pallas_call x1, Pallas kernels, per_device(): pl.pallas_call(second_kernel, out_shape=jax.ShapeDtypeStruct(redrawn.shap...  7.75 us
    pallas_call x1, Pallas kernels, per_device(): pl.pallas_call(first_kernel, out_shape=(jax.ShapeDtypeStruct((FIELDS * F0...  4.22 us
  transfers between devices with their start and end apart: 7, of which 4 were waited for; matrix products, arithmetic and copies ran while one was open for 2% of the time, Pallas kernels for 0%

profile of v1, /device:TPU:39, one launch (start us, length us, event | category | flops | bytes accessed | tf_op | source)
XLA Modules:
  0.0 57.4 jit_solution(3547303241910837271)
XLA Ops:
  0.0 0.9 %slice.3 = f32[1,2,16,1024]{3,2,1,0:T(8,128)S(1)} slice(f32[4,2,16,1024]{3,2,1,0:T(8,128)} %param.2), slice={[3:4], [0:2], [0:16], [0:1024]} | slice | bytes 262144 | tf_op jit(solution)/shard_map/slice | solution.py:227
  0.9 4.0 %collective-permute-start = (f32[1,2,16,1024]{3,2,1,0:T(8,128)S(1)}, f32[1,2,16,1024]{3,2,1,0:T(8,128)S(1)}, u32[]{:S(2)}, u32[]{:S(2)}) collective-permute-start(f32[1,2,16,1024]{3,2,1,0:T(8,128)S(1)} %slice.3), channel_id=1, source_target_pairs={{0,16},{16,32},{32,48},{48,64},{64,80},{80,96},{96,112},{112,128},... | collective-permute-start | bytes 393224 | tf_op jit(solution)/shard_map/ppermute | solution.py:39
  4.9 0.8 %copy.5 = s32[128,1]{1,0:T(8,128)S(1)} copy(s32[128,1]{0,1:T(1,128)} %bitcast.6) | data formatting | bytes 1024 | tf_op jit(solution)/shard_map/reshape.42
  5.7 0.2 reduce-window.8
  5.9 0.1 reduce
  6.0 0.2 convert_reduce_fusion
  6.2 8.8 %collective-permute-done = f32[1,2,16,1024]{3,2,1,0:T(8,128)S(1)} collective-permute-done((f32[1,2,16,1024]{3,2,1,0:T(8,128)S(1)}, f32[1,2,16,1024]{3,2,1,0:T(8,128)S(1)}, u32[]{:S(2)}, u32[]{:S(2)}) %collective-permute-start) | collective-permute-done | bytes 131104 | tf_op jit(solution)/shard_map/ppermute | solution.py:39
  15.0 1.1 %pad_maximum_fusion = f32[5,2,16,1024]{3,2,1,0:T(8,128)S(1)} fusion(f32[4,2,16,1024]{3,2,1,0:T(8,128)} %param.2, f32[1,2,16,1024]{3,2,1,0:T(8,128)S(1)} %collective-permute-done), kind=kLoop, calls=%fused_computation.1 | loop fusion | flops 163840 | bytes 1310720 | tf_op jit(solution)/shard_map/concatenate | solution.py:228
  16.1 0.6 %gather_fusion = f32[4,2,16,1024]{3,2,1,0:T(8,128)S(1)} fusion(f32[5,2,16,1024]{3,2,1,0:T(8,128)S(1)} %pad_maximum_fusion, s32[1024]{0:T(1024)S(1)} %pad_clamp_fusion), kind=kCustom, calls=%fused_computation | custom fusion | bytes 1048592 | tf_op jit(solution)/shard_map/jit(_take)/gather | solution.py:230
  16.7 0.1 broadcast_select_fusion.own_ref
  16.8 3.2 %collective-permute-start.2 = (f32[4,2,16,1024]{3,2,1,0:T(8,128)S(1)}, f32[4,2,16,1024]{3,2,1,0:T(8,128)S(1)}, u32[]{:S(2)}, u32[]{:S(2)}) collective-permute-start(f32[4,2,16,1024]{3,2,1,0:T(8,128)S(1)} %broadcast_select_fusion.own_ref), channel_id=1, source_target_pairs={{1,0},{2,1},{3,2},{4,3},{5,4},{6,5},{7,6},{8,7},{9,8},{10,9},{11,1... | collective-permute-start | bytes 1572872 | tf_op jit(solution)/shard_map/ppermute | solution.py:39
  20.0 2.4 %collective-permute-start.1 = (f32[4,2,16,1024]{3,2,1,0:T(8,128)S(1)}, f32[4,2,16,1024]{3,2,1,0:T(8,128)S(1)}, u32[]{:S(2)}, u32[]{:S(2)}) collective-permute-start(f32[4,2,16,1024]{3,2,1,0:T(8,128)S(1)} %broadcast_select_fusion.own_ref), channel_id=1, source_target_pairs={{0,1},{1,2},{2,3},{3,4},{4,5},{5,6},{6,7},{7,8},{8,9},{9,10},{10,1... | collective-permute-start | bytes 1572872 | tf_op jit(solution)/shard_map/ppermute | solution.py:39
  22.4 5.2 %collective-permute-done.2.hi_ref = f32[4,2,16,1024]{3,2,1,0:T(8,128)S(1)} collective-permute-done((f32[4,2,16,1024]{3,2,1,0:T(8,128)S(1)}, f32[4,2,16,1024]{3,2,1,0:T(8,128)S(1)}, u32[]{:S(2)}, u32[]{:S(2)}) %collective-permute-start.2) | collective-permute-done | bytes 524320 | tf_op jit(solution)/shard_map/ppermute | solution.py:39
  27.6 0.9 %collective-permute-done.1.lo_ref = f32[4,2,16,1024]{3,2,1,0:T(8,128)S(1)} collective-permute-done((f32[4,2,16,1024]{3,2,1,0:T(8,128)S(1)}, f32[4,2,16,1024]{3,2,1,0:T(8,128)S(1)}, u32[]{:S(2)}, u32[]{:S(2)}) %collective-permute-start.1) | collective-permute-done | bytes 524320 | tf_op jit(solution)/shard_map/ppermute | solution.py:39
  28.5 4.2 %shard_map.28 = (f32[384,1024]{1,0:T(8,128)S(1)}, f32[192,512]{1,0:T(8,128)S(1)}, f32[192,512]{1,0:T(8,128)S(1)}, f32[64,256]{1,0:T(8,128)S(1)}) custom-call(s32[1]{0:T(128)} %bitcast.band_ref, f32[4,2,16,1024]{3,2,1,0:T(8,128)S(1)} %collective-permute-done.1.lo_ref, f32[4,2,16,1024]{3,2,1,0:T(8,128)S(1)} %broadcast_select_fusion.own_ref, ...), custom_call_target="tpu_custom_call" | custom-call | tf_op jit(solution)/shard_map/pallas_call | solution.py:236
  32.8 4.0 %collective-permute-start.6 = (f32[64,256]{1,0:T(8,128)S(1)}, f32[64,256]{1,0:T(8,128)S(1)}, u32[]{:S(2)}, u32[]{:S(2)}) collective-permute-start(f32[64,256]{1,0:T(8,128)S(1)} %get-tuple-element.12.t0_ref), channel_id=1, source_target_pairs={{2,0},{3,1},{4,2},{5,3},{6,4},{7,5},{8,6},{9,7},{10,8},{11,9},{12,... | collective-permute-start | bytes 196616 | tf_op jit(solution)/shard_map/ppermute | solution.py:39
  36.8 3.0 %collective-permute-start.5 = (f32[64,256]{1,0:T(8,128)S(1)}, f32[64,256]{1,0:T(8,128)S(1)}, u32[]{:S(2)}, u32[]{:S(2)}) collective-permute-start(f32[64,256]{1,0:T(8,128)S(1)} %get-tuple-element.12.t0_ref), channel_id=1, source_target_pairs={{1,0},{2,1},{3,2},{4,3},{5,4},{6,5},{7,6},{8,7},{9,8},{10,9},{11,1... | collective-permute-start | bytes 196616 | tf_op jit(solution)/shard_map/ppermute | solution.py:39
  39.8 3.5 %collective-permute-start.4 = (f32[64,256]{1,0:T(8,128)S(1)}, f32[64,256]{1,0:T(8,128)S(1)}, u32[]{:S(2)}, u32[]{:S(2)}) collective-permute-start(f32[64,256]{1,0:T(8,128)S(1)} %get-tuple-element.12.t0_ref), channel_id=1, source_target_pairs={{0,1},{1,2},{2,3},{3,4},{4,5},{5,6},{6,7},{7,8},{8,9},{9,10},{10,1... | collective-permute-start | bytes 196616 | tf_op jit(solution)/shard_map/ppermute | solution.py:39
  43.4 2.0 %collective-permute-start.3 = (f32[64,256]{1,0:T(8,128)S(1)}, f32[64,256]{1,0:T(8,128)S(1)}, u32[]{:S(2)}, u32[]{:S(2)}) collective-permute-start(f32[64,256]{1,0:T(8,128)S(1)} %get-tuple-element.12.t0_ref), channel_id=1, source_target_pairs={{0,2},{1,3},{2,4},{3,5},{4,6},{5,7},{6,8},{7,9},{8,10},{9,11},{10,... | collective-permute-start | bytes 196616 | tf_op jit(solution)/shard_map/ppermute | solution.py:39
  45.4 0.0 collective-permute-done.6.tp2_ref
  45.4 0.0 collective-permute-done.5.tp1_ref
  45.4 0.0 collective-permute-done.4.tm1_ref
  45.4 4.2 %collective-permute-done.3.tm2_ref = f32[64,256]{1,0:T(8,128)S(1)} collective-permute-done((f32[64,256]{1,0:T(8,128)S(1)}, f32[64,256]{1,0:T(8,128)S(1)}, u32[]{:S(2)}, u32[]{:S(2)}) %collective-permute-start.3) | collective-permute-done | bytes 65568 | tf_op jit(solution)/shard_map/ppermute | solution.py:39
  49.6 7.7 %shard_map.29 = f32[4,2,16,1024]{3,2,1,0:T(8,128)} custom-call(s32[1]{0:T(128)} %bitcast.band_ref, f32[4,2,16,1024]{3,2,1,0:T(8,128)S(1)} %collective-permute-done.1.lo_ref, f32[4,2,16,1024]{3,2,1,0:T(8,128)S(1)} %broadcast_select_fusion.own_ref, f32[4,2,16,1024]{3,2,1,0:T(8,128)S(1)} %collective-permute-done.2.hi_ref, ...), custom_call_target="tpu_custom_call" | custom-call | tf_op jit(solution)/shard_map/pallas_call | solution.py:256
  (4 shorter events, 0.0 us)
Async XLA Ops:
  0.9 14.1 %collective-permute-start = (f32[1,2,16,1024]{3,2,1,0:T(8,128)S(1)}, f32[1,2,16,1024]{3,2,1,0:T(8,128)S(1)}, u32[]{:S(2)}, u32[]{:S(2)}) collective-permute-start(f32[1,2,16,1024]{3,2,1,0:T(8,128)S(1)} %slice.3), channel_id=1, source_target_pairs={{0,16},{16,32},{32,48},{48,64},{64,80},{80,96},{96,112},{112,128},... | collective-permute-start | bytes 393224 | tf_op jit(solution)/shard_map/ppermute | solution.py:39
  16.8 10.8 %collective-permute-start.2 = (f32[4,2,16,1024]{3,2,1,0:T(8,128)S(1)}, f32[4,2,16,1024]{3,2,1,0:T(8,128)S(1)}, u32[]{:S(2)}, u32[]{:S(2)}) collective-permute-start(f32[4,2,16,1024]{3,2,1,0:T(8,128)S(1)} %broadcast_select_fusion.own_ref), channel_id=1, source_target_pairs={{1,0},{2,1},{3,2},{4,3},{5,4},{6,5},{7,6},{8,7},{9,8},{10,9},{11,1... | collective-permute-start | bytes 1572872 | tf_op jit(solution)/shard_map/ppermute | solution.py:39
  20.0 8.5 %collective-permute-start.1 = (f32[4,2,16,1024]{3,2,1,0:T(8,128)S(1)}, f32[4,2,16,1024]{3,2,1,0:T(8,128)S(1)}, u32[]{:S(2)}, u32[]{:S(2)}) collective-permute-start(f32[4,2,16,1024]{3,2,1,0:T(8,128)S(1)} %broadcast_select_fusion.own_ref), channel_id=1, source_target_pairs={{0,1},{1,2},{2,3},{3,4},{4,5},{5,6},{6,7},{7,8},{8,9},{9,10},{10,1... | collective-permute-start | bytes 1572872 | tf_op jit(solution)/shard_map/ppermute | solution.py:39
  32.8 12.6 %collective-permute-start.6 = (f32[64,256]{1,0:T(8,128)S(1)}, f32[64,256]{1,0:T(8,128)S(1)}, u32[]{:S(2)}, u32[]{:S(2)}) collective-permute-start(f32[64,256]{1,0:T(8,128)S(1)} %get-tuple-element.12.t0_ref), channel_id=1, source_target_pairs={{2,0},{3,1},{4,2},{5,3},{6,4},{7,5},{8,6},{9,7},{10,8},{11,9},{12,... | collective-permute-start | bytes 196616 | tf_op jit(solution)/shard_map/ppermute | solution.py:39
  36.8 8.6 %collective-permute-start.5 = (f32[64,256]{1,0:T(8,128)S(1)}, f32[64,256]{1,0:T(8,128)S(1)}, u32[]{:S(2)}, u32[]{:S(2)}) collective-permute-start(f32[64,256]{1,0:T(8,128)S(1)} %get-tuple-element.12.t0_ref), channel_id=1, source_target_pairs={{1,0},{2,1},{3,2},{4,3},{5,4},{6,5},{7,6},{8,7},{9,8},{10,9},{11,1... | collective-permute-start | bytes 196616 | tf_op jit(solution)/shard_map/ppermute | solution.py:39
  39.8 5.6 %collective-permute-start.4 = (f32[64,256]{1,0:T(8,128)S(1)}, f32[64,256]{1,0:T(8,128)S(1)}, u32[]{:S(2)}, u32[]{:S(2)}) collective-permute-start(f32[64,256]{1,0:T(8,128)S(1)} %get-tuple-element.12.t0_ref), channel_id=1, source_target_pairs={{0,1},{1,2},{2,3},{3,4},{4,5},{5,6},{6,7},{7,8},{8,9},{9,10},{10,1... | collective-permute-start | bytes 196616 | tf_op jit(solution)/shard_map/ppermute | solution.py:39
  43.4 6.3 %collective-permute-start.3 = (f32[64,256]{1,0:T(8,128)S(1)}, f32[64,256]{1,0:T(8,128)S(1)}, u32[]{:S(2)}, u32[]{:S(2)}) collective-permute-start(f32[64,256]{1,0:T(8,128)S(1)} %get-tuple-element.12.t0_ref), channel_id=1, source_target_pairs={{0,2},{1,3},{2,4},{3,5},{4,6},{5,7},{6,8},{7,9},{8,10},{9,11},{10,... | collective-permute-start | bytes 196616 | tf_op jit(solution)/shard_map/ppermute | solution.py:39

commit v2 on v1

--- a/solution.py
+++ b/solution.py
@@ -1,3 +1,5 @@
+import functools
+
 import numpy as np
 import jax
 import jax.numpy as jnp
@@ -141,22 +143,23 @@
 
 
 def second_kernel(
-    band_ref, lo_ref, own_ref, hi_ref, f1_ref, s1_ref, g1_ref,
+    slots, band_ref, lo_ref, own_ref, hi_ref, f1_ref, s1_ref, g1_ref,
     tm2_ref, tm1_ref, t0_ref, tp1_ref, tp2_ref,
     out_ref,
     s2_ref, e2_ref, up1_ref, g4_ref, up0_ref,
 ):
+    fields = 2 * slots
     band = band_ref[0]
     below = rolled(tm1_ref[...], CHUNK // 2, 0)
     above = rolled(tp1_ref[...], CHUNK // 2, 0)
-    for field in range(FIELDS):
+    for field in range(fields):
         piece = pl.ds(field * CHUNK, CHUNK)
         base = field * F2
         s2_ref[pl.ds(base, CHUNK), :] = tm2_ref[piece, :] + below[field * CHUNK : (field + 1) * CHUNK]
         s2_ref[pl.ds(base + CHUNK, CHUNK), :] = t0_ref[piece, :] + above[field * CHUNK : (field + 1) * CHUNK]
         s2_ref[pl.ds(base + 2 * CHUNK, CHUNK), :] = tp2_ref[piece, :]
     mask2 = row_mask(band, F2, -CHUNK, ROWS0 // 4, ROWS0 * 4)
-    for field in range(FIELDS):
+    for field in range(fields):
         d = diag(2, field % 2)
         rows = pl.ds(field * F2, F2)
         s = s2_ref[rows, :]
@@ -165,11 +168,11 @@
             e = smooth(e, s, d, mask2)
         e2_ref[rows, :] = e
     cols = split_dot(e2_ref[...], pair_matrix(COLS0 // 2, True))
-    n2 = FIELDS * F2
+    n2 = fields * F2
     put_blocks(up1_ref, pl.ds(0, n2, stride=2), cols)
     put_blocks(up1_ref, pl.ds(1, n2, stride=2), cols)
     mask1 = row_mask(band, F1, -ROWS0 // 2, ROWS0 // 2, ROWS0 * 8)
-    for field in range(FIELDS):
+    for field in range(fields):
         d = diag(1, field % 2)
         rows = pl.ds(field * F1, F1)
         s = s1_ref[rows, :]
@@ -177,11 +180,11 @@
         g3 = smooth(g2, s, d, mask1)
         g4_ref[rows, :] = smooth(g3, s, d, mask1)
     cols = split_dot(g4_ref[...], pair_matrix(COLS0, True))
-    n1 = FIELDS * F1
+    n1 = fields * F1
     put_blocks(up0_ref, pl.ds(0, n1, stride=2), cols)
     put_blocks(up0_ref, pl.ds(1, n1, stride=2), cols)
     mask0 = row_mask(band, F0, -ROWS0, ROWS0, ROWS0 * 16)
-    for slot in range(SLOTS):
+    for slot in range(slots):
         q, src = sources(lo_ref, own_ref, hi_ref, slot)
         modes = []
         for mode in range(2):
@@ -205,6 +208,15 @@
             out_ref[slot, layer] = new[ROWS0 : 2 * ROWS0]
 
 
+def pick_kernel(index_ref, below_ref, last_ref, rest_ref, out_ref):
+    for slot in range(SLOTS):
+        index = index_ref[slot]
+        value = last_ref[0]
+        for k in range(SLOTS - 2, -1, -1):
+            value = jnp.where(index == k + 1, rest_ref[k], value)
+        out_ref[slot] = jnp.where(index == 0, below_ref[0], value)
+
+
 def vmem():
     return pl.BlockSpec(memory_space=pltpu.VMEM)
 
@@ -224,14 +236,11 @@
     ancestor = jnp.sum(
         (totals[None, :] <= slots[:, None]).astype(jnp.int32), axis=1, dtype=jnp.int32
     )
-    below_last = shifted(states[-1:], "particle", 1)
-    extended = jnp.concatenate([below_last, states], axis=0)
     local_index = ancestor - (group * per_group - 1)
-    redrawn = jnp.take(extended, local_index, axis=0)
 
     band = lax.axis_index("band").astype(jnp.int32).reshape(1)
-    lo_q = shifted(redrawn, "band", 1)
-    hi_q = shifted(redrawn, "band", -1)
+    lo_q = shifted(states, "band", 1)
+    hi_q = shifted(states, "band", -1)
     f32 = jnp.float32
     f1, s1, g1, t = pl.pallas_call(
         first_kernel,
@@ -248,25 +257,52 @@
             pltpu.VMEM((COLS0 // 256, FIELDS * F1, 128), f32),
         ],
         compiler_params=PARAMS,
-    )(band, lo_q, redrawn, hi_q)
+    )(band, lo_q, states, hi_q)
     tm2 = shifted(t, "band", 2)
     tm1 = shifted(t, "band", 1)
     tp1 = shifted(t, "band", -1)
     tp2 = shifted(t, "band", -2)
+    args = (band, lo_q, states, hi_q, f1, s1, g1, tm2, tm1, t, tp1, tp2)
+    last = forecast_slots(SLOTS - 1, 1, args)
+    below = shifted(last, "particle", 1)
+    rest = forecast_slots(0, SLOTS - 1, args)
     return pl.pallas_call(
-        second_kernel,
-        out_shape=jax.ShapeDtypeStruct(redrawn.shape, f32),
-        in_specs=[smem()] + [vmem()] * 11,
+        pick_kernel,
+        out_shape=jax.ShapeDtypeStruct(states.shape, f32),
+        in_specs=[smem(), vmem(), vmem(), vmem()],
         out_specs=vmem(),
+    )(local_index, below, last, rest)
+
+
+def forecast_slots(first, slots, args):
+    fields = 2 * slots
+    block = first // slots
+
+    def rows(count, width):
+        return pl.BlockSpec((count, width), lambda i: (block, 0))
+
+    strips = pl.BlockSpec((slots, 2, ROWS0, COLS0), lambda i: (block, 0, 0, 0))
+    in_specs = [smem(), strips, strips, strips,
+                rows(fields * F0, COLS0), rows(fields * F1, COLS0 // 2), rows(fields * F1, COLS0 // 2)]
+    in_specs += [rows(fields * CHUNK, COLS0 // 4)] * 5
+    f32 = jnp.float32
+    work = fields * F0 * COLS0 * 160
+    return pl.pallas_call(
+        functools.partial(second_kernel, slots),
+        out_shape=jax.ShapeDtypeStruct((slots, 2, ROWS0, COLS0), f32),
+        grid=(1,),
+        in_specs=in_specs,
+        out_specs=pl.BlockSpec((slots, 2, ROWS0, COLS0), lambda i: (0, 0, 0, 0)),
         scratch_shapes=[
-            pltpu.VMEM((FIELDS * F2, COLS0 // 4), f32),
-            pltpu.VMEM((FIELDS * F2, COLS0 // 4), f32),
-            pltpu.VMEM((COLS0 // 256, 2 * FIELDS * F2, 128), f32),
-            pltpu.VMEM((FIELDS * F1, COLS0 // 2), f32),
-            pltpu.VMEM((COLS0 // 128, FIELDS * F0, 128), f32),
+            pltpu.VMEM((fields * F2, COLS0 // 4), f32),
+            pltpu.VMEM((fields * F2, COLS0 // 4), f32),
+            pltpu.VMEM((COLS0 // 256, 2 * fields * F2, 128), f32),
+            pltpu.VMEM((fields * F1, COLS0 // 2), f32),
+            pltpu.VMEM((COLS0 // 128, fields * F0, 128), f32),
         ],
         compiler_params=PARAMS,
-    )(band, lo_q, redrawn, hi_q, f1, s1, g1, tm2, tm1, t, tp1, tp2)
+        cost_estimate=pl.CostEstimate(flops=work, transcendentals=0, bytes_accessed=fields * F0 * COLS0 * 16),
+    )(*args)
 
 
 def solution(mesh):

time: 57.7 us -> 53.5 us (0.927)
  waiting for transfers between devices: 19.1 us -> 13.9 us
  Pallas kernels: 12 us -> 13.5 us
  local copies, waits for them, and re-layouts: 2.26 us -> 3.2 us
  starting transfers between devices: 22.2 us -> 21.5 us
  other arithmetic: 1.68 us -> 1.01 us
    ppermute x7, waiting for transfers between devices: 19.1 us -> 13.9 us  [shifted(): lax.ppermute(value, axis, [(source, source + steps) for source in range(f...]
    unnamed x0 -> x8, local copies, waits for them, and re-layouts: none -> 2.44 us
    pallas_call x1 -> x3, Pallas kernels: 7.75 us -> 9.26 us  [the longest x2 7.21 us: forecast_slots(): pl.pallas_call(functools.partial(second_kernel, slots), out_shape=jax.Sha...]
    concatenate x1 -> x0, other arithmetic: 1.09 us -> none  [per_device(): extended = jnp.concatenate([below_last, states], axis=0)]
    slice x1 -> x0, local copies, waits for them, and re-layouts: 0.91 us -> none  [per_device(): below_last = shifted(states[-1:], 'particle', 1)]
    ppermute x7, starting transfers between devices: 22.2 us -> 21.5 us  [shifted(): lax.ppermute(value, axis, [(source, source + steps) for source in range(f...]
    gather x1 -> x0, local copies, waits for them, and re-layouts: 0.58 us -> none  [per_device(): redrawn = jnp.take(extended, local_index, axis=0)]
  transfers between devices with their start and end apart: 7 -> 7, of which waited for: 4 -> 4; matrix products, arithmetic and copies ran while one was open for 2% -> 3% of each run, Pallas kernels for 0% -> 9%
where the time goes in v2:
time: 53.5 us; the launch traced here: 53.2 us
  starting transfers between devices  21.5 us (40%)
  waiting for transfers between devices  13.9 us (26%)
  Pallas kernels  13.5 us (25%)
  local copies, waits for them, and re-layouts  3.2 us (6%)
  other arithmetic  1.01 us (2%)
    ppermute x7, starting transfers between devices, shifted(): lax.ppermute(value, axis, [(source, source + steps) for source in range(f...  21.5 us
    ppermute x7, waiting for transfers between devices, shifted(): lax.ppermute(value, axis, [(source, source + steps) for source in range(f...  13.9 us
    pallas_call x2, Pallas kernels, forecast_slots(): pl.pallas_call(functools.partial(second_kernel, slots), out_shape=jax.Sha...  7.21 us
    pallas_call x1, Pallas kernels, per_device(): pl.pallas_call(first_kernel, out_shape=(jax.ShapeDtypeStruct((FIELDS * F0...  4.23 us
    unnamed x8, local copies, waits for them, and re-layouts  2.44 us
    pallas_call x1, Pallas kernels, per_device(): pl.pallas_call(pick_kernel, out_shape=jax.ShapeDtypeStruct(states.shape,...  2.05 us
  transfers between devices with their start and end apart: 7, of which 4 were waited for; matrix products, arithmetic and copies ran while one was open for 3% of the time, Pallas kernels for 9%

profile of v2, /device:TPU:39, one launch (start us, length us, event | category | flops | bytes accessed | tf_op | source)
XLA Modules:
  0.0 53.2 jit_solution(12319579594312046050)
XLA Ops:
  0.0 2.6 %collective-permute-start.1 = (f32[4,2,16,1024]{3,2,1,0:T(8,128)}, f32[4,2,16,1024]{3,2,1,0:T(8,128)S(1)}, u32[]{:S(2)}, u32[]{:S(2)}) collective-permute-start(f32[4,2,16,1024]{3,2,1,0:T(8,128)} %own_ref.5), channel_id=1, source_target_pairs={{1,0},{2,1},{3,2},{4,3},{5,4},{6,5},{7,6},{8,7},{9,8},{10,9},{11,1... | collective-permute-start | bytes 1572872 | tf_op jit(solution)/shard_map/ppermute | solution.py:41
  2.6 3.0 %collective-permute-start = (f32[4,2,16,1024]{3,2,1,0:T(8,128)}, f32[4,2,16,1024]{3,2,1,0:T(8,128)S(1)}, u32[]{:S(2)}, u32[]{:S(2)}) collective-permute-start(f32[4,2,16,1024]{3,2,1,0:T(8,128)} %own_ref.5), channel_id=1, source_target_pairs={{0,1},{1,2},{2,3},{3,4},{4,5},{5,6},{6,7},{7,8},{8,9},{9,10},{10,1... | collective-permute-start | bytes 1572872 | tf_op jit(solution)/shard_map/ppermute | solution.py:41
  5.6 0.8 %copy.5 = s32[128,1]{1,0:T(8,128)S(1)} copy(s32[128,1]{0,1:T(1,128)} %bitcast.2) | data formatting | bytes 1024 | tf_op jit(solution)/shard_map/reshape.21
  6.3 0.2 reduce-window.8
  6.5 0.1 reduce
  6.6 4.4 %collective-permute-done.1.hi_ref = f32[4,2,16,1024]{3,2,1,0:T(8,128)S(1)} collective-permute-done((f32[4,2,16,1024]{3,2,1,0:T(8,128)}, f32[4,2,16,1024]{3,2,1,0:T(8,128)S(1)}, u32[]{:S(2)}, u32[]{:S(2)}) %collective-permute-start.1) | collective-permute-done | bytes 524320 | tf_op jit(solution)/shard_map/ppermute | solution.py:41
  11.0 1.0 %collective-permute-done.lo_ref = f32[4,2,16,1024]{3,2,1,0:T(8,128)S(1)} collective-permute-done((f32[4,2,16,1024]{3,2,1,0:T(8,128)}, f32[4,2,16,1024]{3,2,1,0:T(8,128)S(1)}, u32[]{:S(2)}, u32[]{:S(2)}) %collective-permute-start) | collective-permute-done | bytes 524320 | tf_op jit(solution)/shard_map/ppermute | solution.py:41
  12.0 0.0 copy-start
  12.0 1.0 %copy-done = f32[4,2,16,1024]{3,2,1,0:T(8,128)S(1)} copy-done((f32[4,2,16,1024]{3,2,1,0:T(8,128)S(1)}, f32[4,2,16,1024]{3,2,1,0:T(8,128)}, u32[]{:S(2)}) %copy-start) | copy-done | bytes 524312
  13.0 4.2 %shard_map.28 = (f32[384,1024]{1,0:T(8,128)S(1)}, f32[192,512]{1,0:T(8,128)S(1)}, f32[192,512]{1,0:T(8,128)S(1)}, f32[64,256]{1,0:T(8,128)S(1)}) custom-call(s32[1]{0:T(128)} %bitcast.1.band_ref, f32[4,2,16,1024]{3,2,1,0:T(8,128)S(1)} %collective-permute-done.lo_ref, f32[4,2,16,1024]{3,2,1,0:T(8,128)S(1)} %copy-done, ...), custom_call_target="tpu_custom_call" | custom-call | tf_op jit(solution)/shard_map/pallas_call | solution.py:245
  17.3 3.4 %collective-permute-start.5 = (f32[64,256]{1,0:T(8,128)S(1)}, f32[64,256]{1,0:T(8,128)S(1)}, u32[]{:S(2)}, u32[]{:S(2)}) collective-permute-start(f32[64,256]{1,0:T(8,128)S(1)} %get-tuple-element.12.t0_ref), channel_id=1, source_target_pairs={{2,0},{3,1},{4,2},{5,3},{6,4},{7,5},{8,6},{9,7},{10,8},{11,9},{12,... | collective-permute-start | bytes 196616 | tf_op jit(solution)/shard_map/ppermute | solution.py:41
  20.7 2.9 %collective-permute-start.4 = (f32[64,256]{1,0:T(8,128)S(1)}, f32[64,256]{1,0:T(8,128)S(1)}, u32[]{:S(2)}, u32[]{:S(2)}) collective-permute-start(f32[64,256]{1,0:T(8,128)S(1)} %get-tuple-element.12.t0_ref), channel_id=1, source_target_pairs={{1,0},{2,1},{3,2},{4,3},{5,4},{6,5},{7,6},{8,7},{9,8},{10,9},{11,1... | collective-permute-start | bytes 196616 | tf_op jit(solution)/shard_map/ppermute | solution.py:41
  23.6 3.5 %collective-permute-start.3 = (f32[64,256]{1,0:T(8,128)S(1)}, f32[64,256]{1,0:T(8,128)S(1)}, u32[]{:S(2)}, u32[]{:S(2)}) collective-permute-start(f32[64,256]{1,0:T(8,128)S(1)} %get-tuple-element.12.t0_ref), channel_id=1, source_target_pairs={{0,1},{1,2},{2,3},{3,4},{4,5},{5,6},{6,7},{7,8},{8,9},{9,10},{10,1... | collective-permute-start | bytes 196616 | tf_op jit(solution)/shard_map/ppermute | solution.py:41
  27.2 2.0 %collective-permute-start.2 = (f32[64,256]{1,0:T(8,128)S(1)}, f32[64,256]{1,0:T(8,128)S(1)}, u32[]{:S(2)}, u32[]{:S(2)}) collective-permute-start(f32[64,256]{1,0:T(8,128)S(1)} %get-tuple-element.12.t0_ref), channel_id=1, source_target_pairs={{0,2},{1,3},{2,4},{3,5},{4,6},{5,7},{6,8},{7,9},{8,10},{9,11},{10,... | collective-permute-start | bytes 196616 | tf_op jit(solution)/shard_map/ppermute | solution.py:41
  29.2 0.2 convert_reduce_fusion
  29.4 0.0 collective-permute-done.5.tp2_ref
  29.4 0.0 collective-permute-done.4.tp1_ref
  29.4 0.0 collective-permute-done.3.tm1_ref
  29.4 4.0 %collective-permute-done.2.tm2_ref = f32[64,256]{1,0:T(8,128)S(1)} collective-permute-done((f32[64,256]{1,0:T(8,128)S(1)}, f32[64,256]{1,0:T(8,128)S(1)}, u32[]{:S(2)}, u32[]{:S(2)}) %collective-permute-start.2) | collective-permute-done | bytes 65568 | tf_op jit(solution)/shard_map/ppermute | solution.py:41
  33.4 2.3 %shard_map.29.last_ref = f32[1,2,16,1024]{3,2,1,0:T(8,128)S(1)} custom-call(s32[1]{0:T(128)} %bitcast.1.band_ref, f32[4,2,16,1024]{3,2,1,0:T(8,128)S(1)} %collective-permute-done.lo_ref, f32[4,2,16,1024]{3,2,1,0:T(8,128)S(1)} %copy-done, f32[4,2,16,1024]{3,2,1,0:T(8,128)S(1)} %collective-permute-done.1.hi_ref, f32[384,1024]{1,0:T(8,128)S(1)} %get-tuple-element.9.f1_ref, ...), custom_call_target="tpu_custom_call" | custom-call | flops 15728640 | bytes 1572864 | tf_op jit(solution)/shard_map/pallas_call | solution.py:290
  35.7 0.0 copy-start.2
  35.7 4.0 %collective-permute-start.6 = (f32[1,2,16,1024]{3,2,1,0:T(8,128)S(1)}, f32[1,2,16,1024]{3,2,1,0:T(8,128)S(1)}, u32[]{:S(2)}, u32[]{:S(2)}) collective-permute-start(f32[1,2,16,1024]{3,2,1,0:T(8,128)S(1)} %shard_map.29.last_ref), channel_id=1, source_target_pairs={{0,16},{16,32},{32,48},{48,64},{64,80},{80,96},{96,112},{112,128},... | collective-permute-start | bytes 393224 | tf_op jit(solution)/shard_map/ppermute | solution.py:41
  39.7 0.6 %broadcast_subtract_fusion.index_ref = s32[4]{0:T(128)} fusion(s32[4]{0:T(128)S(1)} %convert_reduce_fusion, s32[]{:T(128)S(6)} %sub.9), kind=kLoop, calls=%fused_computation.2 | loop fusion | flops 4 | bytes 36 | tf_op jit(solution)/shard_map/sub | solution.py:239
  40.3 5.0 %shard_map.30.rest_ref = f32[3,2,16,1024]{3,2,1,0:T(8,128)S(1)} custom-call(s32[1]{0:T(128)} %bitcast.1.band_ref, f32[4,2,16,1024]{3,2,1,0:T(8,128)S(1)} %collective-permute-done.lo_ref, f32[4,2,16,1024]{3,2,1,0:T(8,128)S(1)} %copy-done, f32[4,2,16,1024]{3,2,1,0:T(8,128)S(1)} %collective-permute-done.1.hi_ref, f32[384,1024]{1,0:T(8,128)S(1)} %get-tuple-element.9.f1_ref, ...), custom_call_target="tpu_custom_call" | custom-call | flops 47185920 | bytes 4718592 | tf_op jit(solution)/shard_map/pallas_call | solution.py:290
  45.2 0.0 copy-done.2
  45.3 0.0 copy-start.1
  45.3 0.7 %copy-done.1 = f32[3,2,16,1024]{3,2,1,0:T(8,128)} copy-done((f32[3,2,16,1024]{3,2,1,0:T(8,128)}, f32[3,2,16,1024]{3,2,1,0:T(8,128)S(1)}, u32[]{:S(2)}) %copy-start.1) | copy-done | bytes 393240
  46.0 4.5 %collective-permute-done.6.below_ref = f32[1,2,16,1024]{3,2,1,0:T(8,128)S(1)} collective-permute-done((f32[1,2,16,1024]{3,2,1,0:T(8,128)S(1)}, f32[1,2,16,1024]{3,2,1,0:T(8,128)S(1)}, u32[]{:S(2)}, u32[]{:S(2)}) %collective-permute-start.6) | collective-permute-done | bytes 131104 | tf_op jit(solution)/shard_map/ppermute | solution.py:41
  50.5 0.0 copy-start.3
  50.5 0.6 %copy-done.3 = f32[1,2,16,1024]{3,2,1,0:T(8,128)} copy-done((f32[1,2,16,1024]{3,2,1,0:T(8,128)}, f32[1,2,16,1024]{3,2,1,0:T(8,128)S(1)}, u32[]{:S(2)}) %copy-start.3) | copy-done | bytes 131096
  51.1 2.1 %shard_map.31 = f32[4,2,16,1024]{3,2,1,0:T(8,128)} custom-call(s32[4]{0:T(128)} %broadcast_subtract_fusion.index_ref, f32[1,2,16,1024]{3,2,1,0:T(8,128)} %copy-done.3, f32[1,2,16,1024]{3,2,1,0:T(8,128)} %copy-done.2, f32[3,2,16,1024]{3,2,1,0:T(8,128)} %copy-done.1), custom_call_target="tpu_custom_call" | custom-call | tf_op jit(solution)/shard_map/pallas_call | solution.py:269
  (1 shorter events, 0.0 us)
Async XLA Ops:
  0.0 11.0 %collective-permute-start.1 = (f32[4,2,16,1024]{3,2,1,0:T(8,128)}, f32[4,2,16,1024]{3,2,1,0:T(8,128)S(1)}, u32[]{:S(2)}, u32[]{:S(2)}) collective-permute-start(f32[4,2,16,1024]{3,2,1,0:T(8,128)} %own_ref.5), channel_id=1, source_target_pairs={{1,0},{2,1},{3,2},{4,3},{5,4},{6,5},{7,6},{8,7},{9,8},{10,9},{11,1... | collective-permute-start | bytes 1572872 | tf_op jit(solution)/shard_map/ppermute | solution.py:41
  2.6 9.4 %collective-permute-start = (f32[4,2,16,1024]{3,2,1,0:T(8,128)}, f32[4,2,16,1024]{3,2,1,0:T(8,128)S(1)}, u32[]{:S(2)}, u32[]{:S(2)}) collective-permute-start(f32[4,2,16,1024]{3,2,1,0:T(8,128)} %own_ref.5), channel_id=1, source_target_pairs={{0,1},{1,2},{2,3},{3,4},{4,5},{5,6},{6,7},{7,8},{8,9},{9,10},{10,1... | collective-permute-start | bytes 1572872 | tf_op jit(solution)/shard_map/ppermute | solution.py:41
  12.0 1.0 %copy-start = (f32[4,2,16,1024]{3,2,1,0:T(8,128)S(1)}, f32[4,2,16,1024]{3,2,1,0:T(8,128)}, u32[]{:S(2)}) copy-start(f32[4,2,16,1024]{3,2,1,0:T(8,128)} %own_ref.5) | copy-start | bytes 1572868
  17.3 12.1 %collective-permute-start.5 = (f32[64,256]{1,0:T(8,128)S(1)}, f32[64,256]{1,0:T(8,128)S(1)}, u32[]{:S(2)}, u32[]{:S(2)}) collective-permute-start(f32[64,256]{1,0:T(8,128)S(1)} %get-tuple-element.12.t0_ref), channel_id=1, source_target_pairs={{2,0},{3,1},{4,2},{5,3},{6,4},{7,5},{8,6},{9,7},{10,8},{11,9},{12,... | collective-permute-start | bytes 196616 | tf_op jit(solution)/shard_map/ppermute | solution.py:41
  20.7 8.7 %collective-permute-start.4 = (f32[64,256]{1,0:T(8,128)S(1)}, f32[64,256]{1,0:T(8,128)S(1)}, u32[]{:S(2)}, u32[]{:S(2)}) collective-permute-start(f32[64,256]{1,0:T(8,128)S(1)} %get-tuple-element.12.t0_ref), channel_id=1, source_target_pairs={{1,0},{2,1},{3,2},{4,3},{5,4},{6,5},{7,6},{8,7},{9,8},{10,9},{11,1... | collective-permute-start | bytes 196616 | tf_op jit(solution)/shard_map/ppermute | solution.py:41
  23.6 5.8 %collective-permute-start.3 = (f32[64,256]{1,0:T(8,128)S(1)}, f32[64,256]{1,0:T(8,128)S(1)}, u32[]{:S(2)}, u32[]{:S(2)}) collective-permute-start(f32[64,256]{1,0:T(8,128)S(1)} %get-tuple-element.12.t0_ref), channel_id=1, source_target_pairs={{0,1},{1,2},{2,3},{3,4},{4,5},{5,6},{6,7},{7,8},{8,9},{9,10},{10,1... | collective-permute-start | bytes 196616 | tf_op jit(solution)/shard_map/ppermute | solution.py:41
  27.2 6.3 %collective-permute-start.2 = (f32[64,256]{1,0:T(8,128)S(1)}, f32[64,256]{1,0:T(8,128)S(1)}, u32[]{:S(2)}, u32[]{:S(2)}) collective-permute-start(f32[64,256]{1,0:T(8,128)S(1)} %get-tuple-element.12.t0_ref), channel_id=1, source_target_pairs={{0,2},{1,3},{2,4},{3,5},{4,6},{5,7},{6,8},{7,9},{8,10},{9,11},{10,... | collective-permute-start | bytes 196616 | tf_op jit(solution)/shard_map/ppermute | solution.py:41
  35.7 9.5 %copy-start.2 = (f32[1,2,16,1024]{3,2,1,0:T(8,128)}, f32[1,2,16,1024]{3,2,1,0:T(8,128)S(1)}, u32[]{:S(2)}) copy-start(f32[1,2,16,1024]{3,2,1,0:T(8,128)S(1)} %shard_map.29.last_ref) | copy-start | bytes 393220
  35.7 14.8 %collective-permute-start.6 = (f32[1,2,16,1024]{3,2,1,0:T(8,128)S(1)}, f32[1,2,16,1024]{3,2,1,0:T(8,128)S(1)}, u32[]{:S(2)}, u32[]{:S(2)}) collective-permute-start(f32[1,2,16,1024]{3,2,1,0:T(8,128)S(1)} %shard_map.29.last_ref), channel_id=1, source_target_pairs={{0,16},{16,32},{32,48},{48,64},{64,80},{80,96},{96,112},{112,128},... | collective-permute-start | bytes 393224 | tf_op jit(solution)/shard_map/ppermute | solution.py:41
  45.3 0.8 %copy-start.1 = (f32[3,2,16,1024]{3,2,1,0:T(8,128)}, f32[3,2,16,1024]{3,2,1,0:T(8,128)S(1)}, u32[]{:S(2)}) copy-start(f32[3,2,16,1024]{3,2,1,0:T(8,128)S(1)} %shard_map.30.rest_ref) | copy-start | bytes 1179652
  50.5 0.6 %copy-start.3 = (f32[1,2,16,1024]{3,2,1,0:T(8,128)}, f32[1,2,16,1024]{3,2,1,0:T(8,128)S(1)}, u32[]{:S(2)}) copy-start(f32[1,2,16,1024]{3,2,1,0:T(8,128)S(1)} %collective-permute-done.6.below_ref) | copy-start | bytes 393220

commit v3 on v2

--- a/solution.py
+++ b/solution.py
@@ -96,19 +96,26 @@
     return jnp.concatenate([ref[j, rows, :] for j in range(ref.shape[0])], axis=1)
 
 
-def sources(lo_ref, own_ref, hi_ref, slot):
-    q = [
-        jnp.concatenate([lo_ref[slot, layer], own_ref[slot, layer], hi_ref[slot, layer]], axis=0)
-        for layer in range(2)
-    ]
+def sources(refs, index_ref, slot):
+    lo_ref, own_ref, hi_ref, blo_ref, bown_ref, bhi_ref = refs
+    index = index_ref[slot]
+    local = jnp.maximum(index - 1, 0)
+    below = index == 0
+    q = []
+    for layer in range(2):
+        pieces = [
+            jnp.where(below, b_ref[0, layer], x_ref[local, layer])
+            for b_ref, x_ref in ((blo_ref, lo_ref), (bown_ref, own_ref), (bhi_ref, hi_ref))
+        ]
+        q.append(jnp.concatenate(pieces, axis=0))
     return q, [-(0.5 * (q[0] + q[1])), -(0.5 * (q[0] - q[1]))]
 
 
-def first_kernel(band_ref, lo_ref, own_ref, hi_ref, f1_ref, s1_ref, g1_ref, t_ref, r0_ref, r1_ref):
+def first_kernel(band_ref, index_ref, lo_ref, own_ref, hi_ref, blo_ref, bown_ref, bhi_ref, f1_ref, s1_ref, g1_ref, t_ref, r0_ref, r1_ref):
     band = band_ref[0]
     mask0 = row_mask(band, F0, -ROWS0, ROWS0, ROWS0 * 16)
     for slot in range(SLOTS):
-        _, src = sources(lo_ref, own_ref, hi_ref, slot)
+        _, src = sources((lo_ref, own_ref, hi_ref, blo_ref, bown_ref, bhi_ref), index_ref, slot)
         for mode in range(2):
             d = diag(0, mode)
             s = src[mode]
@@ -143,7 +150,8 @@
 
 
 def second_kernel(
-    slots, band_ref, lo_ref, own_ref, hi_ref, f1_ref, s1_ref, g1_ref,
+    slots, band_ref, index_ref, lo_ref, own_ref, hi_ref, blo_ref, bown_ref, bhi_ref,
+    f1_ref, s1_ref, g1_ref,
     tm2_ref, tm1_ref, t0_ref, tp1_ref, tp2_ref,
     out_ref,
     s2_ref, e2_ref, up1_ref, g4_ref, up0_ref,
@@ -185,7 +193,7 @@
     put_blocks(up0_ref, pl.ds(1, n1, stride=2), cols)
     mask0 = row_mask(band, F0, -ROWS0, ROWS0, ROWS0 * 16)
     for slot in range(slots):
-        q, src = sources(lo_ref, own_ref, hi_ref, slot)
+        q, src = sources((lo_ref, own_ref, hi_ref, blo_ref, bown_ref, bhi_ref), index_ref, slot)
         modes = []
         for mode in range(2):
             d = diag(0, mode)
@@ -208,15 +216,6 @@
             out_ref[slot, layer] = new[ROWS0 : 2 * ROWS0]
 
 
-def pick_kernel(index_ref, below_ref, last_ref, rest_ref, out_ref):
-    for slot in range(SLOTS):
-        index = index_ref[slot]
-        value = last_ref[0]
-        for k in range(SLOTS - 2, -1, -1):
-            value = jnp.where(index == k + 1, rest_ref[k], value)
-        out_ref[slot] = jnp.where(index == 0, below_ref[0], value)
-
-
 def vmem():
     return pl.BlockSpec(memory_space=pltpu.VMEM)
 
@@ -241,6 +240,11 @@
     band = lax.axis_index("band").astype(jnp.int32).reshape(1)
     lo_q = shifted(states, "band", 1)
     hi_q = shifted(states, "band", -1)
+    last = states[per_group - 1 :]
+    below_own = shifted(last, "particle", 1)
+    below_lo = diagonal(last, 1, 1)
+    below_hi = diagonal(last, 1, -1)
+    pieces = (lo_q, states, hi_q, below_lo, below_own, below_hi)
     f32 = jnp.float32
     f1, s1, g1, t = pl.pallas_call(
         first_kernel,
@@ -250,49 +254,41 @@
             jax.ShapeDtypeStruct((FIELDS * F1, COLS0 // 2), f32),
             jax.ShapeDtypeStruct((FIELDS * CHUNK, COLS0 // 4), f32),
         ),
-        in_specs=[smem(), vmem(), vmem(), vmem()],
+        in_specs=[smem(), smem()] + [vmem()] * 6,
         out_specs=(vmem(), vmem(), vmem(), vmem()),
         scratch_shapes=[
             pltpu.VMEM((COLS0 // 128, FIELDS * F0, 128), f32),
             pltpu.VMEM((COLS0 // 256, FIELDS * F1, 128), f32),
         ],
         compiler_params=PARAMS,
-    )(band, lo_q, states, hi_q)
+    )(band, local_index, *pieces)
     tm2 = shifted(t, "band", 2)
     tm1 = shifted(t, "band", 1)
     tp1 = shifted(t, "band", -1)
     tp2 = shifted(t, "band", -2)
-    args = (band, lo_q, states, hi_q, f1, s1, g1, tm2, tm1, t, tp1, tp2)
-    last = forecast_slots(SLOTS - 1, 1, args)
-    below = shifted(last, "particle", 1)
-    rest = forecast_slots(0, SLOTS - 1, args)
-    return pl.pallas_call(
-        pick_kernel,
-        out_shape=jax.ShapeDtypeStruct(states.shape, f32),
-        in_specs=[smem(), vmem(), vmem(), vmem()],
-        out_specs=vmem(),
-    )(local_index, below, last, rest)
-
-
-def forecast_slots(first, slots, args):
+    return forecast_slots(SLOTS, (band, local_index) + pieces + (f1, s1, g1, tm2, tm1, t, tp1, tp2))
+
+
+def diagonal(value, particle_steps, band_steps):
+    particles, bands = lax.axis_size("particle"), lax.axis_size("band")
+    pairs = []
+    for p in range(particles):
+        for b in range(bands):
+            tp, tb = p + particle_steps, b + band_steps
+            if 0 <= tp < particles and 0 <= tb < bands:
+                pairs.append((p * bands + b, tp * bands + tb))
+    return lax.ppermute(value, ("particle", "band"), pairs)
+
+
+def forecast_slots(slots, args):
     fields = 2 * slots
-    block = first // slots
-
-    def rows(count, width):
-        return pl.BlockSpec((count, width), lambda i: (block, 0))
-
-    strips = pl.BlockSpec((slots, 2, ROWS0, COLS0), lambda i: (block, 0, 0, 0))
-    in_specs = [smem(), strips, strips, strips,
-                rows(fields * F0, COLS0), rows(fields * F1, COLS0 // 2), rows(fields * F1, COLS0 // 2)]
-    in_specs += [rows(fields * CHUNK, COLS0 // 4)] * 5
     f32 = jnp.float32
     work = fields * F0 * COLS0 * 160
     return pl.pallas_call(
         functools.partial(second_kernel, slots),
         out_shape=jax.ShapeDtypeStruct((slots, 2, ROWS0, COLS0), f32),
-        grid=(1,),
-        in_specs=in_specs,
-        out_specs=pl.BlockSpec((slots, 2, ROWS0, COLS0), lambda i: (0, 0, 0, 0)),
+        in_specs=[smem(), smem()] + [vmem()] * (len(args) - 2),
+        out_specs=vmem(),
         scratch_shapes=[
             pltpu.VMEM((fields * F2, COLS0 // 4), f32),
             pltpu.VMEM((fields * F2, COLS0 // 4), f32),

time: 53.5 us -> 56.6 us (1.058)
  starting transfers between devices: 21.5 us -> 29.9 us
  waiting for transfers between devices: 13.9 us -> 9.83 us
    ppermute x0 -> x2, starting transfers between devices: none -> 9.46 us  [diagonal(): return lax.ppermute(value, ('particle', 'band'), pairs)]
    ppermute x7, waiting for transfers between devices: 13.9 us -> 7.26 us  [shifted(): lax.ppermute(value, axis, [(source, source + steps) for source in range(f...]
    ppermute x0 -> x2, waiting for transfers between devices: none -> 2.58 us  [diagonal(): return lax.ppermute(value, ('particle', 'band'), pairs)]
    pallas_call x1 -> x0, Pallas kernels: 2.05 us -> none  [per_device(): pl.pallas_call(pick_kernel, out_shape=jax.ShapeDtypeStruct(states.shape,...]
    unnamed x8 -> x2, local copies, waits for them, and re-layouts: 2.44 us -> 1.04 us
    pallas_call x2 -> x1, Pallas kernels: 7.21 us -> 8.36 us  [forecast_slots(): pl.pallas_call(functools.partial(second_kernel, slots), out_shape=jax.Sha...]
    ppermute x7, starting transfers between devices: 21.5 us -> 20.4 us  [shifted(): lax.ppermute(value, axis, [(source, source + steps) for source in range(f...]
    slice x0 -> x1, local copies, waits for them, and re-layouts: none -> 0.92 us  [per_device(): last = states[per_group - 1:]]
  transfers between devices with their start and end apart: 7 -> 9, of which waited for: 4 -> 3; matrix products, arithmetic and copies ran while one was open for 3% -> 4% of each run, Pallas kernels for 9% -> 0%
where the time goes in v3:
time: 56.6 us; the launch traced here: 56.3 us
  starting transfers between devices  29.9 us (53%)
  Pallas kernels  13.2 us (23%)
  waiting for transfers between devices  9.83 us (17%)
  local copies, waits for them, and re-layouts  2.73 us (5%)
    ppermute x7, starting transfers between devices, shifted(): lax.ppermute(value, axis, [(source, source + steps) for source in range(f...  20.4 us
    ppermute x2, starting transfers between devices, diagonal(): return lax.ppermute(value, ('particle', 'band'), pairs)  9.46 us
    pallas_call x1, Pallas kernels, forecast_slots(): pl.pallas_call(functools.partial(second_kernel, slots), out_shape=jax.Sha...  8.36 us
    ppermute x7, waiting for transfers between devices, shifted(): lax.ppermute(value, axis, [(source, source + steps) for source in range(f...  7.26 us
    pallas_call x1, Pallas kernels, per_device(): pl.pallas_call(first_kernel, out_shape=(jax.ShapeDtypeStruct((FIELDS * F0...  4.82 us
    ppermute x2, waiting for transfers between devices, diagonal(): return lax.ppermute(value, ('particle', 'band'), pairs)  2.58 us
  transfers between devices with their start and end apart: 9, of which 3 were waited for; matrix products, arithmetic and copies ran while one was open for 4% of the time, Pallas kernels for 0%

profile of v3, /device:TPU:39, one launch (start us, length us, event | category | flops | bytes accessed | tf_op | source)
XLA Modules:
  0.0 56.3 jit_solution(2626830586278868692)
XLA Ops:
  0.0 2.6 %collective-permute-start.1 = (f32[4,2,16,1024]{3,2,1,0:T(8,128)}, f32[4,2,16,1024]{3,2,1,0:T(8,128)S(1)}, u32[]{:S(2)}, u32[]{:S(2)}) collective-permute-start(f32[4,2,16,1024]{3,2,1,0:T(8,128)} %own_ref.3), channel_id=1, source_target_pairs={{1,0},{2,1},{3,2},{4,3},{5,4},{6,5},{7,6},{8,7},{9,8},{10,9},{11,1... | collective-permute-start | bytes 1572872 | tf_op jit(solution)/shard_map/ppermute | solution.py:41
  2.6 3.0 %collective-permute-start = (f32[4,2,16,1024]{3,2,1,0:T(8,128)}, f32[4,2,16,1024]{3,2,1,0:T(8,128)S(1)}, u32[]{:S(2)}, u32[]{:S(2)}) collective-permute-start(f32[4,2,16,1024]{3,2,1,0:T(8,128)} %own_ref.3), channel_id=1, source_target_pairs={{0,1},{1,2},{2,3},{3,4},{4,5},{5,6},{6,7},{7,8},{8,9},{9,10},{10,1... | collective-permute-start | bytes 1572872 | tf_op jit(solution)/shard_map/ppermute | solution.py:41
  5.6 0.9 %slice.3 = f32[1,2,16,1024]{3,2,1,0:T(8,128)S(1)} slice(f32[4,2,16,1024]{3,2,1,0:T(8,128)} %own_ref.3), slice={[3:4], [0:2], [0:16], [0:1024]} | slice | bytes 262144 | tf_op jit(solution)/shard_map/slice | solution.py:243
  6.5 3.3 %collective-permute-start.4 = (f32[1,2,16,1024]{3,2,1,0:T(8,128)S(1)}, f32[1,2,16,1024]{3,2,1,0:T(8,128)S(1)}, u32[]{:S(2)}, u32[]{:S(2)}) collective-permute-start(f32[1,2,16,1024]{3,2,1,0:T(8,128)S(1)} %slice.3), channel_id=1, source_target_pairs={{1,16},{2,17},{3,18},{4,19},{5,20},{6,21},{7,22},{8,23},{9,24},{10... | collective-permute-start | bytes 393224 | tf_op jit(solution)/shard_map/ppermute | solution.py:280
  9.8 4.0 %collective-permute-start.3 = (f32[1,2,16,1024]{3,2,1,0:T(8,128)S(1)}, f32[1,2,16,1024]{3,2,1,0:T(8,128)S(1)}, u32[]{:S(2)}, u32[]{:S(2)}) collective-permute-start(f32[1,2,16,1024]{3,2,1,0:T(8,128)S(1)} %slice.3), channel_id=1, source_target_pairs={{0,16},{16,32},{32,48},{48,64},{64,80},{80,96},{96,112},{112,128},... | collective-permute-start | bytes 393224 | tf_op jit(solution)/shard_map/ppermute | solution.py:41
  13.8 6.1 %collective-permute-start.2 = (f32[1,2,16,1024]{3,2,1,0:T(8,128)S(1)}, f32[1,2,16,1024]{3,2,1,0:T(8,128)S(1)}, u32[]{:S(2)}, u32[]{:S(2)}) collective-permute-start(f32[1,2,16,1024]{3,2,1,0:T(8,128)S(1)} %slice.3), channel_id=1, source_target_pairs={{0,17},{1,18},{2,19},{3,20},{4,21},{5,22},{6,23},{7,24},{8,25},{9,... | collective-permute-start | bytes 393224 | tf_op jit(solution)/shard_map/ppermute | solution.py:280
  20.0 0.8 %copy.5 = s32[128,1]{1,0:T(8,128)S(1)} copy(s32[128,1]{0,1:T(1,128)} %bitcast.2) | data formatting | bytes 1024 | tf_op jit(solution)/shard_map/reshape.21
  20.8 0.2 reduce-window.8
  20.9 0.1 reduce
  21.0 0.2 convert_reduce_fusion
  21.2 0.0 collective-permute-done.4.bhi_ref
  21.2 3.0 %collective-permute-done.3.bown_ref = f32[1,2,16,1024]{3,2,1,0:T(8,128)S(1)} collective-permute-done((f32[1,2,16,1024]{3,2,1,0:T(8,128)S(1)}, f32[1,2,16,1024]{3,2,1,0:T(8,128)S(1)}, u32[]{:S(2)}, u32[]{:S(2)}) %collective-permute-start.3) | collective-permute-done | bytes 131104 | tf_op jit(solution)/shard_map/ppermute | solution.py:41
  24.2 2.6 %collective-permute-done.2.blo_ref = f32[1,2,16,1024]{3,2,1,0:T(8,128)S(1)} collective-permute-done((f32[1,2,16,1024]{3,2,1,0:T(8,128)S(1)}, f32[1,2,16,1024]{3,2,1,0:T(8,128)S(1)}, u32[]{:S(2)}, u32[]{:S(2)}) %collective-permute-start.2) | collective-permute-done | bytes 131104 | tf_op jit(solution)/shard_map/ppermute | solution.py:280
  26.8 0.0 collective-permute-done.1.hi_ref
  26.8 0.0 collective-permute-done.lo_ref
  26.8 0.0 copy-start
  26.8 1.0 %copy-done = f32[4,2,16,1024]{3,2,1,0:T(8,128)S(1)} copy-done((f32[4,2,16,1024]{3,2,1,0:T(8,128)S(1)}, f32[4,2,16,1024]{3,2,1,0:T(8,128)}, u32[]{:S(2)}) %copy-start) | copy-done | bytes 524312
  27.9 4.8 %shard_map.28 = (f32[384,1024]{1,0:T(8,128)S(1)}, f32[192,512]{1,0:T(8,128)S(1)}, f32[192,512]{1,0:T(8,128)S(1)}, f32[64,256]{1,0:T(8,128)S(1)}) custom-call(s32[1]{0:T(128)} %bitcast.band_ref, s32[4]{0:T(128)S(1)} %broadcast_subtract_fusion.index_ref, f32[4,2,16,1024]{3,2,1,0:T(8,128)S(1)} %collective-permute-done.lo_ref, f32[4,2,16,1024]{3,2,1,0:T(8,128)S(1)} %copy-done, ...), custom_call_target="tpu_custom_call" | custom-call | tf_op jit(solution)/shard_map/pallas_call | solution.py:249
  32.7 3.4 %collective-permute-start.8 = (f32[64,256]{1,0:T(8,128)S(1)}, f32[64,256]{1,0:T(8,128)S(1)}, u32[]{:S(2)}, u32[]{:S(2)}) collective-permute-start(f32[64,256]{1,0:T(8,128)S(1)} %get-tuple-element.12.t0_ref), channel_id=1, source_target_pairs={{2,0},{3,1},{4,2},{5,3},{6,4},{7,5},{8,6},{9,7},{10,8},{11,9},{12,... | collective-permute-start | bytes 196616 | tf_op jit(solution)/shard_map/ppermute | solution.py:41
  36.1 1.9 %collective-permute-start.7 = (f32[64,256]{1,0:T(8,128)S(1)}, f32[64,256]{1,0:T(8,128)S(1)}, u32[]{:S(2)}, u32[]{:S(2)}) collective-permute-start(f32[64,256]{1,0:T(8,128)S(1)} %get-tuple-element.12.t0_ref), channel_id=1, source_target_pairs={{1,0},{2,1},{3,2},{4,3},{5,4},{6,5},{7,6},{8,7},{9,8},{10,9},{11,1... | collective-permute-start | bytes 196616 | tf_op jit(solution)/shard_map/ppermute | solution.py:41
  38.0 3.6 %collective-permute-start.6 = (f32[64,256]{1,0:T(8,128)S(1)}, f32[64,256]{1,0:T(8,128)S(1)}, u32[]{:S(2)}, u32[]{:S(2)}) collective-permute-start(f32[64,256]{1,0:T(8,128)S(1)} %get-tuple-element.12.t0_ref), channel_id=1, source_target_pairs={{0,1},{1,2},{2,3},{3,4},{4,5},{5,6},{6,7},{7,8},{8,9},{9,10},{10,1... | collective-permute-start | bytes 196616 | tf_op jit(solution)/shard_map/ppermute | solution.py:41
  41.7 1.9 %collective-permute-start.5 = (f32[64,256]{1,0:T(8,128)S(1)}, f32[64,256]{1,0:T(8,128)S(1)}, u32[]{:S(2)}, u32[]{:S(2)}) collective-permute-start(f32[64,256]{1,0:T(8,128)S(1)} %get-tuple-element.12.t0_ref), channel_id=1, source_target_pairs={{0,2},{1,3},{2,4},{3,5},{4,6},{5,7},{6,8},{7,9},{8,10},{9,11},{10,... | collective-permute-start | bytes 196616 | tf_op jit(solution)/shard_map/ppermute | solution.py:41
  43.6 0.0 collective-permute-done.8.tp2_ref
  43.6 0.0 collective-permute-done.7.tp1_ref
  43.6 0.0 collective-permute-done.6.tm1_ref
  43.6 4.3 %collective-permute-done.5.tm2_ref = f32[64,256]{1,0:T(8,128)S(1)} collective-permute-done((f32[64,256]{1,0:T(8,128)S(1)}, f32[64,256]{1,0:T(8,128)S(1)}, u32[]{:S(2)}, u32[]{:S(2)}) %collective-permute-start.5) | collective-permute-done | bytes 65568 | tf_op jit(solution)/shard_map/ppermute | solution.py:41
  47.9 8.4 %shard_map.29 = f32[4,2,16,1024]{3,2,1,0:T(8,128)} custom-call(s32[1]{0:T(128)} %bitcast.band_ref, s32[4]{0:T(128)S(1)} %broadcast_subtract_fusion.index_ref, f32[4,2,16,1024]{3,2,1,0:T(8,128)S(1)} %collective-permute-done.lo_ref, f32[4,2,16,1024]{3,2,1,0:T(8,128)S(1)} %copy-done, f32[4,2,16,1024]{3,2,1,0:T(8,128)S(1)} %collective-permute-done.1.hi_ref, ...), custom_call_target="tpu_custom_call" | custom-call | flops 62914560 | bytes 6291456 | tf_op jit(solution)/shard_map/pallas_call | solution.py:287
  (2 shorter events, 0.0 us)
Async XLA Ops:
  0.0 26.8 %collective-permute-start.1 = (f32[4,2,16,1024]{3,2,1,0:T(8,128)}, f32[4,2,16,1024]{3,2,1,0:T(8,128)S(1)}, u32[]{:S(2)}, u32[]{:S(2)}) collective-permute-start(f32[4,2,16,1024]{3,2,1,0:T(8,128)} %own_ref.3), channel_id=1, source_target_pairs={{1,0},{2,1},{3,2},{4,3},{5,4},{6,5},{7,6},{8,7},{9,8},{10,9},{11,1... | collective-permute-start | bytes 1572872 | tf_op jit(solution)/shard_map/ppermute | solution.py:41
  2.6 24.2 %collective-permute-start = (f32[4,2,16,1024]{3,2,1,0:T(8,128)}, f32[4,2,16,1024]{3,2,1,0:T(8,128)S(1)}, u32[]{:S(2)}, u32[]{:S(2)}) collective-permute-start(f32[4,2,16,1024]{3,2,1,0:T(8,128)} %own_ref.3), channel_id=1, source_target_pairs={{0,1},{1,2},{2,3},{3,4},{4,5},{5,6},{6,7},{7,8},{8,9},{9,10},{10,1... | collective-permute-start | bytes 1572872 | tf_op jit(solution)/shard_map/ppermute | solution.py:41
  6.5 14.7 %collective-permute-start.4 = (f32[1,2,16,1024]{3,2,1,0:T(8,128)S(1)}, f32[1,2,16,1024]{3,2,1,0:T(8,128)S(1)}, u32[]{:S(2)}, u32[]{:S(2)}) collective-permute-start(f32[1,2,16,1024]{3,2,1,0:T(8,128)S(1)} %slice.3), channel_id=1, source_target_pairs={{1,16},{2,17},{3,18},{4,19},{5,20},{6,21},{7,22},{8,23},{9,24},{10... | collective-permute-start | bytes 393224 | tf_op jit(solution)/shard_map/ppermute | solution.py:280
  9.8 14.4 %collective-permute-start.3 = (f32[1,2,16,1024]{3,2,1,0:T(8,128)S(1)}, f32[1,2,16,1024]{3,2,1,0:T(8,128)S(1)}, u32[]{:S(2)}, u32[]{:S(2)}) collective-permute-start(f32[1,2,16,1024]{3,2,1,0:T(8,128)S(1)} %slice.3), channel_id=1, source_target_pairs={{0,16},{16,32},{32,48},{48,64},{64,80},{80,96},{96,112},{112,128},... | collective-permute-start | bytes 393224 | tf_op jit(solution)/shard_map/ppermute | solution.py:41
  13.8 13.0 %collective-permute-start.2 = (f32[1,2,16,1024]{3,2,1,0:T(8,128)S(1)}, f32[1,2,16,1024]{3,2,1,0:T(8,128)S(1)}, u32[]{:S(2)}, u32[]{:S(2)}) collective-permute-start(f32[1,2,16,1024]{3,2,1,0:T(8,128)S(1)} %slice.3), channel_id=1, source_target_pairs={{0,17},{1,18},{2,19},{3,20},{4,21},{5,22},{6,23},{7,24},{8,25},{9,... | collective-permute-start | bytes 393224 | tf_op jit(solution)/shard_map/ppermute | solution.py:280
  26.8 1.0 %copy-start = (f32[4,2,16,1024]{3,2,1,0:T(8,128)S(1)}, f32[4,2,16,1024]{3,2,1,0:T(8,128)}, u32[]{:S(2)}) copy-start(f32[4,2,16,1024]{3,2,1,0:T(8,128)} %own_ref.3) | copy-start | bytes 1572868
  32.7 10.9 %collective-permute-start.8 = (f32[64,256]{1,0:T(8,128)S(1)}, f32[64,256]{1,0:T(8,128)S(1)}, u32[]{:S(2)}, u32[]{:S(2)}) collective-permute-start(f32[64,256]{1,0:T(8,128)S(1)} %get-tuple-element.12.t0_ref), channel_id=1, source_target_pairs={{2,0},{3,1},{4,2},{5,3},{6,4},{7,5},{8,6},{9,7},{10,8},{11,9},{12,... | collective-permute-start | bytes 196616 | tf_op jit(solution)/shard_map/ppermute | solution.py:41
  36.1 7.5 %collective-permute-start.7 = (f32[64,256]{1,0:T(8,128)S(1)}, f32[64,256]{1,0:T(8,128)S(1)}, u32[]{:S(2)}, u32[]{:S(2)}) collective-permute-start(f32[64,256]{1,0:T(8,128)S(1)} %get-tuple-element.12.t0_ref), channel_id=1, source_target_pairs={{1,0},{2,1},{3,2},{4,3},{5,4},{6,5},{7,6},{8,7},{9,8},{10,9},{11,1... | collective-permute-start | bytes 196616 | tf_op jit(solution)/shard_map/ppermute | solution.py:41
  38.0 5.6 %collective-permute-start.6 = (f32[64,256]{1,0:T(8,128)S(1)}, f32[64,256]{1,0:T(8,128)S(1)}, u32[]{:S(2)}, u32[]{:S(2)}) collective-permute-start(f32[64,256]{1,0:T(8,128)S(1)} %get-tuple-element.12.t0_ref), channel_id=1, source_target_pairs={{0,1},{1,2},{2,3},{3,4},{4,5},{5,6},{6,7},{7,8},{8,9},{9,10},{10,1... | collective-permute-start | bytes 196616 | tf_op jit(solution)/shard_map/ppermute | solution.py:41
  41.7 6.2 %collective-permute-start.5 = (f32[64,256]{1,0:T(8,128)S(1)}, f32[64,256]{1,0:T(8,128)S(1)}, u32[]{:S(2)}, u32[]{:S(2)}) collective-permute-start(f32[64,256]{1,0:T(8,128)S(1)} %get-tuple-element.12.t0_ref), channel_id=1, source_target_pairs={{0,2},{1,3},{2,4},{3,5},{4,6},{5,7},{6,8},{7,9},{8,10},{9,11},{10,... | collective-permute-start | bytes 196616 | tf_op jit(solution)/shard_map/ppermute | solution.py:41

commit v4 on v2

--- a/solution.py
+++ b/solution.py
@@ -208,15 +208,6 @@
             out_ref[slot, layer] = new[ROWS0 : 2 * ROWS0]
 
 
-def pick_kernel(index_ref, below_ref, last_ref, rest_ref, out_ref):
-    for slot in range(SLOTS):
-        index = index_ref[slot]
-        value = last_ref[0]
-        for k in range(SLOTS - 2, -1, -1):
-            value = jnp.where(index == k + 1, rest_ref[k], value)
-        out_ref[slot] = jnp.where(index == 0, below_ref[0], value)
-
-
 def vmem():
     return pl.BlockSpec(memory_space=pltpu.VMEM)
 
@@ -266,12 +257,14 @@
     last = forecast_slots(SLOTS - 1, 1, args)
     below = shifted(last, "particle", 1)
     rest = forecast_slots(0, SLOTS - 1, args)
-    return pl.pallas_call(
-        pick_kernel,
-        out_shape=jax.ShapeDtypeStruct(states.shape, f32),
-        in_specs=[smem(), vmem(), vmem(), vmem()],
-        out_specs=vmem(),
-    )(local_index, below, last, rest)
+    picked = []
+    for slot in range(SLOTS):
+        index = local_index[slot]
+        value = last[0]
+        for k in range(SLOTS - 2, -1, -1):
+            value = jnp.where(index == k + 1, rest[k], value)
+        picked.append(jnp.where(index == 0, below[0], value))
+    return jnp.stack(picked)
 
 
 def forecast_slots(first, slots, args):

time: 53.5 us -> 61.5 us (1.15)
  the two profiles are of different devices: /device:TPU:39 before, /device:TPU:222 now
where the time goes in v4:
time: 61.5 us; the launch traced here: 61.1 us
  starting transfers between devices  24.6 us (40%)
  Pallas kernels  11.4 us (19%)
  waiting for transfers between devices  11 us (18%)
  between operations  10.2 us (17%)
  local copies, waits for them, and re-layouts  2.46 us (4%)
  other arithmetic  1.39 us (2%)
    ppermute x7, starting transfers between devices, shifted(): lax.ppermute(value, axis, [(source, source + steps) for source in range(f...  24.6 us
    ppermute x7, waiting for transfers between devices, shifted(): lax.ppermute(value, axis, [(source, source + steps) for source in range(f...  11 us
    pallas_call x2, Pallas kernels, forecast_slots(): pl.pallas_call(functools.partial(second_kernel, slots), out_shape=jax.Sha...  7.22 us
    pallas_call x1, Pallas kernels, per_device(): pl.pallas_call(first_kernel, out_shape=(jax.ShapeDtypeStruct((FIELDS * F0...  4.23 us
  transfers between devices with their start and end apart: 7, of which 3 were waited for; matrix products, arithmetic and copies ran while one was open for 3% of the time, Pallas kernels for 8%

profile of v4, /device:TPU:222, one launch (start us, length us, event | category | flops | bytes accessed | tf_op | source)
XLA Modules:
  0.0 61.1 jit_solution(4647310756257693983)
XLA Ops:
  0.0 1.9 %collective-permute-start = (f32[4,2,16,1024]{3,2,1,0:T(8,128)}, f32[4,2,16,1024]{3,2,1,0:T(8,128)S(1)}, u32[]{:S(2)}, u32[]{:S(2)}) collective-permute-start(f32[4,2,16,1024]{3,2,1,0:T(8,128)} %own_ref.5), channel_id=1, source_target_pairs={{0,1},{1,2},{2,3},{3,4},{4,5},{5,6},{6,7},{7,8},{8,9},{9,10},{10,1... | collective-permute-start | bytes 1572872 | tf_op jit(solution)/shard_map/ppermute | solution.py:41
  1.9 3.6 %collective-permute-start.1 = (f32[4,2,16,1024]{3,2,1,0:T(8,128)}, f32[4,2,16,1024]{3,2,1,0:T(8,128)S(1)}, u32[]{:S(2)}, u32[]{:S(2)}) collective-permute-start(f32[4,2,16,1024]{3,2,1,0:T(8,128)} %own_ref.5), channel_id=1, source_target_pairs={{1,0},{2,1},{3,2},{4,3},{5,4},{6,5},{7,6},{8,7},{9,8},{10,9},{11,1... | collective-permute-start | bytes 1572872 | tf_op jit(solution)/shard_map/ppermute | solution.py:41
  5.6 0.8 %copy.5 = s32[128,1]{1,0:T(8,128)S(1)} copy(s32[128,1]{0,1:T(1,128)} %bitcast.18) | data formatting | bytes 1024 | tf_op jit(solution)/shard_map/reshape.21
  6.3 0.2 reduce-window.8
  6.5 0.1 reduce
  6.6 4.1 %collective-permute-done.lo_ref = f32[4,2,16,1024]{3,2,1,0:T(8,128)S(1)} collective-permute-done((f32[4,2,16,1024]{3,2,1,0:T(8,128)}, f32[4,2,16,1024]{3,2,1,0:T(8,128)S(1)}, u32[]{:S(2)}, u32[]{:S(2)}) %collective-permute-start) | collective-permute-done | bytes 524320 | tf_op jit(solution)/shard_map/ppermute | solution.py:41
  10.7 1.9 %collective-permute-done.1.hi_ref = f32[4,2,16,1024]{3,2,1,0:T(8,128)S(1)} collective-permute-done((f32[4,2,16,1024]{3,2,1,0:T(8,128)}, f32[4,2,16,1024]{3,2,1,0:T(8,128)S(1)}, u32[]{:S(2)}, u32[]{:S(2)}) %collective-permute-start.1) | collective-permute-done | bytes 524320 | tf_op jit(solution)/shard_map/ppermute | solution.py:41
  12.6 0.0 copy-start
  12.6 1.0 %copy-done = f32[4,2,16,1024]{3,2,1,0:T(8,128)S(1)} copy-done((f32[4,2,16,1024]{3,2,1,0:T(8,128)S(1)}, f32[4,2,16,1024]{3,2,1,0:T(8,128)}, u32[]{:S(2)}) %copy-start) | copy-done | bytes 524312
  13.6 4.2 %shard_map.28 = (f32[384,1024]{1,0:T(8,128)S(1)}, f32[192,512]{1,0:T(8,128)S(1)}, f32[192,512]{1,0:T(8,128)S(1)}, f32[64,256]{1,0:T(8,128)S(1)}) custom-call(s32[1]{0:T(128)} %bitcast.2.band_ref, f32[4,2,16,1024]{3,2,1,0:T(8,128)S(1)} %collective-permute-done.lo_ref, f32[4,2,16,1024]{3,2,1,0:T(8,128)S(1)} %copy-done, ...), custom_call_target="tpu_custom_call" | custom-call | tf_op jit(solution)/shard_map/pallas_call | solution.py:236
  17.8 5.9 %collective-permute-start.2 = (f32[64,256]{1,0:T(8,128)S(1)}, f32[64,256]{1,0:T(8,128)S(1)}, u32[]{:S(2)}, u32[]{:S(2)}) collective-permute-start(f32[64,256]{1,0:T(8,128)S(1)} %get-tuple-element.12.t0_ref), channel_id=1, source_target_pairs={{0,2},{1,3},{2,4},{3,5},{4,6},{5,7},{6,8},{7,9},{8,10},{9,11},{10,... | collective-permute-start | bytes 196616 | tf_op jit(solution)/shard_map/ppermute | solution.py:41
  23.8 2.1 %collective-permute-start.3 = (f32[64,256]{1,0:T(8,128)S(1)}, f32[64,256]{1,0:T(8,128)S(1)}, u32[]{:S(2)}, u32[]{:S(2)}) collective-permute-start(f32[64,256]{1,0:T(8,128)S(1)} %get-tuple-element.12.t0_ref), channel_id=1, source_target_pairs={{0,1},{1,2},{2,3},{3,4},{4,5},{5,6},{6,7},{7,8},{8,9},{9,10},{10,1... | collective-permute-start | bytes 196616 | tf_op jit(solution)/shard_map/ppermute | solution.py:41
  25.9 3.5 %collective-permute-start.4 = (f32[64,256]{1,0:T(8,128)S(1)}, f32[64,256]{1,0:T(8,128)S(1)}, u32[]{:S(2)}, u32[]{:S(2)}) collective-permute-start(f32[64,256]{1,0:T(8,128)S(1)} %get-tuple-element.12.t0_ref), channel_id=1, source_target_pairs={{1,0},{2,1},{3,2},{4,3},{5,4},{6,5},{7,6},{8,7},{9,8},{10,9},{11,1... | collective-permute-start | bytes 196616 | tf_op jit(solution)/shard_map/ppermute | solution.py:41
  29.3 2.1 %collective-permute-start.5 = (f32[64,256]{1,0:T(8,128)S(1)}, f32[64,256]{1,0:T(8,128)S(1)}, u32[]{:S(2)}, u32[]{:S(2)}) collective-permute-start(f32[64,256]{1,0:T(8,128)S(1)} %get-tuple-element.12.t0_ref), channel_id=1, source_target_pairs={{2,0},{3,1},{4,2},{5,3},{6,4},{7,5},{8,6},{9,7},{10,8},{11,9},{12,... | collective-permute-start | bytes 196616 | tf_op jit(solution)/shard_map/ppermute | solution.py:41
  31.4 0.2 convert_reduce_fusion
  31.6 0.0 collective-permute-done.2.tm2_ref
  31.6 0.0 collective-permute-done.3.tm1_ref
  31.6 0.0 collective-permute-done.4.tp1_ref
  31.6 5.1 %collective-permute-done.5.tp2_ref = f32[64,256]{1,0:T(8,128)S(1)} collective-permute-done((f32[64,256]{1,0:T(8,128)S(1)}, f32[64,256]{1,0:T(8,128)S(1)}, u32[]{:S(2)}, u32[]{:S(2)}) %collective-permute-start.5) | collective-permute-done | bytes 65568 | tf_op jit(solution)/shard_map/ppermute | solution.py:41
  36.7 2.3 %shard_map.29 = f32[1,2,16,1024]{3,2,1,0:T(8,128)S(1)} custom-call(s32[1]{0:T(128)} %bitcast.2.band_ref, f32[4,2,16,1024]{3,2,1,0:T(8,128)S(1)} %collective-permute-done.lo_ref, f32[4,2,16,1024]{3,2,1,0:T(8,128)S(1)} %copy-done, f32[4,2,16,1024]{3,2,1,0:T(8,128)S(1)} %collective-permute-done.1.hi_ref, f32[384,1024]{1,0:T(8,128)S(1)} %get-tuple-element.9.f1_ref, ...), custom_call_target="tpu_custom_call" | custom-call | flops 15728640 | bytes 1572864 | tf_op jit(solution)/shard_map/pallas_call | solution.py:283
  39.0 5.5 %collective-permute-start.6 = (f32[1,2,16,1024]{3,2,1,0:T(8,128)S(1)}, f32[1,2,16,1024]{3,2,1,0:T(8,128)S(1)}, u32[]{:S(2)}, u32[]{:S(2)}) collective-permute-start(f32[1,2,16,1024]{3,2,1,0:T(8,128)S(1)} %shard_map.29), channel_id=1, source_target_pairs={{0,16},{16,32},{32,48},{48,64},{64,80},{80,96},{96,112},{112,128},... | collective-permute-start | bytes 393224 | tf_op jit(solution)/shard_map/ppermute | solution.py:41
  44.5 0.7 %fusion = (s32[1]{0:T(128)}, s32[1]{0:T(128)}, s32[1]{0:T(128)}, s32[1]{0:T(128)}) fusion(s32[4]{0:T(128)S(1)} %broadcast_subtract_fusion), kind=kLoop, calls=%fused_computation.8 | loop fusion | bytes 32 | tf_op jit(solution)/shard_map/slice | solution.py:262
  55.2 5.0 %shard_map.30 = f32[3,2,16,1024]{3,2,1,0:T(8,128)S(1)} custom-call(s32[1]{0:T(128)} %bitcast.2.band_ref, f32[4,2,16,1024]{3,2,1,0:T(8,128)S(1)} %collective-permute-done.lo_ref, f32[4,2,16,1024]{3,2,1,0:T(8,128)S(1)} %copy-done, f32[4,2,16,1024]{3,2,1,0:T(8,128)S(1)} %collective-permute-done.1.hi_ref, f32[384,1024]{1,0:T(8,128)S(1)} %get-tuple-element.9.f1_ref, ...), custom_call_target="tpu_custom_call" | custom-call | flops 47185920 | bytes 4718592 | tf_op jit(solution)/shard_map/pallas_call | solution.py:283
  60.1 0.0 collective-permute-done.6
  60.2 0.8 %pad_maximum_fusion = f32[4,2,16,1024]{3,2,1,0:T(8,128)} fusion(f32[1,2,16,1024]{3,2,1,0:T(8,128)S(1)} %get-tuple-element.14, f32[1,2,16,1024]{3,2,1,0:T(8,128)S(1)} %get-tuple-element.16, f32[1,2,16,1024]{3,2,1,0:T(8,128)S(1)} %get-tuple-element.15, f32[1,2,16,1024]{3,2,1,0:T(8,128)S(1)} %get-tuple-element.13), kind=kLoop, calls=%fused_computation | loop fusion | flops 393216 | bytes 1048576 | tf_op jit(solution)/shard_map/stack | solution.py:267
  (4 shorter events, 0.1 us)
Async XLA Ops:
  0.0 10.7 %collective-permute-start = (f32[4,2,16,1024]{3,2,1,0:T(8,128)}, f32[4,2,16,1024]{3,2,1,0:T(8,128)S(1)}, u32[]{:S(2)}, u32[]{:S(2)}) collective-permute-start(f32[4,2,16,1024]{3,2,1,0:T(8,128)} %own_ref.5), channel_id=1, source_target_pairs={{0,1},{1,2},{2,3},{3,4},{4,5},{5,6},{6,7},{7,8},{8,9},{9,10},{10,1... | collective-permute-start | bytes 1572872 | tf_op jit(solution)/shard_map/ppermute | solution.py:41
  1.9 10.6 %collective-permute-start.1 = (f32[4,2,16,1024]{3,2,1,0:T(8,128)}, f32[4,2,16,1024]{3,2,1,0:T(8,128)S(1)}, u32[]{:S(2)}, u32[]{:S(2)}) collective-permute-start(f32[4,2,16,1024]{3,2,1,0:T(8,128)} %own_ref.5), channel_id=1, source_target_pairs={{1,0},{2,1},{3,2},{4,3},{5,4},{6,5},{7,6},{8,7},{9,8},{10,9},{11,1... | collective-permute-start | bytes 1572872 | tf_op jit(solution)/shard_map/ppermute | solution.py:41
  12.6 1.0 %copy-start = (f32[4,2,16,1024]{3,2,1,0:T(8,128)S(1)}, f32[4,2,16,1024]{3,2,1,0:T(8,128)}, u32[]{:S(2)}) copy-start(f32[4,2,16,1024]{3,2,1,0:T(8,128)} %own_ref.5) | copy-start | bytes 1572868
  17.8 13.8 %collective-permute-start.2 = (f32[64,256]{1,0:T(8,128)S(1)}, f32[64,256]{1,0:T(8,128)S(1)}, u32[]{:S(2)}, u32[]{:S(2)}) collective-permute-start(f32[64,256]{1,0:T(8,128)S(1)} %get-tuple-element.12.t0_ref), channel_id=1, source_target_pairs={{0,2},{1,3},{2,4},{3,5},{4,6},{5,7},{6,8},{7,9},{8,10},{9,11},{10,... | collective-permute-start | bytes 196616 | tf_op jit(solution)/shard_map/ppermute | solution.py:41
  23.8 7.9 %collective-permute-start.3 = (f32[64,256]{1,0:T(8,128)S(1)}, f32[64,256]{1,0:T(8,128)S(1)}, u32[]{:S(2)}, u32[]{:S(2)}) collective-permute-start(f32[64,256]{1,0:T(8,128)S(1)} %get-tuple-element.12.t0_ref), channel_id=1, source_target_pairs={{0,1},{1,2},{2,3},{3,4},{4,5},{5,6},{6,7},{7,8},{8,9},{9,10},{10,1... | collective-permute-start | bytes 196616 | tf_op jit(solution)/shard_map/ppermute | solution.py:41
  25.9 5.8 %collective-permute-start.4 = (f32[64,256]{1,0:T(8,128)S(1)}, f32[64,256]{1,0:T(8,128)S(1)}, u32[]{:S(2)}, u32[]{:S(2)}) collective-permute-start(f32[64,256]{1,0:T(8,128)S(1)} %get-tuple-element.12.t0_ref), channel_id=1, source_target_pairs={{1,0},{2,1},{3,2},{4,3},{5,4},{6,5},{7,6},{8,7},{9,8},{10,9},{11,1... | collective-permute-start | bytes 196616 | tf_op jit(solution)/shard_map/ppermute | solution.py:41
  29.3 7.4 %collective-permute-start.5 = (f32[64,256]{1,0:T(8,128)S(1)}, f32[64,256]{1,0:T(8,128)S(1)}, u32[]{:S(2)}, u32[]{:S(2)}) collective-permute-start(f32[64,256]{1,0:T(8,128)S(1)} %get-tuple-element.12.t0_ref), channel_id=1, source_target_pairs={{2,0},{3,1},{4,2},{5,3},{6,4},{7,5},{8,6},{9,7},{10,8},{11,9},{12,... | collective-permute-start | bytes 196616 | tf_op jit(solution)/shard_map/ppermute | solution.py:41
  39.0 21.2 %collective-permute-start.6 = (f32[1,2,16,1024]{3,2,1,0:T(8,128)S(1)}, f32[1,2,16,1024]{3,2,1,0:T(8,128)S(1)}, u32[]{:S(2)}, u32[]{:S(2)}) collective-permute-start(f32[1,2,16,1024]{3,2,1,0:T(8,128)S(1)} %shard_map.29), channel_id=1, source_target_pairs={{0,16},{16,32},{32,48},{48,64},{64,80},{80,96},{96,112},{112,128},... | collective-permute-start | bytes 393224 | tf_op jit(solution)/shard_map/ppermute | solution.py:41

commit v5 on v2

--- a/solution.py
+++ b/solution.py
@@ -208,17 +208,27 @@
             out_ref[slot, layer] = new[ROWS0 : 2 * ROWS0]
 
 
-def pick_kernel(index_ref, below_ref, last_ref, rest_ref, out_ref):
+def pick_kernel(index_ref, below_ref, last_ref, rest_ref, out_ref, sems):
+    choices = [below_ref.at[0]] + [rest_ref.at[k] for k in range(SLOTS - 1)] + [last_ref.at[0]]
     for slot in range(SLOTS):
         index = index_ref[slot]
-        value = last_ref[0]
-        for k in range(SLOTS - 2, -1, -1):
-            value = jnp.where(index == k + 1, rest_ref[k], value)
-        out_ref[slot] = jnp.where(index == 0, below_ref[0], value)
+        last = len(choices) - 1
+        for k, source in enumerate(choices):
+            hit = index <= 0 if k == 0 else (index >= last if k == last else index == k)
+
+            @pl.when(hit)
+            def _():
+                pltpu.make_async_copy(source, out_ref.at[slot], sems.at[slot]).start()
+    for slot in range(SLOTS):
+        pltpu.make_async_copy(choices[0], out_ref.at[slot], sems.at[slot]).wait()
 
 
 def vmem():
     return pl.BlockSpec(memory_space=pltpu.VMEM)
+
+
+def hbm():
+    return pl.BlockSpec(memory_space=pl.ANY)
 
 
 def smem():
@@ -269,8 +279,9 @@
     return pl.pallas_call(
         pick_kernel,
         out_shape=jax.ShapeDtypeStruct(states.shape, f32),
-        in_specs=[smem(), vmem(), vmem(), vmem()],
-        out_specs=vmem(),
+        in_specs=[smem(), hbm(), hbm(), hbm()],
+        out_specs=hbm(),
+        scratch_shapes=[pltpu.SemaphoreType.DMA((SLOTS,))],
     )(local_index, below, last, rest)
 
 

time: 53.5 us -> 69.1 us (1.29)
  Pallas kernels: 13.5 us -> 29.1 us
    pallas_call x1, Pallas kernels: 2.05 us -> 17.7 us  [per_device(): pl.pallas_call(pick_kernel, out_shape=jax.ShapeDtypeStruct(states.shape,...]
  transfers between devices with their start and end apart: 7 -> 7, of which waited for: 4 -> 4; matrix products, arithmetic and copies ran while one was open for 3% -> 3% of each run, Pallas kernels for 9% -> 7%
where the time goes in v5:
time: 69.1 us; the launch traced here: 68.8 us
  Pallas kernels  29.1 us (42%)
  starting transfers between devices  21.5 us (31%)
  waiting for transfers between devices  13.9 us (20%)
  local copies, waits for them, and re-layouts  3.2 us (5%)
  other arithmetic  1.01 us (1%)
    ppermute x7, starting transfers between devices, shifted(): lax.ppermute(value, axis, [(source, source + steps) for source in range(f...  21.5 us
    pallas_call x1, Pallas kernels, per_device(): pl.pallas_call(pick_kernel, out_shape=jax.ShapeDtypeStruct(states.shape,...  17.7 us
    ppermute x7, waiting for transfers between devices, shifted(): lax.ppermute(value, axis, [(source, source + steps) for source in range(f...  13.9 us
    pallas_call x2, Pallas kernels, forecast_slots(): pl.pallas_call(functools.partial(second_kernel, slots), out_shape=jax.Sha...  7.21 us
    pallas_call x1, Pallas kernels, per_device(): pl.pallas_call(first_kernel, out_shape=(jax.ShapeDtypeStruct((FIELDS * F0...  4.23 us
    unnamed x8, local copies, waits for them, and re-layouts  2.44 us
  transfers between devices with their start and end apart: 7, of which 4 were waited for; matrix products, arithmetic and copies ran while one was open for 3% of the time, Pallas kernels for 7%

profile of v5, /device:TPU:39, one launch (start us, length us, event | category | flops | bytes accessed | tf_op | source)
XLA Modules:
  0.0 68.8 jit_solution(6797974520645553694)
XLA Ops:
  0.0 2.6 %collective-permute-start.1 = (f32[4,2,16,1024]{3,2,1,0:T(8,128)}, f32[4,2,16,1024]{3,2,1,0:T(8,128)S(1)}, u32[]{:S(2)}, u32[]{:S(2)}) collective-permute-start(f32[4,2,16,1024]{3,2,1,0:T(8,128)} %own_ref.5), channel_id=1, source_target_pairs={{1,0},{2,1},{3,2},{4,3},{5,4},{6,5},{7,6},{8,7},{9,8},{10,9},{11,1... | collective-permute-start | bytes 1572872 | tf_op jit(solution)/shard_map/ppermute | solution.py:41
  2.6 3.0 %collective-permute-start = (f32[4,2,16,1024]{3,2,1,0:T(8,128)}, f32[4,2,16,1024]{3,2,1,0:T(8,128)S(1)}, u32[]{:S(2)}, u32[]{:S(2)}) collective-permute-start(f32[4,2,16,1024]{3,2,1,0:T(8,128)} %own_ref.5), channel_id=1, source_target_pairs={{0,1},{1,2},{2,3},{3,4},{4,5},{5,6},{6,7},{7,8},{8,9},{9,10},{10,1... | collective-permute-start | bytes 1572872 | tf_op jit(solution)/shard_map/ppermute | solution.py:41
  5.6 0.8 %copy.5 = s32[128,1]{1,0:T(8,128)S(1)} copy(s32[128,1]{0,1:T(1,128)} %bitcast.2) | data formatting | bytes 1024 | tf_op jit(solution)/shard_map/reshape.21
  6.3 0.2 reduce-window.8
  6.5 0.1 reduce
  6.6 4.4 %collective-permute-done.1.hi_ref = f32[4,2,16,1024]{3,2,1,0:T(8,128)S(1)} collective-permute-done((f32[4,2,16,1024]{3,2,1,0:T(8,128)}, f32[4,2,16,1024]{3,2,1,0:T(8,128)S(1)}, u32[]{:S(2)}, u32[]{:S(2)}) %collective-permute-start.1) | collective-permute-done | bytes 524320 | tf_op jit(solution)/shard_map/ppermute | solution.py:41
  11.0 1.0 %collective-permute-done.lo_ref = f32[4,2,16,1024]{3,2,1,0:T(8,128)S(1)} collective-permute-done((f32[4,2,16,1024]{3,2,1,0:T(8,128)}, f32[4,2,16,1024]{3,2,1,0:T(8,128)S(1)}, u32[]{:S(2)}, u32[]{:S(2)}) %collective-permute-start) | collective-permute-done | bytes 524320 | tf_op jit(solution)/shard_map/ppermute | solution.py:41
  12.0 0.0 copy-start
  12.0 1.0 %copy-done = f32[4,2,16,1024]{3,2,1,0:T(8,128)S(1)} copy-done((f32[4,2,16,1024]{3,2,1,0:T(8,128)S(1)}, f32[4,2,16,1024]{3,2,1,0:T(8,128)}, u32[]{:S(2)}) %copy-start) | copy-done | bytes 524312
  13.0 4.2 %shard_map.28 = (f32[384,1024]{1,0:T(8,128)S(1)}, f32[192,512]{1,0:T(8,128)S(1)}, f32[192,512]{1,0:T(8,128)S(1)}, f32[64,256]{1,0:T(8,128)S(1)}) custom-call(s32[1]{0:T(128)} %bitcast.1.band_ref, f32[4,2,16,1024]{3,2,1,0:T(8,128)S(1)} %collective-permute-done.lo_ref, f32[4,2,16,1024]{3,2,1,0:T(8,128)S(1)} %copy-done, ...), custom_call_target="tpu_custom_call" | custom-call | tf_op jit(solution)/shard_map/pallas_call | solution.py:255
  17.3 3.4 %collective-permute-start.5 = (f32[64,256]{1,0:T(8,128)S(1)}, f32[64,256]{1,0:T(8,128)S(1)}, u32[]{:S(2)}, u32[]{:S(2)}) collective-permute-start(f32[64,256]{1,0:T(8,128)S(1)} %get-tuple-element.12.t0_ref), channel_id=1, source_target_pairs={{2,0},{3,1},{4,2},{5,3},{6,4},{7,5},{8,6},{9,7},{10,8},{11,9},{12,... | collective-permute-start | bytes 196616 | tf_op jit(solution)/shard_map/ppermute | solution.py:41
  20.7 2.9 %collective-permute-start.4 = (f32[64,256]{1,0:T(8,128)S(1)}, f32[64,256]{1,0:T(8,128)S(1)}, u32[]{:S(2)}, u32[]{:S(2)}) collective-permute-start(f32[64,256]{1,0:T(8,128)S(1)} %get-tuple-element.12.t0_ref), channel_id=1, source_target_pairs={{1,0},{2,1},{3,2},{4,3},{5,4},{6,5},{7,6},{8,7},{9,8},{10,9},{11,1... | collective-permute-start | bytes 196616 | tf_op jit(solution)/shard_map/ppermute | solution.py:41
  23.6 3.5 %collective-permute-start.3 = (f32[64,256]{1,0:T(8,128)S(1)}, f32[64,256]{1,0:T(8,128)S(1)}, u32[]{:S(2)}, u32[]{:S(2)}) collective-permute-start(f32[64,256]{1,0:T(8,128)S(1)} %get-tuple-element.12.t0_ref), channel_id=1, source_target_pairs={{0,1},{1,2},{2,3},{3,4},{4,5},{5,6},{6,7},{7,8},{8,9},{9,10},{10,1... | collective-permute-start | bytes 196616 | tf_op jit(solution)/shard_map/ppermute | solution.py:41
  27.2 2.0 %collective-permute-start.2 = (f32[64,256]{1,0:T(8,128)S(1)}, f32[64,256]{1,0:T(8,128)S(1)}, u32[]{:S(2)}, u32[]{:S(2)}) collective-permute-start(f32[64,256]{1,0:T(8,128)S(1)} %get-tuple-element.12.t0_ref), channel_id=1, source_target_pairs={{0,2},{1,3},{2,4},{3,5},{4,6},{5,7},{6,8},{7,9},{8,10},{9,11},{10,... | collective-permute-start | bytes 196616 | tf_op jit(solution)/shard_map/ppermute | solution.py:41
  29.2 0.2 convert_reduce_fusion
  29.4 0.0 collective-permute-done.5.tp2_ref
  29.4 0.0 collective-permute-done.4.tp1_ref
  29.4 0.0 collective-permute-done.3.tm1_ref
  29.4 4.0 %collective-permute-done.2.tm2_ref = f32[64,256]{1,0:T(8,128)S(1)} collective-permute-done((f32[64,256]{1,0:T(8,128)S(1)}, f32[64,256]{1,0:T(8,128)S(1)}, u32[]{:S(2)}, u32[]{:S(2)}) %collective-permute-start.2) | collective-permute-done | bytes 65568 | tf_op jit(solution)/shard_map/ppermute | solution.py:41
  33.4 2.3 %shard_map.29.last_ref = f32[1,2,16,1024]{3,2,1,0:T(8,128)S(1)} custom-call(s32[1]{0:T(128)} %bitcast.1.band_ref, f32[4,2,16,1024]{3,2,1,0:T(8,128)S(1)} %collective-permute-done.lo_ref, f32[4,2,16,1024]{3,2,1,0:T(8,128)S(1)} %copy-done, f32[4,2,16,1024]{3,2,1,0:T(8,128)S(1)} %collective-permute-done.1.hi_ref, f32[384,1024]{1,0:T(8,128)S(1)} %get-tuple-element.9.f1_ref, ...), custom_call_target="tpu_custom_call" | custom-call | flops 15728640 | bytes 1572864 | tf_op jit(solution)/shard_map/pallas_call | solution.py:301
  35.7 0.0 copy-start.2
  35.7 4.0 %collective-permute-start.6 = (f32[1,2,16,1024]{3,2,1,0:T(8,128)S(1)}, f32[1,2,16,1024]{3,2,1,0:T(8,128)S(1)}, u32[]{:S(2)}, u32[]{:S(2)}) collective-permute-start(f32[1,2,16,1024]{3,2,1,0:T(8,128)S(1)} %shard_map.29.last_ref), channel_id=1, source_target_pairs={{0,16},{16,32},{32,48},{48,64},{64,80},{80,96},{96,112},{112,128},... | collective-permute-start | bytes 393224 | tf_op jit(solution)/shard_map/ppermute | solution.py:41
  39.7 0.6 broadcast_subtract_fusion.index_ref
  40.3 5.0 %shard_map.30.rest_ref = f32[3,2,16,1024]{3,2,1,0:T(8,128)S(1)} custom-call(s32[1]{0:T(128)} %bitcast.1.band_ref, f32[4,2,16,1024]{3,2,1,0:T(8,128)S(1)} %collective-permute-done.lo_ref, f32[4,2,16,1024]{3,2,1,0:T(8,128)S(1)} %copy-done, f32[4,2,16,1024]{3,2,1,0:T(8,128)S(1)} %collective-permute-done.1.hi_ref, f32[384,1024]{1,0:T(8,128)S(1)} %get-tuple-element.9.f1_ref, ...), custom_call_target="tpu_custom_call" | custom-call | flops 47185920 | bytes 4718592 | tf_op jit(solution)/shard_map/pallas_call | solution.py:301
  45.2 0.0 copy-done.2
  45.3 0.0 copy-start.1
  45.3 0.7 %copy-done.1 = f32[3,2,16,1024]{3,2,1,0:T(8,128)} copy-done((f32[3,2,16,1024]{3,2,1,0:T(8,128)}, f32[3,2,16,1024]{3,2,1,0:T(8,128)S(1)}, u32[]{:S(2)}) %copy-start.1) | copy-done | bytes 393240
  46.0 4.5 %collective-permute-done.6.below_ref = f32[1,2,16,1024]{3,2,1,0:T(8,128)S(1)} collective-permute-done((f32[1,2,16,1024]{3,2,1,0:T(8,128)S(1)}, f32[1,2,16,1024]{3,2,1,0:T(8,128)S(1)}, u32[]{:S(2)}, u32[]{:S(2)}) %collective-permute-start.6) | collective-permute-done | bytes 131104 | tf_op jit(solution)/shard_map/ppermute | solution.py:41
  50.5 0.0 copy-start.3
  50.5 0.6 copy-done.3
  51.1 17.7 %shard_map.31 = f32[4,2,16,1024]{3,2,1,0:T(8,128)} custom-call(s32[4]{0:T(128)} %broadcast_subtract_fusion.index_ref, f32[1,2,16,1024]{3,2,1,0:T(8,128)} %copy-done.3, f32[1,2,16,1024]{3,2,1,0:T(8,128)} %copy-done.2, f32[3,2,16,1024]{3,2,1,0:T(8,128)} %copy-done.1), custom_call_target="tpu_custom_call" | custom-call | tf_op jit(solution)/shard_map/pallas_call | solution.py:279
  (1 shorter events, 0.0 us)
Async XLA Ops:
  0.0 11.0 %collective-permute-start.1 = (f32[4,2,16,1024]{3,2,1,0:T(8,128)}, f32[4,2,16,1024]{3,2,1,0:T(8,128)S(1)}, u32[]{:S(2)}, u32[]{:S(2)}) collective-permute-start(f32[4,2,16,1024]{3,2,1,0:T(8,128)} %own_ref.5), channel_id=1, source_target_pairs={{1,0},{2,1},{3,2},{4,3},{5,4},{6,5},{7,6},{8,7},{9,8},{10,9},{11,1... | collective-permute-start | bytes 1572872 | tf_op jit(solution)/shard_map/ppermute | solution.py:41
  2.6 9.4 %collective-permute-start = (f32[4,2,16,1024]{3,2,1,0:T(8,128)}, f32[4,2,16,1024]{3,2,1,0:T(8,128)S(1)}, u32[]{:S(2)}, u32[]{:S(2)}) collective-permute-start(f32[4,2,16,1024]{3,2,1,0:T(8,128)} %own_ref.5), channel_id=1, source_target_pairs={{0,1},{1,2},{2,3},{3,4},{4,5},{5,6},{6,7},{7,8},{8,9},{9,10},{10,1... | collective-permute-start | bytes 1572872 | tf_op jit(solution)/shard_map/ppermute | solution.py:41
  12.0 1.0 %copy-start = (f32[4,2,16,1024]{3,2,1,0:T(8,128)S(1)}, f32[4,2,16,1024]{3,2,1,0:T(8,128)}, u32[]{:S(2)}) copy-start(f32[4,2,16,1024]{3,2,1,0:T(8,128)} %own_ref.5) | copy-start | bytes 1572868
  17.3 12.1 %collective-permute-start.5 = (f32[64,256]{1,0:T(8,128)S(1)}, f32[64,256]{1,0:T(8,128)S(1)}, u32[]{:S(2)}, u32[]{:S(2)}) collective-permute-start(f32[64,256]{1,0:T(8,128)S(1)} %get-tuple-element.12.t0_ref), channel_id=1, source_target_pairs={{2,0},{3,1},{4,2},{5,3},{6,4},{7,5},{8,6},{9,7},{10,8},{11,9},{12,... | collective-permute-start | bytes 196616 | tf_op jit(solution)/shard_map/ppermute | solution.py:41
  20.7 8.7 %collective-permute-start.4 = (f32[64,256]{1,0:T(8,128)S(1)}, f32[64,256]{1,0:T(8,128)S(1)}, u32[]{:S(2)}, u32[]{:S(2)}) collective-permute-start(f32[64,256]{1,0:T(8,128)S(1)} %get-tuple-element.12.t0_ref), channel_id=1, source_target_pairs={{1,0},{2,1},{3,2},{4,3},{5,4},{6,5},{7,6},{8,7},{9,8},{10,9},{11,1... | collective-permute-start | bytes 196616 | tf_op jit(solution)/shard_map/ppermute | solution.py:41
  23.6 5.8 %collective-permute-start.3 = (f32[64,256]{1,0:T(8,128)S(1)}, f32[64,256]{1,0:T(8,128)S(1)}, u32[]{:S(2)}, u32[]{:S(2)}) collective-permute-start(f32[64,256]{1,0:T(8,128)S(1)} %get-tuple-element.12.t0_ref), channel_id=1, source_target_pairs={{0,1},{1,2},{2,3},{3,4},{4,5},{5,6},{6,7},{7,8},{8,9},{9,10},{10,1... | collective-permute-start | bytes 196616 | tf_op jit(solution)/shard_map/ppermute | solution.py:41
  27.2 6.3 %collective-permute-start.2 = (f32[64,256]{1,0:T(8,128)S(1)}, f32[64,256]{1,0:T(8,128)S(1)}, u32[]{:S(2)}, u32[]{:S(2)}) collective-permute-start(f32[64,256]{1,0:T(8,128)S(1)} %get-tuple-element.12.t0_ref), channel_id=1, source_target_pairs={{0,2},{1,3},{2,4},{3,5},{4,6},{5,7},{6,8},{7,9},{8,10},{9,11},{10,... | collective-permute-start | bytes 196616 | tf_op jit(solution)/shard_map/ppermute | solution.py:41
  35.7 9.5 %copy-start.2 = (f32[1,2,16,1024]{3,2,1,0:T(8,128)}, f32[1,2,16,1024]{3,2,1,0:T(8,128)S(1)}, u32[]{:S(2)}) copy-start(f32[1,2,16,1024]{3,2,1,0:T(8,128)S(1)} %shard_map.29.last_ref) | copy-start | bytes 393220
  35.7 14.8 %collective-permute-start.6 = (f32[1,2,16,1024]{3,2,1,0:T(8,128)S(1)}, f32[1,2,16,1024]{3,2,1,0:T(8,128)S(1)}, u32[]{:S(2)}, u32[]{:S(2)}) collective-permute-start(f32[1,2,16,1024]{3,2,1,0:T(8,128)S(1)} %shard_map.29.last_ref), channel_id=1, source_target_pairs={{0,16},{16,32},{32,48},{48,64},{64,80},{80,96},{96,112},{112,128},... | collective-permute-start | bytes 393224 | tf_op jit(solution)/shard_map/ppermute | solution.py:41
  45.3 0.8 %copy-start.1 = (f32[3,2,16,1024]{3,2,1,0:T(8,128)}, f32[3,2,16,1024]{3,2,1,0:T(8,128)S(1)}, u32[]{:S(2)}) copy-start(f32[3,2,16,1024]{3,2,1,0:T(8,128)S(1)} %shard_map.30.rest_ref) | copy-start | bytes 1179652
  50.5 0.6 copy-start.3

commit v6 on v2

--- a/solution.py
+++ b/solution.py
@@ -143,11 +143,16 @@
 
 
 def second_kernel(
-    slots, band_ref, lo_ref, own_ref, hi_ref, f1_ref, s1_ref, g1_ref,
-    tm2_ref, tm1_ref, t0_ref, tp1_ref, tp2_ref,
-    out_ref,
-    s2_ref, e2_ref, up1_ref, g4_ref, up0_ref,
-):
+    slots, picks, *refs):
+    if picks:
+        (index_ref, band_ref, lo_ref, own_ref, hi_ref, f1_ref, s1_ref, g1_ref,
+         tm2_ref, tm1_ref, t0_ref, tp1_ref, tp2_ref, last_ref,
+         out_ref, s2_ref, e2_ref, up1_ref, g4_ref, up0_ref, own_out) = refs
+    else:
+        (band_ref, lo_ref, own_ref, hi_ref, f1_ref, s1_ref, g1_ref,
+         tm2_ref, tm1_ref, t0_ref, tp1_ref, tp2_ref,
+         out_ref, s2_ref, e2_ref, up1_ref, g4_ref, up0_ref) = refs
+        own_out = out_ref
     fields = 2 * slots
     band = band_ref[0]
     below = rolled(tm1_ref[...], CHUNK // 2, 0)
@@ -205,16 +210,22 @@
             drag = bottom_friction_coefficient if layer else 0.0
             jacobian = stream_x * vort_y - stream_y * vort_x
             new = pv - time_step * (jacobian + beta_slope * stream_x + drag * laplace)
-            out_ref[slot, layer] = new[ROWS0 : 2 * ROWS0]
-
-
-def pick_kernel(index_ref, below_ref, last_ref, rest_ref, out_ref):
+            own_out[slot, layer] = new[ROWS0 : 2 * ROWS0]
+    if picks:
+        pick_slots(index_ref, own_out, last_ref, out_ref)
+
+
+def pick_slots(index_ref, rest_ref, last_ref, out_ref):
     for slot in range(SLOTS):
         index = index_ref[slot]
         value = last_ref[0]
         for k in range(SLOTS - 2, -1, -1):
             value = jnp.where(index == k + 1, rest_ref[k], value)
-        out_ref[slot] = jnp.where(index == 0, below_ref[0], value)
+        out_ref[slot] = value
+
+
+def fix_kernel(index_ref, below_ref, current_ref, out_ref):
+    out_ref[0] = jnp.where(index_ref[0] <= 0, below_ref[0], current_ref[0])
 
 
 def vmem():
@@ -265,16 +276,19 @@
     args = (band, lo_q, states, hi_q, f1, s1, g1, tm2, tm1, t, tp1, tp2)
     last = forecast_slots(SLOTS - 1, 1, args)
     below = shifted(last, "particle", 1)
-    rest = forecast_slots(0, SLOTS - 1, args)
+    picked = forecast_slots(0, SLOTS - 1, args, (local_index, last))
+    strip = pl.BlockSpec((1, 2, ROWS0, COLS0), lambda i: (0, 0, 0, 0))
     return pl.pallas_call(
-        pick_kernel,
+        fix_kernel,
         out_shape=jax.ShapeDtypeStruct(states.shape, f32),
-        in_specs=[smem(), vmem(), vmem(), vmem()],
-        out_specs=vmem(),
-    )(local_index, below, last, rest)
-
-
-def forecast_slots(first, slots, args):
+        grid=(1,),
+        in_specs=[smem(), strip, strip],
+        out_specs=strip,
+        input_output_aliases={2: 0},
+    )(local_index, below, picked)
+
+
+def forecast_slots(first, slots, args, pick=None):
     fields = 2 * slots
     block = first // slots
 
@@ -286,20 +300,30 @@
                 rows(fields * F0, COLS0), rows(fields * F1, COLS0 // 2), rows(fields * F1, COLS0 // 2)]
     in_specs += [rows(fields * CHUNK, COLS0 // 4)] * 5
     f32 = jnp.float32
+    out_shape = jax.ShapeDtypeStruct((slots, 2, ROWS0, COLS0), f32)
+    out_spec = pl.BlockSpec((slots, 2, ROWS0, COLS0), lambda i: (0, 0, 0, 0))
+    extra_scratch = []
+    if pick is not None:
+        whole = pl.BlockSpec((SLOTS, 2, ROWS0, COLS0), lambda i: (0, 0, 0, 0))
+        in_specs = [smem()] + in_specs + [pl.BlockSpec((1, 2, ROWS0, COLS0), lambda i: (0, 0, 0, 0))]
+        args = (pick[0],) + tuple(args) + (pick[1],)
+        out_shape = jax.ShapeDtypeStruct((SLOTS, 2, ROWS0, COLS0), f32)
+        out_spec = whole
+        extra_scratch = [pltpu.VMEM((slots, 2, ROWS0, COLS0), f32)]
     work = fields * F0 * COLS0 * 160
     return pl.pallas_call(
-        functools.partial(second_kernel, slots),
-        out_shape=jax.ShapeDtypeStruct((slots, 2, ROWS0, COLS0), f32),
+        functools.partial(second_kernel, slots, pick is not None),
+        out_shape=out_shape,
         grid=(1,),
         in_specs=in_specs,
-        out_specs=pl.BlockSpec((slots, 2, ROWS0, COLS0), lambda i: (0, 0, 0, 0)),
+        out_specs=out_spec,
         scratch_shapes=[
             pltpu.VMEM((fields * F2, COLS0 // 4), f32),
             pltpu.VMEM((fields * F2, COLS0 // 4), f32),
             pltpu.VMEM((COLS0 // 256, 2 * fields * F2, 128), f32),
             pltpu.VMEM((fields * F1, COLS0 // 2), f32),
             pltpu.VMEM((COLS0 // 128, fields * F0, 128), f32),
-        ],
+        ] + extra_scratch,
         compiler_params=PARAMS,
         cost_estimate=pl.CostEstimate(flops=work, transcendentals=0, bytes_accessed=fields * F0 * COLS0 * 16),
     )(*args)

time: 53.5 us -> 53.1 us (level)
  Pallas kernels: 13.5 us -> 14.4 us
  local copies, waits for them, and re-layouts: 3.2 us -> 2.45 us
  other arithmetic: 1.01 us -> 0.47 us
    pallas_call x3, Pallas kernels: 9.26 us -> 10.2 us  [the longest x2 8.57 us: forecast_slots(): pl.pallas_call(functools.partial(second_kernel, slots, pick is not None),...]
    unnamed x8 -> x6, local copies, waits for them, and re-layouts: 2.44 us -> 1.69 us
    sub x1, other arithmetic: 0.55 us -> 0.01 us  [per_device(): local_index = ancestor - (group * per_group - 1)]
  transfers between devices with their start and end apart: 7 -> 7, of which waited for: 4 -> 4; matrix products, arithmetic and copies ran while one was open for 3% -> 2% of each run, Pallas kernels for 9% -> 12%
where the time goes in v6:
time: 53.1 us; the launch traced here: 52.8 us
  starting transfers between devices  21.5 us (40%)
  Pallas kernels  14.4 us (27%)
  waiting for transfers between devices  13.8 us (26%)
  local copies, waits for them, and re-layouts  2.45 us (5%)
    ppermute x7, starting transfers between devices, shifted(): lax.ppermute(value, axis, [(source, source + steps) for source in range(f...  21.5 us
    ppermute x7, waiting for transfers between devices, shifted(): lax.ppermute(value, axis, [(source, source + steps) for source in range(f...  13.8 us
    pallas_call x2, Pallas kernels, forecast_slots(): pl.pallas_call(functools.partial(second_kernel, slots, pick is not None),...  8.57 us
    pallas_call x1, Pallas kernels, per_device(): pl.pallas_call(first_kernel, out_shape=(jax.ShapeDtypeStruct((FIELDS * F0...  4.22 us
    unnamed x6, local copies, waits for them, and re-layouts  1.69 us
    pallas_call x1, Pallas kernels, per_device(): pl.pallas_call(fix_kernel, out_shape=jax.ShapeDtypeStruct(states.shape, f...  1.65 us
  transfers between devices with their start and end apart: 7, of which 4 were waited for; matrix products, arithmetic and copies ran while one was open for 2% of the time, Pallas kernels for 12%

profile of v6, /device:TPU:39, one launch (start us, length us, event | category | flops | bytes accessed | tf_op | source)
XLA Modules:
  0.0 52.8 jit_solution(14557357994379435448)
XLA Ops:
  0.0 2.6 %collective-permute-start.1 = (f32[4,2,16,1024]{3,2,1,0:T(8,128)}, f32[4,2,16,1024]{3,2,1,0:T(8,128)S(1)}, u32[]{:S(2)}, u32[]{:S(2)}) collective-permute-start(f32[4,2,16,1024]{3,2,1,0:T(8,128)} %refs_3_.1), channel_id=1, source_target_pairs={{1,0},{2,1},{3,2},{4,3},{5,4},{6,5},{7,6},{8,7},{9,8},{10,9},{11,1... | collective-permute-start | bytes 1572872 | tf_op jit(solution)/shard_map/ppermute | solution.py:41
  2.6 3.0 %collective-permute-start = (f32[4,2,16,1024]{3,2,1,0:T(8,128)}, f32[4,2,16,1024]{3,2,1,0:T(8,128)S(1)}, u32[]{:S(2)}, u32[]{:S(2)}) collective-permute-start(f32[4,2,16,1024]{3,2,1,0:T(8,128)} %refs_3_.1), channel_id=1, source_target_pairs={{0,1},{1,2},{2,3},{3,4},{4,5},{5,6},{6,7},{7,8},{8,9},{9,10},{10,1... | collective-permute-start | bytes 1572872 | tf_op jit(solution)/shard_map/ppermute | solution.py:41
  5.6 0.8 %copy.6 = s32[128,1]{1,0:T(8,128)S(1)} copy(s32[128,1]{0,1:T(1,128)} %bitcast.2) | data formatting | bytes 1024 | tf_op jit(solution)/shard_map/reshape.21
  6.3 0.2 reduce-window.8
  6.5 0.1 reduce
  6.6 4.4 %collective-permute-done.1.hi_ref.refs_3_.refs_4_ = f32[4,2,16,1024]{3,2,1,0:T(8,128)S(1)} collective-permute-done((f32[4,2,16,1024]{3,2,1,0:T(8,128)}, f32[4,2,16,1024]{3,2,1,0:T(8,128)S(1)}, u32[]{:S(2)}, u32[]{:S(2)}) %collective-permute-start.1) | collective-permute-done | bytes 524320 | tf_op jit(solution)/shard_map/ppermute | solution.py:41
  11.0 1.0 %collective-permute-done.lo_ref.refs_1_.refs_2_ = f32[4,2,16,1024]{3,2,1,0:T(8,128)S(1)} collective-permute-done((f32[4,2,16,1024]{3,2,1,0:T(8,128)}, f32[4,2,16,1024]{3,2,1,0:T(8,128)S(1)}, u32[]{:S(2)}, u32[]{:S(2)}) %collective-permute-start) | collective-permute-done | bytes 524320 | tf_op jit(solution)/shard_map/ppermute | solution.py:41
  12.0 0.0 copy-start
  12.0 1.0 %copy-done = f32[4,2,16,1024]{3,2,1,0:T(8,128)S(1)} copy-done((f32[4,2,16,1024]{3,2,1,0:T(8,128)S(1)}, f32[4,2,16,1024]{3,2,1,0:T(8,128)}, u32[]{:S(2)}) %copy-start) | copy-done | bytes 524312
  13.0 4.2 %shard_map.28 = (f32[384,1024]{1,0:T(8,128)S(1)}, f32[192,512]{1,0:T(8,128)S(1)}, f32[192,512]{1,0:T(8,128)S(1)}, f32[64,256]{1,0:T(8,128)S(1)}) custom-call(s32[1]{0:T(128)} %bitcast.1.band_ref.refs_0_.refs_1_, f32[4,2,16,1024]{3,2,1,0:T(8,128)S(1)} %collective-permute-done.lo_ref.refs_1_.refs_2_, f32[4,2,16,1024]{3,2,1,0:T(8,128)S(1)} %copy-done, ...), custom_call_target="tpu_custom_call" | custom-call | tf_op jit(solution)/shard_map/pallas_call | solution.py:256
  17.3 3.4 %collective-permute-start.5 = (f32[64,256]{1,0:T(8,128)S(1)}, f32[64,256]{1,0:T(8,128)S(1)}, u32[]{:S(2)}, u32[]{:S(2)}) collective-permute-start(f32[64,256]{1,0:T(8,128)S(1)} %get-tuple-element.12.refs_9_.refs_10_), channel_id=1, source_target_pairs={{2,0},{3,1},{4,2},{5,3},{6,4},{7,5},{8,6},{9,7},{10,8},{11,9},{12,... | collective-permute-start | bytes 196616 | tf_op jit(solution)/shard_map/ppermute | solution.py:41
  20.7 2.9 %collective-permute-start.4 = (f32[64,256]{1,0:T(8,128)S(1)}, f32[64,256]{1,0:T(8,128)S(1)}, u32[]{:S(2)}, u32[]{:S(2)}) collective-permute-start(f32[64,256]{1,0:T(8,128)S(1)} %get-tuple-element.12.refs_9_.refs_10_), channel_id=1, source_target_pairs={{1,0},{2,1},{3,2},{4,3},{5,4},{6,5},{7,6},{8,7},{9,8},{10,9},{11,1... | collective-permute-start | bytes 196616 | tf_op jit(solution)/shard_map/ppermute | solution.py:41
  23.6 3.5 %collective-permute-start.3 = (f32[64,256]{1,0:T(8,128)S(1)}, f32[64,256]{1,0:T(8,128)S(1)}, u32[]{:S(2)}, u32[]{:S(2)}) collective-permute-start(f32[64,256]{1,0:T(8,128)S(1)} %get-tuple-element.12.refs_9_.refs_10_), channel_id=1, source_target_pairs={{0,1},{1,2},{2,3},{3,4},{4,5},{5,6},{6,7},{7,8},{8,9},{9,10},{10,1... | collective-permute-start | bytes 196616 | tf_op jit(solution)/shard_map/ppermute | solution.py:41
  27.2 2.0 %collective-permute-start.2 = (f32[64,256]{1,0:T(8,128)S(1)}, f32[64,256]{1,0:T(8,128)S(1)}, u32[]{:S(2)}, u32[]{:S(2)}) collective-permute-start(f32[64,256]{1,0:T(8,128)S(1)} %get-tuple-element.12.refs_9_.refs_10_), channel_id=1, source_target_pairs={{0,2},{1,3},{2,4},{3,5},{4,6},{5,7},{6,8},{7,9},{8,10},{9,11},{10,... | collective-permute-start | bytes 196616 | tf_op jit(solution)/shard_map/ppermute | solution.py:41
  29.2 0.2 convert_reduce_fusion
  29.4 0.0 collective-permute-done.5.refs_11_.refs_12_
  29.4 0.0 collective-permute-done.4.refs_10_.refs_11_
  29.4 0.0 collective-permute-done.3.refs_8_.refs_9_
  29.4 4.0 %collective-permute-done.2.refs_7_.refs_8_ = f32[64,256]{1,0:T(8,128)S(1)} collective-permute-done((f32[64,256]{1,0:T(8,128)S(1)}, f32[64,256]{1,0:T(8,128)S(1)}, u32[]{:S(2)}, u32[]{:S(2)}) %collective-permute-start.2) | collective-permute-done | bytes 65568 | tf_op jit(solution)/shard_map/ppermute | solution.py:41
  33.4 2.3 %shard_map.29.refs_13_ = f32[1,2,16,1024]{3,2,1,0:T(8,128)S(1)} custom-call(s32[1]{0:T(128)} %bitcast.1.band_ref.refs_0_.refs_1_, f32[4,2,16,1024]{3,2,1,0:T(8,128)S(1)} %collective-permute-done.lo_ref.refs_1_.refs_2_, f32[4,2,16,1024]{3,2,1,0:T(8,128)S(1)} %copy-done, f32[4,2,16,1024]{3,2,1,0:T(8,128)S(1)} %collective-permute-done.1.hi_ref.refs_3_.refs_4_, ...), custom_call_target="tpu_custom_call" | custom-call | flops 15728640 | bytes 1572864 | tf_op jit(solution)/shard_map/pallas_call | solution.py:314
  35.7 4.0 %collective-permute-start.6 = (f32[1,2,16,1024]{3,2,1,0:T(8,128)S(1)}, f32[1,2,16,1024]{3,2,1,0:T(8,128)S(1)}, u32[]{:S(2)}, u32[]{:S(2)}) collective-permute-start(f32[1,2,16,1024]{3,2,1,0:T(8,128)S(1)} %shard_map.29.refs_13_), channel_id=1, source_target_pairs={{0,16},{16,32},{32,48},{48,64},{64,80},{80,96},{96,112},{112,128},... | collective-permute-start | bytes 393224 | tf_op jit(solution)/shard_map/ppermute | solution.py:41
  39.7 0.0 copy-start.1
  39.7 6.3 %shard_map.30.current_ref = f32[4,2,16,1024]{3,2,1,0:T(8,128)} custom-call(s32[4]{0:T(128)S(1)} %broadcast_subtract_fusion.refs_0_.index_ref, s32[1]{0:T(128)} %bitcast.1.band_ref.refs_0_.refs_1_, f32[4,2,16,1024]{3,2,1,0:T(8,128)S(1)} %collective-permute-done.lo_ref.refs_1_.refs_2_, f32[4,2,16,1024]{3,2,1,0:T(8,128)S(1)} %copy-done, ...), custom_call_target="tpu_custom_call" | custom-call | flops 47185920 | bytes 4718592 | tf_op jit(solution)/shard_map/pallas_call | solution.py:314
  46.0 0.0 copy-done.1
  46.0 4.4 %collective-permute-done.6.below_ref = f32[1,2,16,1024]{3,2,1,0:T(8,128)S(1)} collective-permute-done((f32[1,2,16,1024]{3,2,1,0:T(8,128)S(1)}, f32[1,2,16,1024]{3,2,1,0:T(8,128)S(1)}, u32[]{:S(2)}, u32[]{:S(2)}) %collective-permute-start.6) | collective-permute-done | bytes 131104 | tf_op jit(solution)/shard_map/ppermute | solution.py:41
  50.5 0.0 copy-start.2
  50.5 0.6 %copy-done.2 = f32[1,2,16,1024]{3,2,1,0:T(8,128)} copy-done((f32[1,2,16,1024]{3,2,1,0:T(8,128)}, f32[1,2,16,1024]{3,2,1,0:T(8,128)S(1)}, u32[]{:S(2)}) %copy-start.2) | copy-done | bytes 131096
  51.1 1.6 %shard_map.31 = f32[4,2,16,1024]{3,2,1,0:T(8,128)} custom-call(s32[4]{0:T(128)} %copy-done.1, f32[1,2,16,1024]{3,2,1,0:T(8,128)} %copy-done.2, f32[4,2,16,1024]{3,2,1,0:T(8,128)} %shard_map.30.current_ref), custom_call_target="tpu_custom_call", output_to_operand_aliasing={{}: (2, {})} | custom-call | tf_op jit(solution)/shard_map/pallas_call | solution.py:281
  (2 shorter events, 0.0 us)
Async XLA Ops:
  0.0 11.0 %collective-permute-start.1 = (f32[4,2,16,1024]{3,2,1,0:T(8,128)}, f32[4,2,16,1024]{3,2,1,0:T(8,128)S(1)}, u32[]{:S(2)}, u32[]{:S(2)}) collective-permute-start(f32[4,2,16,1024]{3,2,1,0:T(8,128)} %refs_3_.1), channel_id=1, source_target_pairs={{1,0},{2,1},{3,2},{4,3},{5,4},{6,5},{7,6},{8,7},{9,8},{10,9},{11,1... | collective-permute-start | bytes 1572872 | tf_op jit(solution)/shard_map/ppermute | solution.py:41
  2.6 9.4 %collective-permute-start = (f32[4,2,16,1024]{3,2,1,0:T(8,128)}, f32[4,2,16,1024]{3,2,1,0:T(8,128)S(1)}, u32[]{:S(2)}, u32[]{:S(2)}) collective-permute-start(f32[4,2,16,1024]{3,2,1,0:T(8,128)} %refs_3_.1), channel_id=1, source_target_pairs={{0,1},{1,2},{2,3},{3,4},{4,5},{5,6},{6,7},{7,8},{8,9},{9,10},{10,1... | collective-permute-start | bytes 1572872 | tf_op jit(solution)/shard_map/ppermute | solution.py:41
  12.0 1.0 %copy-start = (f32[4,2,16,1024]{3,2,1,0:T(8,128)S(1)}, f32[4,2,16,1024]{3,2,1,0:T(8,128)}, u32[]{:S(2)}) copy-start(f32[4,2,16,1024]{3,2,1,0:T(8,128)} %refs_3_.1) | copy-start | bytes 1572868
  17.3 12.1 %collective-permute-start.5 = (f32[64,256]{1,0:T(8,128)S(1)}, f32[64,256]{1,0:T(8,128)S(1)}, u32[]{:S(2)}, u32[]{:S(2)}) collective-permute-start(f32[64,256]{1,0:T(8,128)S(1)} %get-tuple-element.12.refs_9_.refs_10_), channel_id=1, source_target_pairs={{2,0},{3,1},{4,2},{5,3},{6,4},{7,5},{8,6},{9,7},{10,8},{11,9},{12,... | collective-permute-start | bytes 196616 | tf_op jit(solution)/shard_map/ppermute | solution.py:41
  20.7 8.7 %collective-permute-start.4 = (f32[64,256]{1,0:T(8,128)S(1)}, f32[64,256]{1,0:T(8,128)S(1)}, u32[]{:S(2)}, u32[]{:S(2)}) collective-permute-start(f32[64,256]{1,0:T(8,128)S(1)} %get-tuple-element.12.refs_9_.refs_10_), channel_id=1, source_target_pairs={{1,0},{2,1},{3,2},{4,3},{5,4},{6,5},{7,6},{8,7},{9,8},{10,9},{11,1... | collective-permute-start | bytes 196616 | tf_op jit(solution)/shard_map/ppermute | solution.py:41
  23.6 5.8 %collective-permute-start.3 = (f32[64,256]{1,0:T(8,128)S(1)}, f32[64,256]{1,0:T(8,128)S(1)}, u32[]{:S(2)}, u32[]{:S(2)}) collective-permute-start(f32[64,256]{1,0:T(8,128)S(1)} %get-tuple-element.12.refs_9_.refs_10_), channel_id=1, source_target_pairs={{0,1},{1,2},{2,3},{3,4},{4,5},{5,6},{6,7},{7,8},{8,9},{9,10},{10,1... | collective-permute-start | bytes 196616 | tf_op jit(solution)/shard_map/ppermute | solution.py:41
  27.2 6.3 %collective-permute-start.2 = (f32[64,256]{1,0:T(8,128)S(1)}, f32[64,256]{1,0:T(8,128)S(1)}, u32[]{:S(2)}, u32[]{:S(2)}) collective-permute-start(f32[64,256]{1,0:T(8,128)S(1)} %get-tuple-element.12.refs_9_.refs_10_), channel_id=1, source_target_pairs={{0,2},{1,3},{2,4},{3,5},{4,6},{5,7},{6,8},{7,9},{8,10},{9,11},{10,... | collective-permute-start | bytes 196616 | tf_op jit(solution)/shard_map/ppermute | solution.py:41
  35.7 14.8 %collective-permute-start.6 = (f32[1,2,16,1024]{3,2,1,0:T(8,128)S(1)}, f32[1,2,16,1024]{3,2,1,0:T(8,128)S(1)}, u32[]{:S(2)}, u32[]{:S(2)}) collective-permute-start(f32[1,2,16,1024]{3,2,1,0:T(8,128)S(1)} %shard_map.29.refs_13_), channel_id=1, source_target_pairs={{0,16},{16,32},{32,48},{48,64},{64,80},{80,96},{96,112},{112,128},... | collective-permute-start | bytes 393224 | tf_op jit(solution)/shard_map/ppermute | solution.py:41
  39.7 6.3 %copy-start.1 = (s32[4]{0:T(128)}, s32[4]{0:T(128)S(1)}, u32[]{:S(2)}) copy-start(s32[4]{0:T(128)S(1)} %broadcast_subtract_fusion.refs_0_.index_ref) | copy-start | bytes 52
  50.5 0.6 %copy-start.2 = (f32[1,2,16,1024]{3,2,1,0:T(8,128)}, f32[1,2,16,1024]{3,2,1,0:T(8,128)S(1)}, u32[]{:S(2)}) copy-start(f32[1,2,16,1024]{3,2,1,0:T(8,128)S(1)} %collective-permute-done.6.below_ref) | copy-start | bytes 393220

commit v7 on v6

--- a/solution.py
+++ b/solution.py
@@ -96,9 +96,28 @@
     return jnp.concatenate([ref[j, rows, :] for j in range(ref.shape[0])], axis=1)
 
 
+HALO = 12
+
+
+def halo_window(ref, piece, below):
+    start = HALO * piece
+    if (piece % 2 == 1) == below:
+        window = ref[pl.ds(start - 4 if below else start, ROWS0), :]
+        return window
+    window = ref[pl.ds(start if below else start - 4, ROWS0), :]
+    return rolled(window, 4 if below else -4, 0)
+
+
 def sources(lo_ref, own_ref, hi_ref, slot):
     q = [
-        jnp.concatenate([lo_ref[slot, layer], own_ref[slot, layer], hi_ref[slot, layer]], axis=0)
+        jnp.concatenate(
+            [
+                halo_window(lo_ref, 2 * slot + layer, True),
+                own_ref[slot, layer],
+                halo_window(hi_ref, 2 * slot + layer, False),
+            ],
+            axis=0,
+        )
         for layer in range(2)
     ]
     return q, [-(0.5 * (q[0] + q[1])), -(0.5 * (q[0] - q[1]))]
@@ -250,8 +269,9 @@
     local_index = ancestor - (group * per_group - 1)
 
     band = lax.axis_index("band").astype(jnp.int32).reshape(1)
-    lo_q = shifted(states, "band", 1)
-    hi_q = shifted(states, "band", -1)
+    pieces = states.shape[0] * states.shape[1] * HALO
+    lo_q = shifted(states[:, :, ROWS0 - HALO :, :].reshape(pieces, COLS0), "band", 1)
+    hi_q = shifted(states[:, :, :HALO, :].reshape(pieces, COLS0), "band", -1)
     f32 = jnp.float32
     f1, s1, g1, t = pl.pallas_call(
         first_kernel,
@@ -296,7 +316,8 @@
         return pl.BlockSpec((count, width), lambda i: (block, 0))
 
     strips = pl.BlockSpec((slots, 2, ROWS0, COLS0), lambda i: (block, 0, 0, 0))
-    in_specs = [smem(), strips, strips, strips,
+    halos = rows(fields * HALO, COLS0)
+    in_specs = [smem(), halos, strips, halos,
                 rows(fields * F0, COLS0), rows(fields * F1, COLS0 // 2), rows(fields * F1, COLS0 // 2)]
     in_specs += [rows(fields * CHUNK, COLS0 // 4)] * 5
     f32 = jnp.float32

time: 53.1 us -> 54.8 us (1.032)
  waiting for transfers between devices: 13.8 us -> 15.4 us
    ppermute x7, waiting for transfers between devices: 13.8 us -> 15.4 us  [shifted(): lax.ppermute(value, axis, [(source, source + steps) for source in range(f...]
    slice x0 -> x1, local copies, waits for them, and re-layouts: none -> 1.35 us  [per_device(): hi_q = shifted(states[:, :, :HALO, :].reshape(pieces, COLS0), 'band', -1)]
    unnamed x6 -> x8, local copies, waits for them, and re-layouts: 1.69 us -> 0.67 us
    another operation x1, local copies, waits for them, and re-layouts: 0.76 us -> 0.11 us
  transfers between devices with their start and end apart: 7 -> 7, of which waited for: 4 -> 4; matrix products, arithmetic and copies ran while one was open for 2% -> 1% of each run, Pallas kernels for 12% -> 12%
where the time goes in v7:
time: 54.8 us; the launch traced here: 54.5 us
  starting transfers between devices  21.8 us (40%)
  waiting for transfers between devices  15.4 us (28%)
  Pallas kernels  14.5 us (26%)
  local copies, waits for them, and re-layouts  2.22 us (4%)
    ppermute x7, starting transfers between devices, shifted(): lax.ppermute(value, axis, [(source, source + steps) for source in range(f...  21.8 us
    ppermute x7, waiting for transfers between devices, shifted(): lax.ppermute(value, axis, [(source, source + steps) for source in range(f...  15.4 us
    pallas_call x2, Pallas kernels, forecast_slots(): pl.pallas_call(functools.partial(second_kernel, slots, pick is not None),...  8.56 us
    pallas_call x1, Pallas kernels, per_device(): pl.pallas_call(first_kernel, out_shape=(jax.ShapeDtypeStruct((FIELDS * F0...  4.26 us
    pallas_call x1, Pallas kernels, per_device(): pl.pallas_call(fix_kernel, out_shape=jax.ShapeDtypeStruct(states.shape, f...  1.65 us
    slice x1, local copies, waits for them, and re-layouts, per_device(): hi_q = shifted(states[:, :, :HALO, :].reshape(pieces, COLS0), 'band', -1)  1.35 us
  transfers between devices with their start and end apart: 7, of which 4 were waited for; matrix products, arithmetic and copies ran while one was open for 1% of the time, Pallas kernels for 12%

profile of v7, /device:TPU:39, one launch (start us, length us, event | category | flops | bytes accessed | tf_op | source)
XLA Modules:
  0.0 54.5 jit_solution(10585061415554008908)
XLA Ops:
  0.0 0.0 copy-start.3
  0.0 1.4 %fusion = (f32[4,2,12,1024]{3,2,1,0:T(8,128)S(1)}, f32[4,2,12,1024]{3,2,1,0:T(8,128)S(1)}) fusion(f32[4,2,16,1024]{3,2,1,0:T(8,128)} %refs_3_.1), kind=kLoop, calls=%fused_computation.3 | loop fusion | bytes 1572864 | tf_op jit(solution)/shard_map/slice | solution.py:274
  1.4 0.0 copy-start
  1.4 3.0 %collective-permute-start = (f32[96,1024]{1,0:T(8,128)S(1)}, f32[96,1024]{1,0:T(8,128)S(1)}, u32[]{:S(2)}, u32[]{:S(2)}) collective-permute-start(f32[96,1024]{1,0:T(8,128)S(1)} %reshape.40), channel_id=1, source_target_pairs={{0,1},{1,2},{2,3},{3,4},{4,5},{5,6},{6,7},{7,8},{8,9},{9,10},{10,1... | collective-permute-start | bytes 1179656 | tf_op jit(solution)/shard_map/ppermute | solution.py:41
  4.5 1.9 %collective-permute-start.1 = (f32[96,1024]{1,0:T(8,128)S(1)}, f32[96,1024]{1,0:T(8,128)S(1)}, u32[]{:S(2)}, u32[]{:S(2)}) collective-permute-start(f32[96,1024]{1,0:T(8,128)S(1)} %reshape.41), channel_id=1, source_target_pairs={{1,0},{2,1},{3,2},{4,3},{5,4},{6,5},{7,6},{8,7},{9,8},{10,9},{11,1... | collective-permute-start | bytes 1179656 | tf_op jit(solution)/shard_map/ppermute | solution.py:41
  6.4 0.0 copy-done.3
  6.4 0.1 copy.6
  6.5 0.2 reduce-window.8
  6.7 0.1 reduce
  6.8 2.3 %collective-permute-done.lo_ref.refs_1_.refs_2_ = f32[96,1024]{1,0:T(8,128)S(1)} collective-permute-done((f32[96,1024]{1,0:T(8,128)S(1)}, f32[96,1024]{1,0:T(8,128)S(1)}, u32[]{:S(2)}, u32[]{:S(2)}) %collective-permute-start) | collective-permute-done | bytes 393248 | tf_op jit(solution)/shard_map/ppermute | solution.py:41
  9.1 4.5 %collective-permute-done.1.hi_ref.refs_3_.refs_4_ = f32[96,1024]{1,0:T(8,128)S(1)} collective-permute-done((f32[96,1024]{1,0:T(8,128)S(1)}, f32[96,1024]{1,0:T(8,128)S(1)}, u32[]{:S(2)}, u32[]{:S(2)}) %collective-permute-start.1) | collective-permute-done | bytes 393248 | tf_op jit(solution)/shard_map/ppermute | solution.py:41
  13.6 0.0 copy-done
  13.6 4.3 %shard_map.28 = (f32[384,1024]{1,0:T(8,128)S(1)}, f32[192,512]{1,0:T(8,128)S(1)}, f32[192,512]{1,0:T(8,128)S(1)}, f32[64,256]{1,0:T(8,128)S(1)}) custom-call(s32[1]{0:T(128)} %bitcast.1.band_ref.refs_0_.refs_1_, f32[96,1024]{1,0:T(8,128)S(1)} %collective-permute-done.lo_ref.refs_1_.refs_2_, f32[4,2,16,1024]{3,2,1,0:T(8,128)S(1)} %copy-done, ...), custom_call_target="tpu_custom_call" | custom-call | tf_op jit(solution)/shard_map/pallas_call | solution.py:276
  17.9 5.4 %collective-permute-start.5 = (f32[64,256]{1,0:T(8,128)S(1)}, f32[64,256]{1,0:T(8,128)S(1)}, u32[]{:S(2)}, u32[]{:S(2)}) collective-permute-start(f32[64,256]{1,0:T(8,128)S(1)} %get-tuple-element.12.refs_9_.refs_10_), channel_id=1, source_target_pairs={{2,0},{3,1},{4,2},{5,3},{6,4},{7,5},{8,6},{9,7},{10,8},{11,9},{12,... | collective-permute-start | bytes 196616 | tf_op jit(solution)/shard_map/ppermute | solution.py:41
  23.3 1.9 %collective-permute-start.4 = (f32[64,256]{1,0:T(8,128)S(1)}, f32[64,256]{1,0:T(8,128)S(1)}, u32[]{:S(2)}, u32[]{:S(2)}) collective-permute-start(f32[64,256]{1,0:T(8,128)S(1)} %get-tuple-element.12.refs_9_.refs_10_), channel_id=1, source_target_pairs={{1,0},{2,1},{3,2},{4,3},{5,4},{6,5},{7,6},{8,7},{9,8},{10,9},{11,1... | collective-permute-start | bytes 196616 | tf_op jit(solution)/shard_map/ppermute | solution.py:41
  25.2 3.6 %collective-permute-start.3 = (f32[64,256]{1,0:T(8,128)S(1)}, f32[64,256]{1,0:T(8,128)S(1)}, u32[]{:S(2)}, u32[]{:S(2)}) collective-permute-start(f32[64,256]{1,0:T(8,128)S(1)} %get-tuple-element.12.refs_9_.refs_10_), channel_id=1, source_target_pairs={{0,1},{1,2},{2,3},{3,4},{4,5},{5,6},{6,7},{7,8},{8,9},{9,10},{10,1... | collective-permute-start | bytes 196616 | tf_op jit(solution)/shard_map/ppermute | solution.py:41
  28.8 1.9 %collective-permute-start.2 = (f32[64,256]{1,0:T(8,128)S(1)}, f32[64,256]{1,0:T(8,128)S(1)}, u32[]{:S(2)}, u32[]{:S(2)}) collective-permute-start(f32[64,256]{1,0:T(8,128)S(1)} %get-tuple-element.12.refs_9_.refs_10_), channel_id=1, source_target_pairs={{0,2},{1,3},{2,4},{3,5},{4,6},{5,7},{6,8},{7,9},{8,10},{9,11},{10,... | collective-permute-start | bytes 196616 | tf_op jit(solution)/shard_map/ppermute | solution.py:41
  30.8 0.2 convert_reduce_fusion
  31.0 0.0 collective-permute-done.5.refs_11_.refs_12_
  31.0 0.0 collective-permute-done.4.refs_10_.refs_11_
  31.0 0.0 collective-permute-done.3.refs_8_.refs_9_
  31.0 4.1 %collective-permute-done.2.refs_7_.refs_8_ = f32[64,256]{1,0:T(8,128)S(1)} collective-permute-done((f32[64,256]{1,0:T(8,128)S(1)}, f32[64,256]{1,0:T(8,128)S(1)}, u32[]{:S(2)}, u32[]{:S(2)}) %collective-permute-start.2) | collective-permute-done | bytes 65568 | tf_op jit(solution)/shard_map/ppermute | solution.py:41
  35.1 2.2 %shard_map.29.refs_13_ = f32[1,2,16,1024]{3,2,1,0:T(8,128)S(1)} custom-call(s32[1]{0:T(128)} %bitcast.1.band_ref.refs_0_.refs_1_, f32[96,1024]{1,0:T(8,128)S(1)} %collective-permute-done.lo_ref.refs_1_.refs_2_, f32[4,2,16,1024]{3,2,1,0:T(8,128)S(1)} %copy-done, f32[96,1024]{1,0:T(8,128)S(1)} %collective-permute-done.1.hi_ref.refs_3_.refs_4_, ...), custom_call_target="tpu_custom_call" | custom-call | flops 15728640 | bytes 1572864 | tf_op jit(solution)/shard_map/pallas_call | solution.py:335
  37.3 4.0 %collective-permute-start.6 = (f32[1,2,16,1024]{3,2,1,0:T(8,128)S(1)}, f32[1,2,16,1024]{3,2,1,0:T(8,128)S(1)}, u32[]{:S(2)}, u32[]{:S(2)}) collective-permute-start(f32[1,2,16,1024]{3,2,1,0:T(8,128)S(1)} %shard_map.29.refs_13_), channel_id=1, source_target_pairs={{0,16},{16,32},{32,48},{48,64},{64,80},{80,96},{96,112},{112,128},... | collective-permute-start | bytes 393224 | tf_op jit(solution)/shard_map/ppermute | solution.py:41
  41.3 0.0 copy-start.1
  41.3 6.3 %shard_map.30.current_ref = f32[4,2,16,1024]{3,2,1,0:T(8,128)} custom-call(s32[4]{0:T(128)S(1)} %broadcast_subtract_fusion.refs_0_.index_ref, s32[1]{0:T(128)} %bitcast.1.band_ref.refs_0_.refs_1_, f32[96,1024]{1,0:T(8,128)S(1)} %collective-permute-done.lo_ref.refs_1_.refs_2_, f32[4,2,16,1024]{3,2,1,0:T(8,128)S(1)} %copy-done, ...), custom_call_target="tpu_custom_call" | custom-call | flops 47185920 | bytes 4718592 | tf_op jit(solution)/shard_map/pallas_call | solution.py:335
  47.7 0.0 copy-done.1
  47.7 4.5 %collective-permute-done.6.below_ref = f32[1,2,16,1024]{3,2,1,0:T(8,128)S(1)} collective-permute-done((f32[1,2,16,1024]{3,2,1,0:T(8,128)S(1)}, f32[1,2,16,1024]{3,2,1,0:T(8,128)S(1)}, u32[]{:S(2)}, u32[]{:S(2)}) %collective-permute-start.6) | collective-permute-done | bytes 131104 | tf_op jit(solution)/shard_map/ppermute | solution.py:41
  52.2 0.0 copy-start.2
  52.2 0.7 %copy-done.2 = f32[1,2,16,1024]{3,2,1,0:T(8,128)} copy-done((f32[1,2,16,1024]{3,2,1,0:T(8,128)}, f32[1,2,16,1024]{3,2,1,0:T(8,128)S(1)}, u32[]{:S(2)}) %copy-start.2) | copy-done | bytes 131096
  52.8 1.6 %shard_map.31 = f32[4,2,16,1024]{3,2,1,0:T(8,128)} custom-call(s32[4]{0:T(128)} %copy-done.1, f32[1,2,16,1024]{3,2,1,0:T(8,128)} %copy-done.2, f32[4,2,16,1024]{3,2,1,0:T(8,128)} %shard_map.30.current_ref), custom_call_target="tpu_custom_call", output_to_operand_aliasing={{}: (2, {})} | custom-call | tf_op jit(solution)/shard_map/pallas_call | solution.py:301
  (4 shorter events, 0.1 us)
Async XLA Ops:
  0.0 6.4 %copy-start.3 = (s32[128]{0:T(128)S(1)}, s32[128]{0:T(128)}, u32[]{:S(2)}) copy-start(s32[128]{0:T(128)} %param.3) | copy-start | bytes 1540
  1.4 12.2 %copy-start = (f32[4,2,16,1024]{3,2,1,0:T(8,128)S(1)}, f32[4,2,16,1024]{3,2,1,0:T(8,128)}, u32[]{:S(2)}) copy-start(f32[4,2,16,1024]{3,2,1,0:T(8,128)} %refs_3_.1) | copy-start | bytes 1572868
  1.4 7.7 %collective-permute-start = (f32[96,1024]{1,0:T(8,128)S(1)}, f32[96,1024]{1,0:T(8,128)S(1)}, u32[]{:S(2)}, u32[]{:S(2)}) collective-permute-start(f32[96,1024]{1,0:T(8,128)S(1)} %reshape.40), channel_id=1, source_target_pairs={{0,1},{1,2},{2,3},{3,4},{4,5},{5,6},{6,7},{7,8},{8,9},{9,10},{10,1... | collective-permute-start | bytes 1179656 | tf_op jit(solution)/shard_map/ppermute | solution.py:41
  4.5 9.1 %collective-permute-start.1 = (f32[96,1024]{1,0:T(8,128)S(1)}, f32[96,1024]{1,0:T(8,128)S(1)}, u32[]{:S(2)}, u32[]{:S(2)}) collective-permute-start(f32[96,1024]{1,0:T(8,128)S(1)} %reshape.41), channel_id=1, source_target_pairs={{1,0},{2,1},{3,2},{4,3},{5,4},{6,5},{7,6},{8,7},{9,8},{10,9},{11,1... | collective-permute-start | bytes 1179656 | tf_op jit(solution)/shard_map/ppermute | solution.py:41
  17.9 13.1 %collective-permute-start.5 = (f32[64,256]{1,0:T(8,128)S(1)}, f32[64,256]{1,0:T(8,128)S(1)}, u32[]{:S(2)}, u32[]{:S(2)}) collective-permute-start(f32[64,256]{1,0:T(8,128)S(1)} %get-tuple-element.12.refs_9_.refs_10_), channel_id=1, source_target_pairs={{2,0},{3,1},{4,2},{5,3},{6,4},{7,5},{8,6},{9,7},{10,8},{11,9},{12,... | collective-permute-start | bytes 196616 | tf_op jit(solution)/shard_map/ppermute | solution.py:41
  23.3 7.7 %collective-permute-start.4 = (f32[64,256]{1,0:T(8,128)S(1)}, f32[64,256]{1,0:T(8,128)S(1)}, u32[]{:S(2)}, u32[]{:S(2)}) collective-permute-start(f32[64,256]{1,0:T(8,128)S(1)} %get-tuple-element.12.refs_9_.refs_10_), channel_id=1, source_target_pairs={{1,0},{2,1},{3,2},{4,3},{5,4},{6,5},{7,6},{8,7},{9,8},{10,9},{11,1... | collective-permute-start | bytes 196616 | tf_op jit(solution)/shard_map/ppermute | solution.py:41
  25.2 5.8 %collective-permute-start.3 = (f32[64,256]{1,0:T(8,128)S(1)}, f32[64,256]{1,0:T(8,128)S(1)}, u32[]{:S(2)}, u32[]{:S(2)}) collective-permute-start(f32[64,256]{1,0:T(8,128)S(1)} %get-tuple-element.12.refs_9_.refs_10_), channel_id=1, source_target_pairs={{0,1},{1,2},{2,3},{3,4},{4,5},{5,6},{6,7},{7,8},{8,9},{9,10},{10,1... | collective-permute-start | bytes 196616 | tf_op jit(solution)/shard_map/ppermute | solution.py:41
  28.8 6.2 %collective-permute-start.2 = (f32[64,256]{1,0:T(8,128)S(1)}, f32[64,256]{1,0:T(8,128)S(1)}, u32[]{:S(2)}, u32[]{:S(2)}) collective-permute-start(f32[64,256]{1,0:T(8,128)S(1)} %get-tuple-element.12.refs_9_.refs_10_), channel_id=1, source_target_pairs={{0,2},{1,3},{2,4},{3,5},{4,6},{5,7},{6,8},{7,9},{8,10},{9,11},{10,... | collective-permute-start | bytes 196616 | tf_op jit(solution)/shard_map/ppermute | solution.py:41
  37.3 14.9 %collective-permute-start.6 = (f32[1,2,16,1024]{3,2,1,0:T(8,128)S(1)}, f32[1,2,16,1024]{3,2,1,0:T(8,128)S(1)}, u32[]{:S(2)}, u32[]{:S(2)}) collective-permute-start(f32[1,2,16,1024]{3,2,1,0:T(8,128)S(1)} %shard_map.29.refs_13_), channel_id=1, source_target_pairs={{0,16},{16,32},{32,48},{48,64},{64,80},{80,96},{96,112},{112,128},... | collective-permute-start | bytes 393224 | tf_op jit(solution)/shard_map/ppermute | solution.py:41
  41.3 6.3 %copy-start.1 = (s32[4]{0:T(128)}, s32[4]{0:T(128)S(1)}, u32[]{:S(2)}) copy-start(s32[4]{0:T(128)S(1)} %broadcast_subtract_fusion.refs_0_.index_ref) | copy-start | bytes 52
  52.2 0.7 %copy-start.2 = (f32[1,2,16,1024]{3,2,1,0:T(8,128)}, f32[1,2,16,1024]{3,2,1,0:T(8,128)S(1)}, u32[]{:S(2)}) copy-start(f32[1,2,16,1024]{3,2,1,0:T(8,128)S(1)} %collective-permute-done.6.below_ref) | copy-start | bytes 393220

commit v8 on v6

--- a/solution.py
+++ b/solution.py
@@ -224,8 +224,14 @@
         out_ref[slot] = value
 
 
-def fix_kernel(index_ref, below_ref, current_ref, out_ref):
-    out_ref[0] = jnp.where(index_ref[0] <= 0, below_ref[0], current_ref[0])
+def fix_kernel(index_ref, below_ref, current_ref, out_ref, sem):
+    del current_ref
+
+    @pl.when(index_ref[0] <= 0)
+    def _():
+        copy = pltpu.make_async_copy(below_ref.at[0], out_ref.at[0], sem)
+        copy.start()
+        copy.wait()
 
 
 def vmem():
@@ -277,13 +283,13 @@
     last = forecast_slots(SLOTS - 1, 1, args)
     below = shifted(last, "particle", 1)
     picked = forecast_slots(0, SLOTS - 1, args, (local_index, last))
-    strip = pl.BlockSpec((1, 2, ROWS0, COLS0), lambda i: (0, 0, 0, 0))
+    anywhere = pl.BlockSpec(memory_space=pl.ANY)
     return pl.pallas_call(
         fix_kernel,
         out_shape=jax.ShapeDtypeStruct(states.shape, f32),
-        grid=(1,),
-        in_specs=[smem(), strip, strip],
-        out_specs=strip,
+        in_specs=[smem(), vmem(), anywhere],
+        out_specs=anywhere,
+        scratch_shapes=[pltpu.SemaphoreType.DMA(())],
         input_output_aliases={2: 0},
     )(local_index, below, picked)
 

time: 53.1 us -> 53 us (level)
  no operation moved by 1% of the time
where the time goes in v8:
time: 53 us; the launch traced here: 52.7 us
  starting transfers between devices  21.5 us (41%)
  Pallas kernels  14.4 us (27%)
  waiting for transfers between devices  13.8 us (26%)
  local copies, waits for them, and re-layouts  2.45 us (5%)
    ppermute x7, starting transfers between devices, shifted(): lax.ppermute(value, axis, [(source, source + steps) for source in range(f...  21.5 us
    ppermute x7, waiting for transfers between devices, shifted(): lax.ppermute(value, axis, [(source, source + steps) for source in range(f...  13.8 us
    pallas_call x2, Pallas kernels, forecast_slots(): pl.pallas_call(functools.partial(second_kernel, slots, pick is not None),...  8.57 us
    pallas_call x1, Pallas kernels, per_device(): pl.pallas_call(first_kernel, out_shape=(jax.ShapeDtypeStruct((FIELDS * F0...  4.22 us
    unnamed x6, local copies, waits for them, and re-layouts  1.69 us
    pallas_call x1, Pallas kernels, per_device(): pl.pallas_call(fix_kernel, out_shape=jax.ShapeDtypeStruct(states.shape, f...  1.58 us
  transfers between devices with their start and end apart: 7, of which 4 were waited for; matrix products, arithmetic and copies ran while one was open for 2% of the time, Pallas kernels for 12%

profile of v8, /device:TPU:39, one launch (start us, length us, event | category | flops | bytes accessed | tf_op | source)
XLA Modules:
  0.0 52.7 jit_solution(16944249603744803515)
XLA Ops:
  0.0 2.6 %collective-permute-start.1 = (f32[4,2,16,1024]{3,2,1,0:T(8,128)}, f32[4,2,16,1024]{3,2,1,0:T(8,128)S(1)}, u32[]{:S(2)}, u32[]{:S(2)}) collective-permute-start(f32[4,2,16,1024]{3,2,1,0:T(8,128)} %refs_3_.1), channel_id=1, source_target_pairs={{1,0},{2,1},{3,2},{4,3},{5,4},{6,5},{7,6},{8,7},{9,8},{10,9},{11,1... | collective-permute-start | bytes 1572872 | tf_op jit(solution)/shard_map/ppermute | solution.py:41
  2.6 3.0 %collective-permute-start = (f32[4,2,16,1024]{3,2,1,0:T(8,128)}, f32[4,2,16,1024]{3,2,1,0:T(8,128)S(1)}, u32[]{:S(2)}, u32[]{:S(2)}) collective-permute-start(f32[4,2,16,1024]{3,2,1,0:T(8,128)} %refs_3_.1), channel_id=1, source_target_pairs={{0,1},{1,2},{2,3},{3,4},{4,5},{5,6},{6,7},{7,8},{8,9},{9,10},{10,1... | collective-permute-start | bytes 1572872 | tf_op jit(solution)/shard_map/ppermute | solution.py:41
  5.6 0.8 %copy.6 = s32[128,1]{1,0:T(8,128)S(1)} copy(s32[128,1]{0,1:T(1,128)} %bitcast.2) | data formatting | bytes 1024 | tf_op jit(solution)/shard_map/reshape.21
  6.3 0.2 reduce-window.8
  6.5 0.1 reduce
  6.6 4.4 %collective-permute-done.1.hi_ref.refs_3_.refs_4_ = f32[4,2,16,1024]{3,2,1,0:T(8,128)S(1)} collective-permute-done((f32[4,2,16,1024]{3,2,1,0:T(8,128)}, f32[4,2,16,1024]{3,2,1,0:T(8,128)S(1)}, u32[]{:S(2)}, u32[]{:S(2)}) %collective-permute-start.1) | collective-permute-done | bytes 524320 | tf_op jit(solution)/shard_map/ppermute | solution.py:41
  11.0 1.0 %collective-permute-done.lo_ref.refs_1_.refs_2_ = f32[4,2,16,1024]{3,2,1,0:T(8,128)S(1)} collective-permute-done((f32[4,2,16,1024]{3,2,1,0:T(8,128)}, f32[4,2,16,1024]{3,2,1,0:T(8,128)S(1)}, u32[]{:S(2)}, u32[]{:S(2)}) %collective-permute-start) | collective-permute-done | bytes 524320 | tf_op jit(solution)/shard_map/ppermute | solution.py:41
  12.0 0.0 copy-start
  12.0 1.0 %copy-done = f32[4,2,16,1024]{3,2,1,0:T(8,128)S(1)} copy-done((f32[4,2,16,1024]{3,2,1,0:T(8,128)S(1)}, f32[4,2,16,1024]{3,2,1,0:T(8,128)}, u32[]{:S(2)}) %copy-start) | copy-done | bytes 524312
  13.0 4.2 %shard_map.28 = (f32[384,1024]{1,0:T(8,128)S(1)}, f32[192,512]{1,0:T(8,128)S(1)}, f32[192,512]{1,0:T(8,128)S(1)}, f32[64,256]{1,0:T(8,128)S(1)}) custom-call(s32[1]{0:T(128)} %bitcast.1.band_ref.refs_0_.refs_1_, f32[4,2,16,1024]{3,2,1,0:T(8,128)S(1)} %collective-permute-done.lo_ref.refs_1_.refs_2_, f32[4,2,16,1024]{3,2,1,0:T(8,128)S(1)} %copy-done, ...), custom_call_target="tpu_custom_call" | custom-call | tf_op jit(solution)/shard_map/pallas_call | solution.py:262
  17.3 3.4 %collective-permute-start.5 = (f32[64,256]{1,0:T(8,128)S(1)}, f32[64,256]{1,0:T(8,128)S(1)}, u32[]{:S(2)}, u32[]{:S(2)}) collective-permute-start(f32[64,256]{1,0:T(8,128)S(1)} %get-tuple-element.12.refs_9_.refs_10_), channel_id=1, source_target_pairs={{2,0},{3,1},{4,2},{5,3},{6,4},{7,5},{8,6},{9,7},{10,8},{11,9},{12,... | collective-permute-start | bytes 196616 | tf_op jit(solution)/shard_map/ppermute | solution.py:41
  20.7 2.9 %collective-permute-start.4 = (f32[64,256]{1,0:T(8,128)S(1)}, f32[64,256]{1,0:T(8,128)S(1)}, u32[]{:S(2)}, u32[]{:S(2)}) collective-permute-start(f32[64,256]{1,0:T(8,128)S(1)} %get-tuple-element.12.refs_9_.refs_10_), channel_id=1, source_target_pairs={{1,0},{2,1},{3,2},{4,3},{5,4},{6,5},{7,6},{8,7},{9,8},{10,9},{11,1... | collective-permute-start | bytes 196616 | tf_op jit(solution)/shard_map/ppermute | solution.py:41
  23.6 3.5 %collective-permute-start.3 = (f32[64,256]{1,0:T(8,128)S(1)}, f32[64,256]{1,0:T(8,128)S(1)}, u32[]{:S(2)}, u32[]{:S(2)}) collective-permute-start(f32[64,256]{1,0:T(8,128)S(1)} %get-tuple-element.12.refs_9_.refs_10_), channel_id=1, source_target_pairs={{0,1},{1,2},{2,3},{3,4},{4,5},{5,6},{6,7},{7,8},{8,9},{9,10},{10,1... | collective-permute-start | bytes 196616 | tf_op jit(solution)/shard_map/ppermute | solution.py:41
  27.2 2.0 %collective-permute-start.2 = (f32[64,256]{1,0:T(8,128)S(1)}, f32[64,256]{1,0:T(8,128)S(1)}, u32[]{:S(2)}, u32[]{:S(2)}) collective-permute-start(f32[64,256]{1,0:T(8,128)S(1)} %get-tuple-element.12.refs_9_.refs_10_), channel_id=1, source_target_pairs={{0,2},{1,3},{2,4},{3,5},{4,6},{5,7},{6,8},{7,9},{8,10},{9,11},{10,... | collective-permute-start | bytes 196616 | tf_op jit(solution)/shard_map/ppermute | solution.py:41
  29.2 0.2 convert_reduce_fusion
  29.4 0.0 collective-permute-done.5.refs_11_.refs_12_
  29.4 0.0 collective-permute-done.4.refs_10_.refs_11_
  29.4 0.0 collective-permute-done.3.refs_8_.refs_9_
  29.4 4.0 %collective-permute-done.2.refs_7_.refs_8_ = f32[64,256]{1,0:T(8,128)S(1)} collective-permute-done((f32[64,256]{1,0:T(8,128)S(1)}, f32[64,256]{1,0:T(8,128)S(1)}, u32[]{:S(2)}, u32[]{:S(2)}) %collective-permute-start.2) | collective-permute-done | bytes 65568 | tf_op jit(solution)/shard_map/ppermute | solution.py:41
  33.4 2.3 %shard_map.29.refs_13_ = f32[1,2,16,1024]{3,2,1,0:T(8,128)S(1)} custom-call(s32[1]{0:T(128)} %bitcast.1.band_ref.refs_0_.refs_1_, f32[4,2,16,1024]{3,2,1,0:T(8,128)S(1)} %collective-permute-done.lo_ref.refs_1_.refs_2_, f32[4,2,16,1024]{3,2,1,0:T(8,128)S(1)} %copy-done, f32[4,2,16,1024]{3,2,1,0:T(8,128)S(1)} %collective-permute-done.1.hi_ref.refs_3_.refs_4_, ...), custom_call_target="tpu_custom_call" | custom-call | flops 15728640 | bytes 1572864 | tf_op jit(solution)/shard_map/pallas_call | solution.py:320
  35.7 4.0 %collective-permute-start.6 = (f32[1,2,16,1024]{3,2,1,0:T(8,128)S(1)}, f32[1,2,16,1024]{3,2,1,0:T(8,128)S(1)}, u32[]{:S(2)}, u32[]{:S(2)}) collective-permute-start(f32[1,2,16,1024]{3,2,1,0:T(8,128)S(1)} %shard_map.29.refs_13_), channel_id=1, source_target_pairs={{0,16},{16,32},{32,48},{48,64},{64,80},{80,96},{96,112},{112,128},... | collective-permute-start | bytes 393224 | tf_op jit(solution)/shard_map/ppermute | solution.py:41
  39.7 0.0 copy-start.1
  39.7 6.3 %shard_map.30.current_ref = f32[4,2,16,1024]{3,2,1,0:T(8,128)} custom-call(s32[4]{0:T(128)S(1)} %broadcast_subtract_fusion.refs_0_.index_ref, s32[1]{0:T(128)} %bitcast.1.band_ref.refs_0_.refs_1_, f32[4,2,16,1024]{3,2,1,0:T(8,128)S(1)} %collective-permute-done.lo_ref.refs_1_.refs_2_, f32[4,2,16,1024]{3,2,1,0:T(8,128)S(1)} %copy-done, ...), custom_call_target="tpu_custom_call" | custom-call | flops 47185920 | bytes 4718592 | tf_op jit(solution)/shard_map/pallas_call | solution.py:320
  46.0 0.0 copy-done.1
  46.0 4.4 %collective-permute-done.6.below_ref = f32[1,2,16,1024]{3,2,1,0:T(8,128)S(1)} collective-permute-done((f32[1,2,16,1024]{3,2,1,0:T(8,128)S(1)}, f32[1,2,16,1024]{3,2,1,0:T(8,128)S(1)}, u32[]{:S(2)}, u32[]{:S(2)}) %collective-permute-start.6) | collective-permute-done | bytes 131104 | tf_op jit(solution)/shard_map/ppermute | solution.py:41
  50.5 0.0 copy-start.2
  50.5 0.6 %copy-done.2 = f32[1,2,16,1024]{3,2,1,0:T(8,128)} copy-done((f32[1,2,16,1024]{3,2,1,0:T(8,128)}, f32[1,2,16,1024]{3,2,1,0:T(8,128)S(1)}, u32[]{:S(2)}) %copy-start.2) | copy-done | bytes 131096
  51.1 1.6 %shard_map.31 = f32[4,2,16,1024]{3,2,1,0:T(8,128)} custom-call(s32[4]{0:T(128)} %copy-done.1, f32[1,2,16,1024]{3,2,1,0:T(8,128)} %copy-done.2, f32[4,2,16,1024]{3,2,1,0:T(8,128)} %shard_map.30.current_ref), custom_call_target="tpu_custom_call", output_to_operand_aliasing={{}: (2, {})} | custom-call | tf_op jit(solution)/shard_map/pallas_call | solution.py:287
  (2 shorter events, 0.0 us)
Async XLA Ops:
  0.0 11.0 %collective-permute-start.1 = (f32[4,2,16,1024]{3,2,1,0:T(8,128)}, f32[4,2,16,1024]{3,2,1,0:T(8,128)S(1)}, u32[]{:S(2)}, u32[]{:S(2)}) collective-permute-start(f32[4,2,16,1024]{3,2,1,0:T(8,128)} %refs_3_.1), channel_id=1, source_target_pairs={{1,0},{2,1},{3,2},{4,3},{5,4},{6,5},{7,6},{8,7},{9,8},{10,9},{11,1... | collective-permute-start | bytes 1572872 | tf_op jit(solution)/shard_map/ppermute | solution.py:41
  2.6 9.4 %collective-permute-start = (f32[4,2,16,1024]{3,2,1,0:T(8,128)}, f32[4,2,16,1024]{3,2,1,0:T(8,128)S(1)}, u32[]{:S(2)}, u32[]{:S(2)}) collective-permute-start(f32[4,2,16,1024]{3,2,1,0:T(8,128)} %refs_3_.1), channel_id=1, source_target_pairs={{0,1},{1,2},{2,3},{3,4},{4,5},{5,6},{6,7},{7,8},{8,9},{9,10},{10,1... | collective-permute-start | bytes 1572872 | tf_op jit(solution)/shard_map/ppermute | solution.py:41
  12.0 1.0 %copy-start = (f32[4,2,16,1024]{3,2,1,0:T(8,128)S(1)}, f32[4,2,16,1024]{3,2,1,0:T(8,128)}, u32[]{:S(2)}) copy-start(f32[4,2,16,1024]{3,2,1,0:T(8,128)} %refs_3_.1) | copy-start | bytes 1572868
  17.3 12.1 %collective-permute-start.5 = (f32[64,256]{1,0:T(8,128)S(1)}, f32[64,256]{1,0:T(8,128)S(1)}, u32[]{:S(2)}, u32[]{:S(2)}) collective-permute-start(f32[64,256]{1,0:T(8,128)S(1)} %get-tuple-element.12.refs_9_.refs_10_), channel_id=1, source_target_pairs={{2,0},{3,1},{4,2},{5,3},{6,4},{7,5},{8,6},{9,7},{10,8},{11,9},{12,... | collective-permute-start | bytes 196616 | tf_op jit(solution)/shard_map/ppermute | solution.py:41
  20.7 8.7 %collective-permute-start.4 = (f32[64,256]{1,0:T(8,128)S(1)}, f32[64,256]{1,0:T(8,128)S(1)}, u32[]{:S(2)}, u32[]{:S(2)}) collective-permute-start(f32[64,256]{1,0:T(8,128)S(1)} %get-tuple-element.12.refs_9_.refs_10_), channel_id=1, source_target_pairs={{1,0},{2,1},{3,2},{4,3},{5,4},{6,5},{7,6},{8,7},{9,8},{10,9},{11,1... | collective-permute-start | bytes 196616 | tf_op jit(solution)/shard_map/ppermute | solution.py:41
  23.6 5.8 %collective-permute-start.3 = (f32[64,256]{1,0:T(8,128)S(1)}, f32[64,256]{1,0:T(8,128)S(1)}, u32[]{:S(2)}, u32[]{:S(2)}) collective-permute-start(f32[64,256]{1,0:T(8,128)S(1)} %get-tuple-element.12.refs_9_.refs_10_), channel_id=1, source_target_pairs={{0,1},{1,2},{2,3},{3,4},{4,5},{5,6},{6,7},{7,8},{8,9},{9,10},{10,1... | collective-permute-start | bytes 196616 | tf_op jit(solution)/shard_map/ppermute | solution.py:41
  27.2 6.3 %collective-permute-start.2 = (f32[64,256]{1,0:T(8,128)S(1)}, f32[64,256]{1,0:T(8,128)S(1)}, u32[]{:S(2)}, u32[]{:S(2)}) collective-permute-start(f32[64,256]{1,0:T(8,128)S(1)} %get-tuple-element.12.refs_9_.refs_10_), channel_id=1, source_target_pairs={{0,2},{1,3},{2,4},{3,5},{4,6},{5,7},{6,8},{7,9},{8,10},{9,11},{10,... | collective-permute-start | bytes 196616 | tf_op jit(solution)/shard_map/ppermute | solution.py:41
  35.7 14.8 %collective-permute-start.6 = (f32[1,2,16,1024]{3,2,1,0:T(8,128)S(1)}, f32[1,2,16,1024]{3,2,1,0:T(8,128)S(1)}, u32[]{:S(2)}, u32[]{:S(2)}) collective-permute-start(f32[1,2,16,1024]{3,2,1,0:T(8,128)S(1)} %shard_map.29.refs_13_), channel_id=1, source_target_pairs={{0,16},{16,32},{32,48},{48,64},{64,80},{80,96},{96,112},{112,128},... | collective-permute-start | bytes 393224 | tf_op jit(solution)/shard_map/ppermute | solution.py:41
  39.7 6.3 %copy-start.1 = (s32[4]{0:T(128)}, s32[4]{0:T(128)S(1)}, u32[]{:S(2)}) copy-start(s32[4]{0:T(128)S(1)} %broadcast_subtract_fusion.refs_0_.index_ref) | copy-start | bytes 52
  50.5 0.6 %copy-start.2 = (f32[1,2,16,1024]{3,2,1,0:T(8,128)}, f32[1,2,16,1024]{3,2,1,0:T(8,128)S(1)}, u32[]{:S(2)}) copy-start(f32[1,2,16,1024]{3,2,1,0:T(8,128)S(1)} %collective-permute-done.6.below_ref) | copy-start | bytes 393220

commit v9 on v6

--- a/solution.py
+++ b/solution.py
@@ -115,7 +115,8 @@
             f0 = smoothing_weight * s / d
             f1 = smooth(f0, s, d, mask0)
             rows = pl.ds((2 * slot + mode) * F0, F0)
-            f1_ref[rows, :] = f1
+            if slot == SLOTS - 1:
+                f1_ref[pl.ds(mode * F0, F0), :] = f1
             put_blocks(r0_ref, rows, residual(f1, s, d, mask0))
     half = FIELDS * F1
     paired = get_blocks(r0_ref, pl.ds(0, half, stride=2)) + get_blocks(r0_ref, pl.ds(1, half, stride=2))
@@ -195,7 +196,11 @@
         for mode in range(2):
             d = diag(0, mode)
             rows = pl.ds((2 * slot + mode) * F0, F0)
-            f2 = f1_ref[rows, :] + get_blocks(up0_ref, rows)
+            if picks:
+                f1 = smooth(smoothing_weight * src[mode] / d, src[mode], d, mask0)
+            else:
+                f1 = f1_ref[pl.ds(mode * F0, F0), :]
+            f2 = f1 + get_blocks(up0_ref, rows)
             f3 = smooth(f2, src[mode], d, mask0)
             modes.append(smooth(f3, src[mode], d, mask0))
         streams = [modes[0] + modes[1], modes[0] - modes[1]]
@@ -256,7 +261,7 @@
     f1, s1, g1, t = pl.pallas_call(
         first_kernel,
         out_shape=(
-            jax.ShapeDtypeStruct((FIELDS * F0, COLS0), f32),
+            jax.ShapeDtypeStruct((2 * F0, COLS0), f32),
             jax.ShapeDtypeStruct((FIELDS * F1, COLS0 // 2), f32),
             jax.ShapeDtypeStruct((FIELDS * F1, COLS0 // 2), f32),
             jax.ShapeDtypeStruct((FIELDS * CHUNK, COLS0 // 4), f32),
@@ -297,7 +302,7 @@
 
     strips = pl.BlockSpec((slots, 2, ROWS0, COLS0), lambda i: (block, 0, 0, 0))
     in_specs = [smem(), strips, strips, strips,
-                rows(fields * F0, COLS0), rows(fields * F1, COLS0 // 2), rows(fields * F1, COLS0 // 2)]
+                pl.BlockSpec((2 * F0, COLS0), lambda i: (0, 0)), rows(fields * F1, COLS0 // 2), rows(fields * F1, COLS0 // 2)]
     in_specs += [rows(fields * CHUNK, COLS0 // 4)] * 5
     f32 = jnp.float32
     out_shape = jax.ShapeDtypeStruct((slots, 2, ROWS0, COLS0), f32)

time: 53.1 us -> 53.1 us (level)
  waiting for transfers between devices: 13.8 us -> 12.7 us
  Pallas kernels: 14.4 us -> 15.4 us
    ppermute x7, waiting for transfers between devices: 13.8 us -> 12.7 us  [shifted(): lax.ppermute(value, axis, [(source, source + steps) for source in range(f...]
    pallas_call x2, Pallas kernels: 8.57 us -> 9.52 us  [forecast_slots(): pl.pallas_call(functools.partial(second_kernel, slots, pick is not None),...]
    another operation x1, local copies, waits for them, and re-layouts: 0.76 us -> 0.11 us
    unnamed x6 -> x8, local copies, waits for them, and re-layouts: 1.69 us -> 2.34 us
  transfers between devices with their start and end apart: 7 -> 7, of which waited for: 4 -> 4; matrix products, arithmetic and copies ran while one was open for 2% -> 1% of each run, Pallas kernels for 12% -> 14%
where the time goes in v9:
time: 53.1 us; the launch traced here: 52.8 us
  starting transfers between devices  21.7 us (41%)
  Pallas kernels  15.4 us (29%)
  waiting for transfers between devices  12.7 us (24%)
  local copies, waits for them, and re-layouts  2.45 us (5%)
    ppermute x7, starting transfers between devices, shifted(): lax.ppermute(value, axis, [(source, source + steps) for source in range(f...  21.7 us
    ppermute x7, waiting for transfers between devices, shifted(): lax.ppermute(value, axis, [(source, source + steps) for source in range(f...  12.7 us
    pallas_call x2, Pallas kernels, forecast_slots(): pl.pallas_call(functools.partial(second_kernel, slots, pick is not None),...  9.52 us
    pallas_call x1, Pallas kernels, per_device(): pl.pallas_call(first_kernel, out_shape=(jax.ShapeDtypeStruct((2 * F0, COL...  4.26 us
    unnamed x8, local copies, waits for them, and re-layouts  2.34 us
    pallas_call x1, Pallas kernels, per_device(): pl.pallas_call(fix_kernel, out_shape=jax.ShapeDtypeStruct(states.shape, f...  1.65 us
  transfers between devices with their start and end apart: 7, of which 4 were waited for; matrix products, arithmetic and copies ran while one was open for 1% of the time, Pallas kernels for 14%

profile of v9, /device:TPU:39, one launch (start us, length us, event | category | flops | bytes accessed | tf_op | source)
XLA Modules:
  0.0 52.8 jit_solution(17380365703145583105)
XLA Ops:
  0.0 2.6 %collective-permute-start.1 = (f32[4,2,16,1024]{3,2,1,0:T(8,128)}, f32[4,2,16,1024]{3,2,1,0:T(8,128)S(1)}, u32[]{:S(2)}, u32[]{:S(2)}) collective-permute-start(f32[4,2,16,1024]{3,2,1,0:T(8,128)} %refs_3_.1), channel_id=1, source_target_pairs={{1,0},{2,1},{3,2},{4,3},{5,4},{6,5},{7,6},{8,7},{9,8},{10,9},{11,1... | collective-permute-start | bytes 1572872 | tf_op jit(solution)/shard_map/ppermute | solution.py:41
  2.6 3.0 %collective-permute-start = (f32[4,2,16,1024]{3,2,1,0:T(8,128)}, f32[4,2,16,1024]{3,2,1,0:T(8,128)S(1)}, u32[]{:S(2)}, u32[]{:S(2)}) collective-permute-start(f32[4,2,16,1024]{3,2,1,0:T(8,128)} %refs_3_.1), channel_id=1, source_target_pairs={{0,1},{1,2},{2,3},{3,4},{4,5},{5,6},{6,7},{7,8},{8,9},{9,10},{10,1... | collective-permute-start | bytes 1572872 | tf_op jit(solution)/shard_map/ppermute | solution.py:41
  5.6 0.0 copy-start.3
  5.6 0.6 %copy-done.3 = s32[128]{0:T(128)S(1)} copy-done((s32[128]{0:T(128)S(1)}, s32[128]{0:T(128)}, u32[]{:S(2)}) %copy-start.3) | copy-done | bytes 536
  6.2 0.1 copy.6
  6.3 0.2 reduce-window.8
  6.5 0.1 reduce
  6.6 4.4 %collective-permute-done.1.hi_ref.refs_3_.refs_4_ = f32[4,2,16,1024]{3,2,1,0:T(8,128)S(1)} collective-permute-done((f32[4,2,16,1024]{3,2,1,0:T(8,128)}, f32[4,2,16,1024]{3,2,1,0:T(8,128)S(1)}, u32[]{:S(2)}, u32[]{:S(2)}) %collective-permute-start.1) | collective-permute-done | bytes 524320 | tf_op jit(solution)/shard_map/ppermute | solution.py:41
  11.0 1.0 %collective-permute-done.lo_ref.refs_1_.refs_2_ = f32[4,2,16,1024]{3,2,1,0:T(8,128)S(1)} collective-permute-done((f32[4,2,16,1024]{3,2,1,0:T(8,128)}, f32[4,2,16,1024]{3,2,1,0:T(8,128)S(1)}, u32[]{:S(2)}, u32[]{:S(2)}) %collective-permute-start) | collective-permute-done | bytes 524320 | tf_op jit(solution)/shard_map/ppermute | solution.py:41
  12.0 0.0 copy-start
  12.0 1.0 %copy-done = f32[4,2,16,1024]{3,2,1,0:T(8,128)S(1)} copy-done((f32[4,2,16,1024]{3,2,1,0:T(8,128)S(1)}, f32[4,2,16,1024]{3,2,1,0:T(8,128)}, u32[]{:S(2)}) %copy-start) | copy-done | bytes 524312
  13.0 4.3 %shard_map.28 = (f32[96,1024]{1,0:T(8,128)S(1)}, f32[192,512]{1,0:T(8,128)S(1)}, f32[192,512]{1,0:T(8,128)S(1)}, f32[64,256]{1,0:T(8,128)S(1)}) custom-call(s32[1]{0:T(128)} %bitcast.1.band_ref.refs_0_.refs_1_, f32[4,2,16,1024]{3,2,1,0:T(8,128)S(1)} %collective-permute-done.lo_ref.refs_1_.refs_2_, f32[4,2,16,1024]{3,2,1,0:T(8,128)S(1)} %copy-done, ...), custom_call_target="tpu_custom_call" | custom-call | tf_op jit(solution)/shard_map/pallas_call | solution.py:261
  17.3 3.4 %collective-permute-start.5 = (f32[64,256]{1,0:T(8,128)S(1)}, f32[64,256]{1,0:T(8,128)S(1)}, u32[]{:S(2)}, u32[]{:S(2)}) collective-permute-start(f32[64,256]{1,0:T(8,128)S(1)} %get-tuple-element.12.refs_9_.refs_10_), channel_id=1, source_target_pairs={{2,0},{3,1},{4,2},{5,3},{6,4},{7,5},{8,6},{9,7},{10,8},{11,9},{12,... | collective-permute-start | bytes 196616 | tf_op jit(solution)/shard_map/ppermute | solution.py:41
  20.7 2.9 %collective-permute-start.4 = (f32[64,256]{1,0:T(8,128)S(1)}, f32[64,256]{1,0:T(8,128)S(1)}, u32[]{:S(2)}, u32[]{:S(2)}) collective-permute-start(f32[64,256]{1,0:T(8,128)S(1)} %get-tuple-element.12.refs_9_.refs_10_), channel_id=1, source_target_pairs={{1,0},{2,1},{3,2},{4,3},{5,4},{6,5},{7,6},{8,7},{9,8},{10,9},{11,1... | collective-permute-start | bytes 196616 | tf_op jit(solution)/shard_map/ppermute | solution.py:41
  23.7 3.5 %collective-permute-start.3 = (f32[64,256]{1,0:T(8,128)S(1)}, f32[64,256]{1,0:T(8,128)S(1)}, u32[]{:S(2)}, u32[]{:S(2)}) collective-permute-start(f32[64,256]{1,0:T(8,128)S(1)} %get-tuple-element.12.refs_9_.refs_10_), channel_id=1, source_target_pairs={{0,1},{1,2},{2,3},{3,4},{4,5},{5,6},{6,7},{7,8},{8,9},{9,10},{10,1... | collective-permute-start | bytes 196616 | tf_op jit(solution)/shard_map/ppermute | solution.py:41
  27.2 2.0 %collective-permute-start.2 = (f32[64,256]{1,0:T(8,128)S(1)}, f32[64,256]{1,0:T(8,128)S(1)}, u32[]{:S(2)}, u32[]{:S(2)}) collective-permute-start(f32[64,256]{1,0:T(8,128)S(1)} %get-tuple-element.12.refs_9_.refs_10_), channel_id=1, source_target_pairs={{0,2},{1,3},{2,4},{3,5},{4,6},{5,7},{6,8},{7,9},{8,10},{9,11},{10,... | collective-permute-start | bytes 196616 | tf_op jit(solution)/shard_map/ppermute | solution.py:41
  29.3 0.2 convert_reduce_fusion
  29.4 0.0 collective-permute-done.5.refs_11_.refs_12_
  29.4 0.0 collective-permute-done.4.refs_10_.refs_11_
  29.5 0.0 collective-permute-done.3.refs_8_.refs_9_
  29.5 4.0 %collective-permute-done.2.refs_7_.refs_8_ = f32[64,256]{1,0:T(8,128)S(1)} collective-permute-done((f32[64,256]{1,0:T(8,128)S(1)}, f32[64,256]{1,0:T(8,128)S(1)}, u32[]{:S(2)}, u32[]{:S(2)}) %collective-permute-start.2) | collective-permute-done | bytes 65568 | tf_op jit(solution)/shard_map/ppermute | solution.py:41
  33.5 2.3 %shard_map.29.refs_13_ = f32[1,2,16,1024]{3,2,1,0:T(8,128)S(1)} custom-call(s32[1]{0:T(128)} %bitcast.1.band_ref.refs_0_.refs_1_, f32[4,2,16,1024]{3,2,1,0:T(8,128)S(1)} %collective-permute-done.lo_ref.refs_1_.refs_2_, f32[4,2,16,1024]{3,2,1,0:T(8,128)S(1)} %copy-done, f32[4,2,16,1024]{3,2,1,0:T(8,128)S(1)} %collective-permute-done.1.hi_ref.refs_3_.refs_4_, ...), custom_call_target="tpu_custom_call" | custom-call | flops 15728640 | bytes 1572864 | tf_op jit(solution)/shard_map/pallas_call | solution.py:319
  35.7 4.2 %collective-permute-start.6 = (f32[1,2,16,1024]{3,2,1,0:T(8,128)S(1)}, f32[1,2,16,1024]{3,2,1,0:T(8,128)S(1)}, u32[]{:S(2)}, u32[]{:S(2)}) collective-permute-start(f32[1,2,16,1024]{3,2,1,0:T(8,128)S(1)} %shard_map.29.refs_13_), channel_id=1, source_target_pairs={{0,16},{16,32},{32,48},{48,64},{64,80},{80,96},{96,112},{112,128},... | collective-permute-start | bytes 393224 | tf_op jit(solution)/shard_map/ppermute | solution.py:41
  39.9 0.0 copy-start.1
  40.0 7.3 %shard_map.30.current_ref = f32[4,2,16,1024]{3,2,1,0:T(8,128)} custom-call(s32[4]{0:T(128)S(1)} %broadcast_subtract_fusion.refs_0_.index_ref, s32[1]{0:T(128)} %bitcast.1.band_ref.refs_0_.refs_1_, f32[4,2,16,1024]{3,2,1,0:T(8,128)S(1)} %collective-permute-done.lo_ref.refs_1_.refs_2_, f32[4,2,16,1024]{3,2,1,0:T(8,128)S(1)} %copy-done, ...), custom_call_target="tpu_custom_call" | custom-call | flops 47185920 | bytes 4718592 | tf_op jit(solution)/shard_map/pallas_call | solution.py:319
  47.2 0.0 copy-done.1
  47.2 3.3 %collective-permute-done.6.below_ref = f32[1,2,16,1024]{3,2,1,0:T(8,128)S(1)} collective-permute-done((f32[1,2,16,1024]{3,2,1,0:T(8,128)S(1)}, f32[1,2,16,1024]{3,2,1,0:T(8,128)S(1)}, u32[]{:S(2)}, u32[]{:S(2)}) %collective-permute-start.6) | collective-permute-done | bytes 131104 | tf_op jit(solution)/shard_map/ppermute | solution.py:41
  50.5 0.0 copy-start.2
  50.5 0.6 %copy-done.2 = f32[1,2,16,1024]{3,2,1,0:T(8,128)} copy-done((f32[1,2,16,1024]{3,2,1,0:T(8,128)}, f32[1,2,16,1024]{3,2,1,0:T(8,128)S(1)}, u32[]{:S(2)}) %copy-start.2) | copy-done | bytes 131096
  51.2 1.6 %shard_map.31 = f32[4,2,16,1024]{3,2,1,0:T(8,128)} custom-call(s32[4]{0:T(128)} %copy-done.1, f32[1,2,16,1024]{3,2,1,0:T(8,128)} %copy-done.2, f32[4,2,16,1024]{3,2,1,0:T(8,128)} %shard_map.30.current_ref), custom_call_target="tpu_custom_call", output_to_operand_aliasing={{}: (2, {})} | custom-call | tf_op jit(solution)/shard_map/pallas_call | solution.py:286
  (2 shorter events, 0.0 us)
Async XLA Ops:
  0.0 11.0 %collective-permute-start.1 = (f32[4,2,16,1024]{3,2,1,0:T(8,128)}, f32[4,2,16,1024]{3,2,1,0:T(8,128)S(1)}, u32[]{:S(2)}, u32[]{:S(2)}) collective-permute-start(f32[4,2,16,1024]{3,2,1,0:T(8,128)} %refs_3_.1), channel_id=1, source_target_pairs={{1,0},{2,1},{3,2},{4,3},{5,4},{6,5},{7,6},{8,7},{9,8},{10,9},{11,1... | collective-permute-start | bytes 1572872 | tf_op jit(solution)/shard_map/ppermute | solution.py:41
  2.6 9.4 %collective-permute-start = (f32[4,2,16,1024]{3,2,1,0:T(8,128)}, f32[4,2,16,1024]{3,2,1,0:T(8,128)S(1)}, u32[]{:S(2)}, u32[]{:S(2)}) collective-permute-start(f32[4,2,16,1024]{3,2,1,0:T(8,128)} %refs_3_.1), channel_id=1, source_target_pairs={{0,1},{1,2},{2,3},{3,4},{4,5},{5,6},{6,7},{7,8},{8,9},{9,10},{10,1... | collective-permute-start | bytes 1572872 | tf_op jit(solution)/shard_map/ppermute | solution.py:41
  5.6 0.7 %copy-start.3 = (s32[128]{0:T(128)S(1)}, s32[128]{0:T(128)}, u32[]{:S(2)}) copy-start(s32[128]{0:T(128)} %param.3) | copy-start | bytes 1540
  12.0 1.0 %copy-start = (f32[4,2,16,1024]{3,2,1,0:T(8,128)S(1)}, f32[4,2,16,1024]{3,2,1,0:T(8,128)}, u32[]{:S(2)}) copy-start(f32[4,2,16,1024]{3,2,1,0:T(8,128)} %refs_3_.1) | copy-start | bytes 1572868
  17.3 12.1 %collective-permute-start.5 = (f32[64,256]{1,0:T(8,128)S(1)}, f32[64,256]{1,0:T(8,128)S(1)}, u32[]{:S(2)}, u32[]{:S(2)}) collective-permute-start(f32[64,256]{1,0:T(8,128)S(1)} %get-tuple-element.12.refs_9_.refs_10_), channel_id=1, source_target_pairs={{2,0},{3,1},{4,2},{5,3},{6,4},{7,5},{8,6},{9,7},{10,8},{11,9},{12,... | collective-permute-start | bytes 196616 | tf_op jit(solution)/shard_map/ppermute | solution.py:41
  20.7 8.7 %collective-permute-start.4 = (f32[64,256]{1,0:T(8,128)S(1)}, f32[64,256]{1,0:T(8,128)S(1)}, u32[]{:S(2)}, u32[]{:S(2)}) collective-permute-start(f32[64,256]{1,0:T(8,128)S(1)} %get-tuple-element.12.refs_9_.refs_10_), channel_id=1, source_target_pairs={{1,0},{2,1},{3,2},{4,3},{5,4},{6,5},{7,6},{8,7},{9,8},{10,9},{11,1... | collective-permute-start | bytes 196616 | tf_op jit(solution)/shard_map/ppermute | solution.py:41
  23.7 5.8 %collective-permute-start.3 = (f32[64,256]{1,0:T(8,128)S(1)}, f32[64,256]{1,0:T(8,128)S(1)}, u32[]{:S(2)}, u32[]{:S(2)}) collective-permute-start(f32[64,256]{1,0:T(8,128)S(1)} %get-tuple-element.12.refs_9_.refs_10_), channel_id=1, source_target_pairs={{0,1},{1,2},{2,3},{3,4},{4,5},{5,6},{6,7},{7,8},{8,9},{9,10},{10,1... | collective-permute-start | bytes 196616 | tf_op jit(solution)/shard_map/ppermute | solution.py:41
  27.2 6.3 %collective-permute-start.2 = (f32[64,256]{1,0:T(8,128)S(1)}, f32[64,256]{1,0:T(8,128)S(1)}, u32[]{:S(2)}, u32[]{:S(2)}) collective-permute-start(f32[64,256]{1,0:T(8,128)S(1)} %get-tuple-element.12.refs_9_.refs_10_), channel_id=1, source_target_pairs={{0,2},{1,3},{2,4},{3,5},{4,6},{5,7},{6,8},{7,9},{8,10},{9,11},{10,... | collective-permute-start | bytes 196616 | tf_op jit(solution)/shard_map/ppermute | solution.py:41
  35.7 14.8 %collective-permute-start.6 = (f32[1,2,16,1024]{3,2,1,0:T(8,128)S(1)}, f32[1,2,16,1024]{3,2,1,0:T(8,128)S(1)}, u32[]{:S(2)}, u32[]{:S(2)}) collective-permute-start(f32[1,2,16,1024]{3,2,1,0:T(8,128)S(1)} %shard_map.29.refs_13_), channel_id=1, source_target_pairs={{0,16},{16,32},{32,48},{48,64},{64,80},{80,96},{96,112},{112,128},... | collective-permute-start | bytes 393224 | tf_op jit(solution)/shard_map/ppermute | solution.py:41
  39.9 7.3 %copy-start.1 = (s32[4]{0:T(128)}, s32[4]{0:T(128)S(1)}, u32[]{:S(2)}) copy-start(s32[4]{0:T(128)S(1)} %broadcast_subtract_fusion.refs_0_.index_ref) | copy-start | bytes 52
  50.5 0.6 %copy-start.2 = (f32[1,2,16,1024]{3,2,1,0:T(8,128)}, f32[1,2,16,1024]{3,2,1,0:T(8,128)S(1)}, u32[]{:S(2)}) copy-start(f32[1,2,16,1024]{3,2,1,0:T(8,128)S(1)} %collective-permute-done.6.below_ref) | copy-start | bytes 393220
